TPU v7x, 512 devices: a whole 4x8x8 slice. The times are simulated.
512 devices in a mesh: ctx: 128 (over z, x, y_hi), tp: 4 (over y_lo, core).
Axes of the slice: x: 4, y: 8 (y_hi: 4, y_lo: 2; y = y_hi * 2 + y_lo), z: 8, core: 2. Of those that a mesh axis runs over, the one named last changes fastest.
Arguments:
- query_proj: bfloat16 [128, 131072], P('tp', 'ctx'), may hold values from -15 to 15
- key_proj: bfloat16 [128, 131072], P('tp', 'ctx'), may hold values from -6 to 6
- value_proj: bfloat16 [128, 131072], P('tp', 'ctx'), may hold values from -6 to 6
- short_taps: float32 [3, 128, 3], P(None, 'tp'), may hold values from -3 to 3
- long_filter: float32 [8, 131072], P('tp', 'ctx'), may hold values from -1.1 to 1.1, as said below
- skip_scale: float32 [128], P('tp'), may hold values from 0.5 to 1.5
- norm_gain: float32 [128], P('tp'), may hold values from 0.5 to 2
Outputs:
- mixer_out: bfloat16 [128, 131072], P('tp', 'ctx')
Inputs may be any that keep to these rules, and one draw needn't show every extreme that they name: `long_filter`: filter taps.
All inputs are finite; a program needn't handle non-finite values.
Results may differ from a plain program's by a relative error of at most 0.001.
Values may be sent and summed in bfloat16 or wider, within the bound.
No kernel may reach another device: no remote copies, remote signals or barrier semaphores. Data moves between devices by JAX's collectives and lax.ppermute only.
A program may use at most 64 MiB of HBM per device.

v0:
```python
import math

import jax
import jax.numpy as jnp
from jax import lax
from jax.sharding import PartitionSpec as P

HIGHEST = lax.Precision.HIGHEST


def shifted(x, axis, by):
    length = lax.axis_size(axis)
    pairs = [(i, i + by) for i in range(length) if 0 <= i + by < length]
    return lax.ppermute(x, axis, pairs)


def trig_pair(steps_int, modulus):
    angle = (steps_int % modulus).astype(jnp.float32) * (2.0 * math.pi / modulus)
    return (jnp.cos(angle), jnp.sin(angle))


def grid_product(first_len, second_len, modulus):
    left = lax.broadcasted_iota(jnp.int32, (first_len, second_len), 0)
    right = lax.broadcasted_iota(jnp.int32, (first_len, second_len), 1)
    return trig_pair(left * right, modulus)


def apply_rows(table, values):
    return jnp.einsum("kt,ctn->ckn", table, values, precision=HIGHEST)


def apply_cols(table, values):
    return jnp.einsum("ckn,nm->ckm", values, table, precision=HIGHEST)


def dft_section(apply_fn, real_part, imag_part, tables, direction):
    cos_table, sin_table = tables
    if imag_part is None:
        return (apply_fn(cos_table, real_part), direction * apply_fn(sin_table, real_part))
    new_real = apply_fn(cos_table, real_part) - direction * apply_fn(sin_table, imag_part)
    new_imag = direction * apply_fn(sin_table, real_part) + apply_fn(cos_table, imag_part)
    return (new_real, new_imag)


def rotate(real_part, imag_part, tables, direction):
    cos_table, sin_table = tables
    new_real = real_part * cos_table - direction * imag_part * sin_table
    new_imag = direction * real_part * sin_table + imag_part * cos_table
    return (new_real, new_imag)


def forward_local(real_part, imag_part, first_len, ctx_count, ctx_index):
    rows_real = real_part.shape[1]
    padded_len = first_len * ctx_count * ctx_count
    extra_rows = ((0, 0), (0, first_len - rows_real), (0, 0))
    real_part = jnp.pad(real_part, extra_rows)
    imag_part = jnp.pad(imag_part, extra_rows)
    first_tables = grid_product(first_len, first_len, first_len)
    real_part, imag_part = dft_section(apply_rows, real_part, imag_part, first_tables, -1.0)
    real_part, imag_part = rotate(
        real_part, imag_part, grid_product(first_len, ctx_count, first_len * ctx_count), -1.0
    )
    real_part, imag_part = dft_section(
        apply_cols, real_part, imag_part, grid_product(ctx_count, ctx_count, ctx_count), -1.0
    )
    freq_first = lax.broadcasted_iota(jnp.int32, (first_len, ctx_count), 0)
    freq_second = lax.broadcasted_iota(jnp.int32, (first_len, ctx_count), 1)
    twist = trig_pair((freq_first + first_len * freq_second) * ctx_index, padded_len)
    return rotate(real_part, imag_part, twist, -1.0)


def causal_three(values, before, taps):
    extended = jnp.concatenate([before.astype(jnp.float32), values.astype(jnp.float32)], axis=1)
    return (
        taps[:, 0:1] * extended[:, 2:]
        + taps[:, 1:2] * extended[:, 1:-1]
        + taps[:, 2:3] * extended[:, :-2]
    )


def pack_pairs(values, filter_count):
    grouped = values.reshape((filter_count, 2, -1) + values.shape[1:])
    return (
        grouped[:, 0].reshape((-1,) + values.shape[1:]),
        grouped[:, 1].reshape((-1,) + values.shape[1:]),
    )


def unpack_pairs(real_part, imag_part, filter_count):
    shape = (filter_count, 1, -1) + real_part.shape[1:]
    both = jnp.concatenate([real_part.reshape(shape), imag_part.reshape(shape)], axis=1)
    return both.reshape((-1,) + real_part.shape[1:])


def shards(query_proj, key_proj, value_proj, short_taps, long_filter, skip_scale, norm_gain):
    chan_count = query_proj.shape[0]
    tok_count = query_proj.shape[1]
    ctx_count = lax.axis_size("ctx")
    ctx_index = lax.axis_index("ctx")
    row_count = tok_count // ctx_count
    first_len = 2 * row_count
    padded_len = first_len * ctx_count * ctx_count
    filter_count = long_filter.shape[0]
    pair_count = chan_count // 2
    tails = jnp.stack([query_proj[:, -2:], key_proj[:, -2:], value_proj[:, -2:]])
    before = shifted(tails, "ctx", 1)
    q_conv = causal_three(query_proj, before[0], short_taps[0])
    k_conv = causal_three(key_proj, before[1], short_taps[1])
    v_conv = causal_three(value_proj, before[2], short_taps[2])
    product = k_conv * v_conv
    both_in = jnp.concatenate(
        [
            product.reshape(chan_count, row_count, ctx_count),
            long_filter.reshape(filter_count, row_count, ctx_count),
        ],
        axis=0,
    )
    moved = lax.all_to_all(both_in, "ctx", split_axis=2, concat_axis=1, tiled=True)
    moved = moved.reshape(chan_count + filter_count, row_count, ctx_count)
    data_cols = moved[:chan_count]
    filter_cols = moved[chan_count:]
    pair_real, pair_imag = pack_pairs(data_cols, filter_count)
    in_real = jnp.concatenate([pair_real, filter_cols], axis=0)
    in_imag = jnp.concatenate([pair_imag, jnp.zeros_like(filter_cols)], axis=0)
    spec_real, spec_imag = forward_local(in_real, in_imag, first_len, ctx_count, ctx_index)
    spec = lax.all_to_all(
        jnp.concatenate([spec_real, spec_imag], axis=0), "ctx", split_axis=2, concat_axis=2,
        tiled=True,
    )
    square_tables = grid_product(ctx_count, ctx_count, ctx_count)
    row_total = pair_count + filter_count
    spec_real, spec_imag = dft_section(
        apply_cols, spec[:row_total], spec[row_total:], square_tables, -1.0
    )
    data_real = spec_real[:pair_count]
    data_imag = spec_imag[:pair_count]
    filt_real = spec_real[pair_count:]
    filt_imag = spec_imag[pair_count:]
    grouped_shape = (filter_count, pair_count // filter_count, first_len, ctx_count)
    group_real = data_real.reshape(grouped_shape)
    group_imag = data_imag.reshape(grouped_shape)
    prod_real = (group_real * filt_real[:, None] - group_imag * filt_imag[:, None]).reshape(
        data_real.shape
    )
    prod_imag = (group_real * filt_imag[:, None] + group_imag * filt_real[:, None]).reshape(
        data_real.shape
    )
    back_real, back_imag = dft_section(apply_cols, prod_real, prod_imag, square_tables, 1.0)
    freq_first = lax.broadcasted_iota(jnp.int32, (first_len, ctx_count), 0)
    time_third = lax.broadcasted_iota(jnp.int32, (first_len, ctx_count), 1)
    twist = trig_pair((freq_first + first_len * ctx_index) * time_third, padded_len)
    back_real, back_imag = rotate(back_real, back_imag, twist, 1.0)
    back = lax.all_to_all(
        jnp.concatenate([back_real, back_imag], axis=0), "ctx", split_axis=2, concat_axis=2,
        tiled=True,
    )
    back_real, back_imag = dft_section(
        apply_cols, back[:pair_count], back[pair_count:], square_tables, 1.0
    )
    back_real, back_imag = rotate(
        back_real, back_imag, grid_product(first_len, ctx_count, first_len * ctx_count), 1.0
    )
    first_tables = grid_product(first_len, first_len, first_len)
    time_real, time_imag = dft_section(apply_rows, back_real, back_imag, first_tables, 1.0)
    time_vals = unpack_pairs(time_real[:, :row_count], time_imag[:, :row_count], filter_count)
    time_vals = time_vals.reshape(chan_count, row_count * ctx_count, 1) * (1.0 / padded_len)
    convolved = lax.all_to_all(time_vals, "ctx", split_axis=1, concat_axis=2, tiled=True).reshape(
        chan_count, tok_count
    )
    mixed = q_conv * (convolved + skip_scale[:, None] * product)
    power = lax.psum(jnp.sum(mixed * mixed, axis=0), "tp")
    total_channels = chan_count * lax.axis_size("tp")
    return (norm_gain[:, None] * mixed * lax.rsqrt(power / total_channels + 1e-05)).astype(
        jnp.bfloat16
    )


def solution(mesh):
    return jax.shard_map(
        shards,
        mesh=mesh,
        in_specs=(
            P("tp", "ctx"),
            P("tp", "ctx"),
            P("tp", "ctx"),
            P(None, "tp", None),
            P("tp", "ctx"),
            P("tp"),
            P("tp"),
        ),
        out_specs=P("tp", "ctx"),
        check_vma=False,
    )
```

profile of v0, /device:TPU:1, one launch (start us, length us, event | category | flops | bytes accessed | tf_op | source)
XLA Modules:
  0.0 156.3 jit_solution(9124750565130972556)
XLA Ops:
  0.0 0.8 slice.123
  0.9 0.8 slice.122
  1.7 0.8 slice.121
  2.6 5.0 %collective-permute-start = (bf16[3,32,2]{1,2,0:T(2,128)(2,1)S(1)}, bf16[3,32,2]{1,2,0:T(2,128)(2,1)S(1)}, u32[]{:S(2)}, u32[]{:S(2)}) collective-permute-start(bf16[3,32,2]{1,2,0:T(2,128)(2,1)S(1)} %pad_maximum_fusion.6), channel_id=1, source_target_pairs={{0,4},{4,8},{8,12},{12,16},{16,20},{20,24},{24,28},{28,32},{32,36}... | collective-permute-start | bytes 1160 | tf_op jit(solution)/shard_map/ppermute | solution.py:14
  7.7 0.7 slice_bitcast_fusion.2
  8.4 0.9 convert_element_type.136
  9.3 0.9 convert_element_type.133
  11.6 1.2 reshape.204
  12.8 19.2 %all-to-all-start = ((f32[128,1,272]{2,1,0:T(1,128)}), f32[128,1,272]{2,1,0:T(1,128)S(1)}, u32[]{:S(2)}, u32[]{:S(2)}) async-start(f32[128,1,272]{2,1,0:T(1,128)} %reshape.204), calls=%async_computation | async-start | bytes 393216 | tf_op jit(solution)/shard_map/all_to_all | solution.py:118
  32.1 13.7 %all-to-all-done = f32[128,1,272]{2,1,0:T(1,128)S(1)} async-done(((f32[128,1,272]{2,1,0:T(1,128)}), f32[128,1,272]{2,1,0:T(1,128)S(1)}, u32[]{:S(2)}, u32[]{:S(2)}) %all-to-all-start) | async-done | bytes 139296 | tf_op jit(solution)/shard_map/all_to_all | solution.py:118
  46.3 1.1 reduce
  48.0 1.7 %reshape.203 = f32[2,2,8,8,128]{2,1,0,4,3:T(2,128)S(1)} reshape(f32[32,128,8,1]{0,2,1,3:T(8,128)S(1)} %bitcast.180) | data formatting | bytes 262144 | tf_op jit(solution)/shard_map/reshape | solution.py:82
  49.7 3.0 %fusion.231 = (f32[2,1,8,8,128]{2,1,0,4,3:T(1,128)S(1)}, f32[2,1,8,8,128]{2,1,0,4,3:T(1,128)}) fusion(f32[2,2,8,8,128]{2,1,0,4,3:T(2,128)S(1)} %reshape.203), kind=kLoop, calls=%fused_computation.289 | loop fusion | bytes 262144 | tf_op jit(solution)/shard_map/slice | solution.py:85
  52.7 1.4 copy.81
  54.1 1.1 copy.82
  59.2 1.8 %reshape.206 = f32[128,1,576]{2,1,0:T(1,128)} reshape(f32[128,16,36]{2,1,0:T(8,128)S(1)} %bitcast.182) | data formatting | bytes 589824
  61.0 6.4 %all-to-all-start.1 = ((f32[128,1,576]{2,1,0:T(1,128)}), f32[128,1,576]{2,1,0:T(1,128)S(1)}, u32[]{:S(2)}, u32[]{:S(2)}) async-start(f32[128,1,576]{2,1,0:T(1,128)} %reshape.206), calls=%async_computation.1 | async-start | bytes 655360 | tf_op jit(solution)/shard_map/all_to_all | solution.py:126
  67.5 14.8 %all-to-all-done.1 = f32[128,1,576]{2,1,0:T(1,128)S(1)} async-done(((f32[128,1,576]{2,1,0:T(1,128)}), f32[128,1,576]{2,1,0:T(1,128)S(1)}, u32[]{:S(2)}, u32[]{:S(2)}) %all-to-all-start.1) | async-done | bytes 294944 | tf_op jit(solution)/shard_map/all_to_all | solution.py:126
  82.4 1.4 reduce.1
  83.8 0.7 reshape.207
  90.6 1.2 reshape.208
  91.8 6.4 %all-to-all-start.2 = ((f32[128,1,512]{2,1,0:T(1,128)}), f32[128,1,512]{2,1,0:T(1,128)S(1)}, u32[]{:S(2)}, u32[]{:S(2)}) async-start(f32[128,1,512]{2,1,0:T(1,128)} %reshape.208), calls=%async_computation.2 | async-start | bytes 524288 | tf_op jit(solution)/shard_map/all_to_all | solution.py:153
  98.3 14.5 %all-to-all-done.2 = f32[128,1,512]{2,1,0:T(1,128)S(1)} async-done(((f32[128,1,512]{2,1,0:T(1,128)}), f32[128,1,512]{2,1,0:T(1,128)S(1)}, u32[]{:S(2)}, u32[]{:S(2)}) %all-to-all-start.2) | async-done | bytes 262176 | tf_op jit(solution)/shard_map/all_to_all | solution.py:153
  112.8 1.3 reduce.2
  119.4 2.0 %reduce.3 = f32[1024,32]{1,0:T(8,128)S(1)} reduce(f32[1024,1,32]{2,1,0:T(1,128)S(1)} %bitcast.185, f32[]{:T(128)} %broadcast.503), dimensions={1}, to_apply=%bitcast.155.reduce_sub_computation | reduce | bytes 262148
  121.4 0.9 reshape.210
  122.3 6.2 %all-to-all-start.3 = ((f32[128,1,256]{2,1,0:T(1,128)}), f32[128,1,256]{2,1,0:T(1,128)S(1)}, u32[]{:S(2)}, u32[]{:S(2)}) async-start(f32[128,1,256]{2,1,0:T(1,128)} %reshape.210), calls=%async_computation.3 | async-start | bytes 262144 | tf_op jit(solution)/shard_map/all_to_all | solution.py:167
  128.6 13.3 %all-to-all-done.3 = f32[128,1,256]{2,1,0:T(1,128)S(1)} async-done(((f32[128,1,256]{2,1,0:T(1,128)}), f32[128,1,256]{2,1,0:T(1,128)S(1)}, u32[]{:S(2)}, u32[]{:S(2)}) %all-to-all-start.3) | async-done | bytes 131104 | tf_op jit(solution)/shard_map/all_to_all | solution.py:167
  141.9 1.0 reduce.4
  142.9 0.9 reshape.211
  144.2 11.3 %psum.7 = f32[1024]{0:T(1024)S(1)} all-reduce(f32[1024]{0:T(1024)S(1)} %get-tuple-element.5), channel_id=1, replica_groups=mesh['ctx'=128,'tp'=4] {'tp'}, use_global_device_ids=true, to_apply=%region_1.2 | all-reduce | flops 1024 | bytes 8192 | tf_op jit(solution)/shard_map/psum | solution.py:171
  155.5 0.7 multiply_convert_fusion
  (80 shorter events, 18.8 us)
Async XLA Ops:
  2.6 8.2 %collective-permute-start = (bf16[3,32,2]{1,2,0:T(2,128)(2,1)S(1)}, bf16[3,32,2]{1,2,0:T(2,128)(2,1)S(1)}, u32[]{:S(2)}, u32[]{:S(2)}) collective-permute-start(bf16[3,32,2]{1,2,0:T(2,128)(2,1)S(1)} %pad_maximum_fusion.6), channel_id=1, source_target_pairs={{0,4},{4,8},{8,12},{12,16},{16,20},{20,24},{24,28},{28,32},{32,36}... | collective-permute-start | bytes 1160 | tf_op jit(solution)/shard_map/ppermute | solution.py:14
  12.8 33.0 %all-to-all-start = ((f32[128,1,272]{2,1,0:T(1,128)}), f32[128,1,272]{2,1,0:T(1,128)S(1)}, u32[]{:S(2)}, u32[]{:S(2)}) async-start(f32[128,1,272]{2,1,0:T(1,128)} %reshape.204), calls=%async_computation | async-start | bytes 393216 | tf_op jit(solution)/shard_map/all_to_all | solution.py:118
  61.0 21.4 %all-to-all-start.1 = ((f32[128,1,576]{2,1,0:T(1,128)}), f32[128,1,576]{2,1,0:T(1,128)S(1)}, u32[]{:S(2)}, u32[]{:S(2)}) async-start(f32[128,1,576]{2,1,0:T(1,128)} %reshape.206), calls=%async_computation.1 | async-start | bytes 655360 | tf_op jit(solution)/shard_map/all_to_all | solution.py:126
  91.8 21.0 %all-to-all-start.2 = ((f32[128,1,512]{2,1,0:T(1,128)}), f32[128,1,512]{2,1,0:T(1,128)S(1)}, u32[]{:S(2)}, u32[]{:S(2)}) async-start(f32[128,1,512]{2,1,0:T(1,128)} %reshape.208), calls=%async_computation.2 | async-start | bytes 524288 | tf_op jit(solution)/shard_map/all_to_all | solution.py:153
  118.7 9.8 %copy-start = (bf16[32,1024]{1,0:T(8,128)(2,1)S(1)}, bf16[32,1024]{1,0:T(8,128)(2,1)}, u32[]{:S(2)}) copy-start(bf16[32,1024]{1,0:T(8,128)(2,1)} %param.7) | copy-start | bytes 196612
  119.1 24.9 %copy-start.2 = (f32[32]{0:T(128)S(1)}, f32[32]{0:T(128)}, u32[]{:S(2)}) copy-start(f32[32]{0:T(128)} %param.12) | copy-start | bytes 388
  119.4 36.1 %copy-start.1 = (f32[32]{0:T(128)S(1)}, f32[32]{0:T(128)}, u32[]{:S(2)}) copy-start(f32[32]{0:T(128)} %param.13) | copy-start | bytes 388
  122.3 19.6 %all-to-all-start.3 = ((f32[128,1,256]{2,1,0:T(1,128)}), f32[128,1,256]{2,1,0:T(1,128)S(1)}, u32[]{:S(2)}, u32[]{:S(2)}) async-start(f32[128,1,256]{2,1,0:T(1,128)} %reshape.210), calls=%async_computation.3 | async-start | bytes 262144 | tf_op jit(solution)/shard_map/all_to_all | solution.py:167
where the time goes:
time: 157 us; the launch traced here: 156 us
  waiting for transfers between devices  56.4 us (36%)
  starting transfers between devices  43.2 us (28%)
  local copies, waits for them, and re-layouts  24 us (15%)
  blocking collectives  11.3 us (7%)
  matrix products  10.8 us (7%)
  other arithmetic  9.98 us (6%)
    all_to_all x1, starting transfers between devices, shards(): lax.all_to_all(both_in, 'ctx', split_axis=2, concat_axis=1, tiled=True)  19.2 us
    all_to_all x1, waiting for transfers between devices, shards(): lax.all_to_all(jnp.concatenate([spec_real, spec_imag], axis=0), 'ctx', sp...  14.8 us
    all_to_all x1, waiting for transfers between devices, shards(): lax.all_to_all(jnp.concatenate([back_real, back_imag], axis=0), 'ctx', sp...  14.5 us
    all_to_all x1, waiting for transfers between devices, shards(): lax.all_to_all(both_in, 'ctx', split_axis=2, concat_axis=1, tiled=True)  13.7 us
    all_to_all x1, waiting for transfers between devices, shards(): lax.all_to_all(time_vals, 'ctx', split_axis=1, concat_axis=2, tiled=True)  13.3 us
    unnamed x22, local copies, waits for them, and re-layouts  12.2 us
    psum x1, blocking collectives, shards(): power = lax.psum(jnp.sum(mixed * mixed, axis=0), 'tp')  11.3 us
    dot_general x16, matrix products, apply_cols(): return jnp.einsum('ckn,nm->ckm', values, table, precision=HIGHEST)  8.3 us
  transfers between devices with their start and end apart: 5, of which 4 were waited for; matrix products, arithmetic and copies ran while one was open for 2% of the time, Pallas kernels for 0%

commit v1 on v0

--- a/solution.py
+++ b/solution.py
@@ -76,6 +76,15 @@
         + taps[:, 1:2] * extended[:, 1:-1]
         + taps[:, 2:3] * extended[:, :-2]
     )
+
+
+def exchange_sum(x, axis):
+    length = lax.axis_size(axis)
+    step = 1
+    while step < length:
+        x = x + lax.ppermute(x, axis, [(i, i ^ step) for i in range(length)])
+        step *= 2
+    return x
 
 
 def pack_pairs(values, filter_count):
@@ -168,7 +177,7 @@
         chan_count, tok_count
     )
     mixed = q_conv * (convolved + skip_scale[:, None] * product)
-    power = lax.psum(jnp.sum(mixed * mixed, axis=0), "tp")
+    power = exchange_sum(jnp.sum(mixed * mixed, axis=0), "tp")
     total_channels = chan_count * lax.axis_size("tp")
     return (norm_gain[:, None] * mixed * lax.rsqrt(power / total_channels + 1e-05)).astype(
         jnp.bfloat16

time: 157 us -> 159 us (1.013)
  blocking collectives: 11.3 us -> 0 us
  starting transfers between devices: 43.2 us -> 54 us
  waiting for transfers between devices: 56.4 us -> 58.8 us
    psum x1 -> x0, blocking collectives: 11.3 us -> none  [shards(): power = lax.psum(jnp.sum(mixed * mixed, axis=0), 'tp')]
    ppermute x0 -> x2, starting transfers between devices: none -> 10.9 us  [exchange_sum(): x = x + lax.ppermute(x, axis, [(i, i ^ step) for i in range(length)])]
    ppermute x0 -> x2, waiting for transfers between devices: none -> 2.43 us  [exchange_sum(): x = x + lax.ppermute(x, axis, [(i, i ^ step) for i in range(length)])]
  transfers between devices with their start and end apart: 5 -> 7, of which waited for: 4 -> 6; matrix products, arithmetic and copies ran while one was open for 2% -> 2% of each run, Pallas kernels for 0% -> 0%
where the time goes in v1:
time: 159 us; the launch traced here: 158 us
  waiting for transfers between devices  58.8 us (37%)
  starting transfers between devices  54 us (34%)
  local copies, waits for them, and re-layouts  24 us (15%)
  matrix products  10.8 us (7%)
  other arithmetic  9.98 us (6%)
    all_to_all x1, starting transfers between devices, shards(): lax.all_to_all(both_in, 'ctx', split_axis=2, concat_axis=1, tiled=True)  19.2 us
    all_to_all x1, waiting for transfers between devices, shards(): lax.all_to_all(jnp.concatenate([spec_real, spec_imag], axis=0), 'ctx', sp...  14.8 us
    all_to_all x1, waiting for transfers between devices, shards(): lax.all_to_all(jnp.concatenate([back_real, back_imag], axis=0), 'ctx', sp...  14.5 us
    all_to_all x1, waiting for transfers between devices, shards(): lax.all_to_all(both_in, 'ctx', split_axis=2, concat_axis=1, tiled=True)  13.7 us
    all_to_all x1, waiting for transfers between devices, shards(): lax.all_to_all(time_vals, 'ctx', split_axis=1, concat_axis=2, tiled=True)  13.3 us
    unnamed x22, local copies, waits for them, and re-layouts  12.2 us
    ppermute x2, starting transfers between devices, exchange_sum(): x = x + lax.ppermute(x, axis, [(i, i ^ step) for i in range(length)])  10.9 us
    dot_general x16, matrix products, apply_cols(): return jnp.einsum('ckn,nm->ckm', values, table, precision=HIGHEST)  8.3 us
  transfers between devices with their start and end apart: 7, of which 6 were waited for; matrix products, arithmetic and copies ran while one was open for 2% of the time, Pallas kernels for 0%

profile of v1, /device:TPU:1, one launch (start us, length us, event | category | flops | bytes accessed | tf_op | source)
XLA Modules:
  0.0 158.2 jit_solution(6152494152402613921)
XLA Ops:
  0.0 0.8 slice.123
  0.9 0.8 slice.122
  1.7 0.8 slice.121
  2.6 5.0 %collective-permute-start = (bf16[3,32,2]{1,2,0:T(2,128)(2,1)S(1)}, bf16[3,32,2]{1,2,0:T(2,128)(2,1)S(1)}, u32[]{:S(2)}, u32[]{:S(2)}) collective-permute-start(bf16[3,32,2]{1,2,0:T(2,128)(2,1)S(1)} %pad_maximum_fusion.6), channel_id=1, source_target_pairs={{0,4},{4,8},{8,12},{12,16},{16,20},{20,24},{24,28},{28,32},{32,36}... | collective-permute-start | bytes 1160 | tf_op jit(solution)/shard_map/ppermute | solution.py:14
  8.4 0.9 convert_element_type.136
  9.3 0.9 convert_element_type.133
  11.6 1.2 reshape.204
  12.8 19.2 %all-to-all-start = ((f32[128,1,272]{2,1,0:T(1,128)}), f32[128,1,272]{2,1,0:T(1,128)S(1)}, u32[]{:S(2)}, u32[]{:S(2)}) async-start(f32[128,1,272]{2,1,0:T(1,128)} %reshape.204), calls=%async_computation | async-start | bytes 393216 | tf_op jit(solution)/shard_map/all_to_all | solution.py:127
  32.1 13.7 %all-to-all-done = f32[128,1,272]{2,1,0:T(1,128)S(1)} async-done(((f32[128,1,272]{2,1,0:T(1,128)}), f32[128,1,272]{2,1,0:T(1,128)S(1)}, u32[]{:S(2)}, u32[]{:S(2)}) %all-to-all-start) | async-done | bytes 139296 | tf_op jit(solution)/shard_map/all_to_all | solution.py:127
  46.3 1.1 reduce
  48.0 1.7 %reshape.203 = f32[2,2,8,8,128]{2,1,0,4,3:T(2,128)S(1)} reshape(f32[32,128,8,1]{0,2,1,3:T(8,128)S(1)} %bitcast.180) | data formatting | bytes 262144 | tf_op jit(solution)/shard_map/reshape | solution.py:91
  49.7 3.0 %fusion.231 = (f32[2,1,8,8,128]{2,1,0,4,3:T(1,128)S(1)}, f32[2,1,8,8,128]{2,1,0,4,3:T(1,128)}) fusion(f32[2,2,8,8,128]{2,1,0,4,3:T(2,128)S(1)} %reshape.203), kind=kLoop, calls=%fused_computation.289 | loop fusion | bytes 262144 | tf_op jit(solution)/shard_map/slice | solution.py:94
  52.7 1.4 copy.81
  54.1 1.1 copy.82
  59.2 1.8 %reshape.206 = f32[128,1,576]{2,1,0:T(1,128)} reshape(f32[128,16,36]{2,1,0:T(8,128)S(1)} %bitcast.182) | data formatting | bytes 589824
  61.0 6.4 %all-to-all-start.1 = ((f32[128,1,576]{2,1,0:T(1,128)}), f32[128,1,576]{2,1,0:T(1,128)S(1)}, u32[]{:S(2)}, u32[]{:S(2)}) async-start(f32[128,1,576]{2,1,0:T(1,128)} %reshape.206), calls=%async_computation.1 | async-start | bytes 655360 | tf_op jit(solution)/shard_map/all_to_all | solution.py:135
  67.5 14.8 %all-to-all-done.1 = f32[128,1,576]{2,1,0:T(1,128)S(1)} async-done(((f32[128,1,576]{2,1,0:T(1,128)}), f32[128,1,576]{2,1,0:T(1,128)S(1)}, u32[]{:S(2)}, u32[]{:S(2)}) %all-to-all-start.1) | async-done | bytes 294944 | tf_op jit(solution)/shard_map/all_to_all | solution.py:135
  82.4 1.4 reduce.1
  90.7 1.2 reshape.208
  91.8 6.4 %all-to-all-start.2 = ((f32[128,1,512]{2,1,0:T(1,128)}), f32[128,1,512]{2,1,0:T(1,128)S(1)}, u32[]{:S(2)}, u32[]{:S(2)}) async-start(f32[128,1,512]{2,1,0:T(1,128)} %reshape.208), calls=%async_computation.2 | async-start | bytes 524288 | tf_op jit(solution)/shard_map/all_to_all | solution.py:162
  98.3 14.5 %all-to-all-done.2 = f32[128,1,512]{2,1,0:T(1,128)S(1)} async-done(((f32[128,1,512]{2,1,0:T(1,128)}), f32[128,1,512]{2,1,0:T(1,128)S(1)}, u32[]{:S(2)}, u32[]{:S(2)}) %all-to-all-start.2) | async-done | bytes 262176 | tf_op jit(solution)/shard_map/all_to_all | solution.py:162
  112.8 1.3 reduce.2
  119.4 2.0 %reduce.3 = f32[1024,32]{1,0:T(8,128)S(1)} reduce(f32[1024,1,32]{2,1,0:T(1,128)S(1)} %bitcast.185, f32[]{:T(128)} %broadcast.503), dimensions={1}, to_apply=%bitcast.155.reduce_sub_computation | reduce | bytes 262148
  121.4 0.9 reshape.210
  122.3 6.1 %all-to-all-start.3 = ((f32[128,1,256]{2,1,0:T(1,128)}), f32[128,1,256]{2,1,0:T(1,128)S(1)}, u32[]{:S(2)}, u32[]{:S(2)}) async-start(f32[128,1,256]{2,1,0:T(1,128)} %reshape.210), calls=%async_computation.3 | async-start | bytes 262144 | tf_op jit(solution)/shard_map/all_to_all | solution.py:176
  128.5 13.3 %all-to-all-done.3 = f32[128,1,256]{2,1,0:T(1,128)S(1)} async-done(((f32[128,1,256]{2,1,0:T(1,128)}), f32[128,1,256]{2,1,0:T(1,128)S(1)}, u32[]{:S(2)}, u32[]{:S(2)}) %all-to-all-start.3) | async-done | bytes 131104 | tf_op jit(solution)/shard_map/all_to_all | solution.py:176
  141.9 1.0 reduce.4
  142.8 0.9 reshape.211
  144.2 8.2 %collective-permute-start.1 = (f32[1024]{0:T(1024)S(1)}, f32[1024]{0:T(1024)S(1)}, u32[]{:S(2)}, u32[]{:S(2)}) collective-permute-start(f32[1024]{0:T(1024)S(1)} %get-tuple-element.5), channel_id=1, source_target_pairs={{0,1},{1,0},{2,3},{3,2},{4,5},{5,4},{6,7},{7,6},{8,9},{9,8},{10,11... | collective-permute-start | bytes 12296 | tf_op jit(solution)/shard_map/ppermute | solution.py:85
  152.3 0.8 collective-permute-done.1
  153.1 2.7 %collective-permute-start.2 = (f32[1024]{0:T(1024)S(1)}, f32[1024]{0:T(1024)S(1)}, u32[]{:S(2)}, u32[]{:S(2)}) collective-permute-start(f32[1024]{0:T(1024)S(1)} %add.235), channel_id=1, source_target_pairs={{0,2},{1,3},{2,0},{3,1},{4,6},{5,7},{6,4},{7,5},{8,10},{9,11},{10,... | collective-permute-start | bytes 12296 | tf_op jit(solution)/shard_map/ppermute | solution.py:85
  155.8 1.6 %collective-permute-done.2 = f32[1024]{0:T(1024)S(1)} collective-permute-done((f32[1024]{0:T(1024)S(1)}, f32[1024]{0:T(1024)S(1)}, u32[]{:S(2)}, u32[]{:S(2)}) %collective-permute-start.2) | collective-permute-done | bytes 4128 | tf_op jit(solution)/shard_map/ppermute | solution.py:85
  (84 shorter events, 21.0 us)
Async XLA Ops:
  2.6 8.2 %collective-permute-start = (bf16[3,32,2]{1,2,0:T(2,128)(2,1)S(1)}, bf16[3,32,2]{1,2,0:T(2,128)(2,1)S(1)}, u32[]{:S(2)}, u32[]{:S(2)}) collective-permute-start(bf16[3,32,2]{1,2,0:T(2,128)(2,1)S(1)} %pad_maximum_fusion.6), channel_id=1, source_target_pairs={{0,4},{4,8},{8,12},{12,16},{16,20},{20,24},{24,28},{28,32},{32,36}... | collective-permute-start | bytes 1160 | tf_op jit(solution)/shard_map/ppermute | solution.py:14
  12.8 33.0 %all-to-all-start = ((f32[128,1,272]{2,1,0:T(1,128)}), f32[128,1,272]{2,1,0:T(1,128)S(1)}, u32[]{:S(2)}, u32[]{:S(2)}) async-start(f32[128,1,272]{2,1,0:T(1,128)} %reshape.204), calls=%async_computation | async-start | bytes 393216 | tf_op jit(solution)/shard_map/all_to_all | solution.py:127
  61.0 21.4 %all-to-all-start.1 = ((f32[128,1,576]{2,1,0:T(1,128)}), f32[128,1,576]{2,1,0:T(1,128)S(1)}, u32[]{:S(2)}, u32[]{:S(2)}) async-start(f32[128,1,576]{2,1,0:T(1,128)} %reshape.206), calls=%async_computation.1 | async-start | bytes 655360 | tf_op jit(solution)/shard_map/all_to_all | solution.py:135
  91.8 21.0 %all-to-all-start.2 = ((f32[128,1,512]{2,1,0:T(1,128)}), f32[128,1,512]{2,1,0:T(1,128)S(1)}, u32[]{:S(2)}, u32[]{:S(2)}) async-start(f32[128,1,512]{2,1,0:T(1,128)} %reshape.208), calls=%async_computation.2 | async-start | bytes 524288 | tf_op jit(solution)/shard_map/all_to_all | solution.py:162
  118.6 9.8 %copy-start = (bf16[32,1024]{1,0:T(8,128)(2,1)S(1)}, bf16[32,1024]{1,0:T(8,128)(2,1)}, u32[]{:S(2)}) copy-start(bf16[32,1024]{1,0:T(8,128)(2,1)} %param.7) | copy-start | bytes 196612
  119.1 24.9 %copy-start.2 = (f32[32]{0:T(128)S(1)}, f32[32]{0:T(128)}, u32[]{:S(2)}) copy-start(f32[32]{0:T(128)} %param.12) | copy-start | bytes 388
  119.4 38.1 %copy-start.1 = (f32[32]{0:T(128)S(1)}, f32[32]{0:T(128)}, u32[]{:S(2)}) copy-start(f32[32]{0:T(128)} %param.13) | copy-start | bytes 388
  122.3 19.6 %all-to-all-start.3 = ((f32[128,1,256]{2,1,0:T(1,128)}), f32[128,1,256]{2,1,0:T(1,128)S(1)}, u32[]{:S(2)}, u32[]{:S(2)}) async-start(f32[128,1,256]{2,1,0:T(1,128)} %reshape.210), calls=%async_computation.3 | async-start | bytes 262144 | tf_op jit(solution)/shard_map/all_to_all | solution.py:176
  144.2 9.0 %collective-permute-start.1 = (f32[1024]{0:T(1024)S(1)}, f32[1024]{0:T(1024)S(1)}, u32[]{:S(2)}, u32[]{:S(2)}) collective-permute-start(f32[1024]{0:T(1024)S(1)} %get-tuple-element.5), channel_id=1, source_target_pairs={{0,1},{1,0},{2,3},{3,2},{4,5},{5,4},{6,7},{7,6},{8,9},{9,8},{10,11... | collective-permute-start | bytes 12296 | tf_op jit(solution)/shard_map/ppermute | solution.py:85
  153.1 4.3 %collective-permute-start.2 = (f32[1024]{0:T(1024)S(1)}, f32[1024]{0:T(1024)S(1)}, u32[]{:S(2)}, u32[]{:S(2)}) collective-permute-start(f32[1024]{0:T(1024)S(1)} %add.235), channel_id=1, source_target_pairs={{0,2},{1,3},{2,0},{3,1},{4,6},{5,7},{6,4},{7,5},{8,10},{9,11},{10,... | collective-permute-start | bytes 12296 | tf_op jit(solution)/shard_map/ppermute | solution.py:85

commit v2 on v0

--- a/solution.py
+++ b/solution.py
@@ -52,10 +52,7 @@
 def forward_local(real_part, imag_part, first_len, ctx_count, ctx_index):
     rows_real = real_part.shape[1]
     padded_len = first_len * ctx_count * ctx_count
-    extra_rows = ((0, 0), (0, first_len - rows_real), (0, 0))
-    real_part = jnp.pad(real_part, extra_rows)
-    imag_part = jnp.pad(imag_part, extra_rows)
-    first_tables = grid_product(first_len, first_len, first_len)
+    first_tables = grid_product(first_len, rows_real, first_len)
     real_part, imag_part = dft_section(apply_rows, real_part, imag_part, first_tables, -1.0)
     real_part, imag_part = rotate(
         real_part, imag_part, grid_product(first_len, ctx_count, first_len * ctx_count), -1.0
@@ -78,20 +75,6 @@
     )
 
 
-def pack_pairs(values, filter_count):
-    grouped = values.reshape((filter_count, 2, -1) + values.shape[1:])
-    return (
-        grouped[:, 0].reshape((-1,) + values.shape[1:]),
-        grouped[:, 1].reshape((-1,) + values.shape[1:]),
-    )
-
-
-def unpack_pairs(real_part, imag_part, filter_count):
-    shape = (filter_count, 1, -1) + real_part.shape[1:]
-    both = jnp.concatenate([real_part.reshape(shape), imag_part.reshape(shape)], axis=1)
-    return both.reshape((-1,) + real_part.shape[1:])
-
-
 def shards(query_proj, key_proj, value_proj, short_taps, long_filter, skip_scale, norm_gain):
     chan_count = query_proj.shape[0]
     tok_count = query_proj.shape[1]
@@ -108,27 +91,30 @@
     k_conv = causal_three(key_proj, before[1], short_taps[1])
     v_conv = causal_three(value_proj, before[2], short_taps[2])
     product = k_conv * v_conv
+    halves = product.reshape(filter_count, 2, -1, tok_count)
     both_in = jnp.concatenate(
         [
-            product.reshape(chan_count, row_count, ctx_count),
-            long_filter.reshape(filter_count, row_count, ctx_count),
+            halves[:, 0].reshape(pair_count, tok_count),
+            long_filter,
+            halves[:, 1].reshape(pair_count, tok_count),
+            jnp.zeros_like(long_filter),
         ],
         axis=0,
     )
-    moved = lax.all_to_all(both_in, "ctx", split_axis=2, concat_axis=1, tiled=True)
-    moved = moved.reshape(chan_count + filter_count, row_count, ctx_count)
-    data_cols = moved[:chan_count]
-    filter_cols = moved[chan_count:]
-    pair_real, pair_imag = pack_pairs(data_cols, filter_count)
-    in_real = jnp.concatenate([pair_real, filter_cols], axis=0)
-    in_imag = jnp.concatenate([pair_imag, jnp.zeros_like(filter_cols)], axis=0)
-    spec_real, spec_imag = forward_local(in_real, in_imag, first_len, ctx_count, ctx_index)
+    row_total = pair_count + filter_count
+    moved = lax.all_to_all(
+        both_in.reshape(2 * row_total, row_count, ctx_count), "ctx", split_axis=2, concat_axis=1,
+        tiled=True,
+    )
+    moved = moved.reshape(2 * row_total, row_count, ctx_count)
+    spec_real, spec_imag = forward_local(
+        moved[:row_total], moved[row_total:], first_len, ctx_count, ctx_index
+    )
     spec = lax.all_to_all(
         jnp.concatenate([spec_real, spec_imag], axis=0), "ctx", split_axis=2, concat_axis=2,
         tiled=True,
     )
     square_tables = grid_product(ctx_count, ctx_count, ctx_count)
-    row_total = pair_count + filter_count
     spec_real, spec_imag = dft_section(
         apply_cols, spec[:row_total], spec[row_total:], square_tables, -1.0
     )
@@ -160,13 +146,13 @@
     back_real, back_imag = rotate(
         back_real, back_imag, grid_product(first_len, ctx_count, first_len * ctx_count), 1.0
     )
-    first_tables = grid_product(first_len, first_len, first_len)
-    time_real, time_imag = dft_section(apply_rows, back_real, back_imag, first_tables, 1.0)
-    time_vals = unpack_pairs(time_real[:, :row_count], time_imag[:, :row_count], filter_count)
+    last_tables = grid_product(row_count, first_len, first_len)
+    time_real, time_imag = dft_section(apply_rows, back_real, back_imag, last_tables, 1.0)
+    time_vals = jnp.concatenate([time_real, time_imag], axis=0)
     time_vals = time_vals.reshape(chan_count, row_count * ctx_count, 1) * (1.0 / padded_len)
-    convolved = lax.all_to_all(time_vals, "ctx", split_axis=1, concat_axis=2, tiled=True).reshape(
-        chan_count, tok_count
-    )
+    convolved = lax.all_to_all(time_vals, "ctx", split_axis=1, concat_axis=2, tiled=True)
+    convolved = convolved.reshape(2, filter_count, -1, tok_count).transpose(1, 0, 2, 3)
+    convolved = convolved.reshape(chan_count, tok_count)
     mixed = q_conv * (convolved + skip_scale[:, None] * product)
     power = lax.psum(jnp.sum(mixed * mixed, axis=0), "tp")
     total_channels = chan_count * lax.axis_size("tp")

time: 157 us -> 152 us (0.968)
  local copies, waits for them, and re-layouts: 24 us -> 17.7 us
  starting transfers between devices: 43.2 us -> 45.4 us
  other arithmetic: 9.98 us -> 8.37 us
    slice x5 -> x3, local copies, waits for them, and re-layouts: 3.39 us -> 0.59 us  [the longest x2 0.39 us: shards(): moved[row_total:]]
    all_to_all x1, starting transfers between devices: 19.2 us -> 21.3 us  [shards(): lax.all_to_all(both_in.reshape(2 * row_total, row_count, ctx_count), 'ctx...]
    convert_element_type x3, other arithmetic: 1.72 us -> 0.03 us  [causal_three(): values.astype(jnp.float32)]
    reshape x1, local copies, waits for them, and re-layouts: 1.66 us -> 0.03 us  [shards(): convolved.reshape(2, filter_count, -1, tok_count).transpose(1, 0, 2, 3)]
    unnamed x22 -> x30, local copies, waits for them, and re-layouts: 12.2 us -> 11.1 us
  transfers between devices with their start and end apart: 5 -> 5, of which waited for: 4 -> 4; matrix products, arithmetic and copies ran while one was open for 2% -> 0% of each run, Pallas kernels for 0% -> 0%
where the time goes in v2:
time: 152 us; the launch traced here: 151 us
  waiting for transfers between devices  56.6 us (37%)
  starting transfers between devices  45.4 us (30%)
  local copies, waits for them, and re-layouts  17.7 us (12%)
  blocking collectives  11.3 us (7%)
  matrix products  10.8 us (7%)
  other arithmetic  8.37 us (6%)
    all_to_all x1, starting transfers between devices, shards(): lax.all_to_all(both_in.reshape(2 * row_total, row_count, ctx_count), 'ctx...  21.3 us
    all_to_all x1, waiting for transfers between devices, shards(): lax.all_to_all(jnp.concatenate([spec_real, spec_imag], axis=0), 'ctx', sp...  14.9 us
    all_to_all x1, waiting for transfers between devices, shards(): lax.all_to_all(jnp.concatenate([back_real, back_imag], axis=0), 'ctx', sp...  14.5 us
    all_to_all x1, waiting for transfers between devices, shards(): lax.all_to_all(both_in.reshape(2 * row_total, row_count, ctx_count), 'ctx...  13.8 us
    all_to_all x1, waiting for transfers between devices, shards(): lax.all_to_all(time_vals, 'ctx', split_axis=1, concat_axis=2, tiled=True)  13.3 us
    psum x1, blocking collectives, shards(): power = lax.psum(jnp.sum(mixed * mixed, axis=0), 'tp')  11.3 us
    unnamed x30, local copies, waits for them, and re-layouts  11.1 us
    dot_general x16, matrix products, apply_cols(): return jnp.einsum('ckn,nm->ckm', values, table, precision=HIGHEST)  8.3 us
  transfers between devices with their start and end apart: 5, of which 4 were waited for; matrix products, arithmetic and copies ran while one was open for 0% of the time, Pallas kernels for 0%

profile of v2, /device:TPU:1, one launch (start us, length us, event | category | flops | bytes accessed | tf_op | source)
XLA Modules:
  0.0 150.8 jit_solution(6932710549709696402)
XLA Ops:
  0.0 0.8 slice.117
  0.9 0.8 slice.118
  1.8 0.8 slice.119
  2.7 5.2 %collective-permute-start = (bf16[3,32,2]{1,2,0:T(2,128)(2,1)S(1)}, bf16[3,32,2]{1,2,0:T(2,128)(2,1)S(1)}, u32[]{:S(2)}, u32[]{:S(2)}) collective-permute-start(bf16[3,32,2]{1,2,0:T(2,128)(2,1)S(1)} %pad_maximum_fusion.5), channel_id=1, source_target_pairs={{0,4},{4,8},{8,12},{12,16},{16,20},{20,24},{24,28},{28,32},{32,36}... | collective-permute-start | bytes 1160 | tf_op jit(solution)/shard_map/ppermute | solution.py:14
  8.0 0.6 copy-done.4
  9.6 1.2 reshape.200
  10.8 21.3 %all-to-all-start = ((f32[128,1,288]{2,1,0:T(1,128)}), f32[128,1,288]{2,1,0:T(1,128)S(1)}, u32[]{:S(2)}, u32[]{:S(2)}) async-start(f32[128,1,288]{2,1,0:T(1,128)} %reshape.200), calls=%async_computation | async-start | bytes 393216 | tf_op jit(solution)/shard_map/all_to_all | solution.py:105
  32.2 13.8 %all-to-all-done = f32[128,1,288]{2,1,0:T(1,128)S(1)} async-done(((f32[128,1,288]{2,1,0:T(1,128)}), f32[128,1,288]{2,1,0:T(1,128)S(1)}, u32[]{:S(2)}, u32[]{:S(2)}) %all-to-all-start) | async-done | bytes 147488 | tf_op jit(solution)/shard_map/all_to_all | solution.py:105
  46.6 1.1 reduce
  51.2 0.5 fusion.1
  51.7 0.5 multiply_subtract_fusion
  52.3 0.6 copy.85
  52.8 1.8 %reshape.202 = f32[128,1,576]{2,1,0:T(1,128)} reshape(f32[128,16,36]{2,1,0:T(8,128)S(1)} %bitcast.189) | data formatting | bytes 589824
  54.6 6.4 %all-to-all-start.1 = ((f32[128,1,576]{2,1,0:T(1,128)}), f32[128,1,576]{2,1,0:T(1,128)S(1)}, u32[]{:S(2)}, u32[]{:S(2)}) async-start(f32[128,1,576]{2,1,0:T(1,128)} %reshape.202), calls=%async_computation.1 | async-start | bytes 655360 | tf_op jit(solution)/shard_map/all_to_all | solution.py:113
  61.1 14.9 %all-to-all-done.1 = f32[128,1,576]{2,1,0:T(1,128)S(1)} async-done(((f32[128,1,576]{2,1,0:T(1,128)}), f32[128,1,576]{2,1,0:T(1,128)S(1)}, u32[]{:S(2)}, u32[]{:S(2)}) %all-to-all-start.1) | async-done | bytes 294944 | tf_op jit(solution)/shard_map/all_to_all | solution.py:113
  76.0 1.4 reduce.1
  77.5 0.7 reshape.203
  83.8 0.5 copy.88
  84.3 1.2 reshape.204
  85.5 6.4 %all-to-all-start.2 = ((f32[128,1,512]{2,1,0:T(1,128)}), f32[128,1,512]{2,1,0:T(1,128)S(1)}, u32[]{:S(2)}, u32[]{:S(2)}) async-start(f32[128,1,512]{2,1,0:T(1,128)} %reshape.204), calls=%async_computation.2 | async-start | bytes 524288 | tf_op jit(solution)/shard_map/all_to_all | solution.py:139
  91.9 14.5 %all-to-all-done.2 = f32[128,1,512]{2,1,0:T(1,128)S(1)} async-done(((f32[128,1,512]{2,1,0:T(1,128)}), f32[128,1,512]{2,1,0:T(1,128)S(1)}, u32[]{:S(2)}, u32[]{:S(2)}) %all-to-all-start.2) | async-done | bytes 262176 | tf_op jit(solution)/shard_map/all_to_all | solution.py:139
  106.5 1.3 reduce.2
  112.6 2.0 %reduce.3 = f32[1024,32]{1,0:T(8,128)S(1)} reduce(f32[1024,1,32]{2,1,0:T(1,128)S(1)} %bitcast.192, f32[]{:T(128)} %broadcast.458), dimensions={1}, to_apply=%bitcast.160.reduce_sub_computation | reduce | bytes 262148
  114.5 0.9 reshape.206
  115.4 6.3 %all-to-all-start.3 = ((f32[128,1,256]{2,1,0:T(1,128)}), f32[128,1,256]{2,1,0:T(1,128)S(1)}, u32[]{:S(2)}, u32[]{:S(2)}) async-start(f32[128,1,256]{2,1,0:T(1,128)} %reshape.206), calls=%async_computation.3 | async-start | bytes 262144 | tf_op jit(solution)/shard_map/all_to_all | solution.py:153
  121.8 13.3 %all-to-all-done.3 = f32[128,1,256]{2,1,0:T(1,128)S(1)} async-done(((f32[128,1,256]{2,1,0:T(1,128)}), f32[128,1,256]{2,1,0:T(1,128)S(1)}, u32[]{:S(2)}, u32[]{:S(2)}) %all-to-all-start.3) | async-done | bytes 131104 | tf_op jit(solution)/shard_map/all_to_all | solution.py:153
  135.2 1.0 reduce.4
  136.1 0.9 reshape.207
  137.4 0.6 copy-done.6
  138.2 11.3 %psum.7 = f32[1024]{0:T(1024)S(1)} all-reduce(f32[1024]{0:T(1024)S(1)} %get-tuple-element.5), channel_id=1, replica_groups=mesh['ctx'=128,'tp'=4] {'tp'}, use_global_device_ids=true, to_apply=%region_1.2 | all-reduce | flops 1024 | bytes 8192 | tf_op jit(solution)/shard_map/psum | solution.py:157
  149.5 0.7 copy-done.5
  150.1 0.7 multiply_convert_fusion
  (88 shorter events, 16.4 us)
Async XLA Ops:
  0.0 7.8 %copy-start = (bf16[32,1024]{1,0:T(8,128)(2,1)S(1)}, bf16[32,1024]{1,0:T(8,128)(2,1)}, u32[]{:S(2)}) copy-start(bf16[32,1024]{1,0:T(8,128)(2,1)} %param.8) | copy-start | bytes 196612
  2.7 5.2 %copy-start.1 = (bf16[32,1024]{1,0:T(8,128)(2,1)S(1)}, bf16[32,1024]{1,0:T(8,128)(2,1)}, u32[]{:S(2)}) copy-start(bf16[32,1024]{1,0:T(8,128)(2,1)} %param.9) | copy-start | bytes 196612
  2.7 6.1 %collective-permute-start = (bf16[3,32,2]{1,2,0:T(2,128)(2,1)S(1)}, bf16[3,32,2]{1,2,0:T(2,128)(2,1)S(1)}, u32[]{:S(2)}, u32[]{:S(2)}) collective-permute-start(bf16[3,32,2]{1,2,0:T(2,128)(2,1)S(1)} %pad_maximum_fusion.5), channel_id=1, source_target_pairs={{0,4},{4,8},{8,12},{12,16},{16,20},{20,24},{24,28},{28,32},{32,36}... | collective-permute-start | bytes 1160 | tf_op jit(solution)/shard_map/ppermute | solution.py:14
  7.9 0.7 copy-start.4
  8.0 0.7 copy-start.3
  10.8 35.2 %all-to-all-start = ((f32[128,1,288]{2,1,0:T(1,128)}), f32[128,1,288]{2,1,0:T(1,128)S(1)}, u32[]{:S(2)}, u32[]{:S(2)}) async-start(f32[128,1,288]{2,1,0:T(1,128)} %reshape.200), calls=%async_computation | async-start | bytes 393216 | tf_op jit(solution)/shard_map/all_to_all | solution.py:105
  54.6 21.4 %all-to-all-start.1 = ((f32[128,1,576]{2,1,0:T(1,128)}), f32[128,1,576]{2,1,0:T(1,128)S(1)}, u32[]{:S(2)}, u32[]{:S(2)}) async-start(f32[128,1,576]{2,1,0:T(1,128)} %reshape.202), calls=%async_computation.1 | async-start | bytes 655360 | tf_op jit(solution)/shard_map/all_to_all | solution.py:113
  85.5 21.0 %all-to-all-start.2 = ((f32[128,1,512]{2,1,0:T(1,128)}), f32[128,1,512]{2,1,0:T(1,128)S(1)}, u32[]{:S(2)}, u32[]{:S(2)}) async-start(f32[128,1,512]{2,1,0:T(1,128)} %reshape.204), calls=%async_computation.2 | async-start | bytes 524288 | tf_op jit(solution)/shard_map/all_to_all | solution.py:139
  115.4 6.3 %copy-start.2 = (bf16[32,1024]{1,0:T(8,128)(2,1)S(1)}, bf16[32,1024]{1,0:T(8,128)(2,1)}, u32[]{:S(2)}) copy-start(bf16[32,1024]{1,0:T(8,128)(2,1)} %param.7) | copy-start | bytes 196612
  115.4 19.7 %all-to-all-start.3 = ((f32[128,1,256]{2,1,0:T(1,128)}), f32[128,1,256]{2,1,0:T(1,128)S(1)}, u32[]{:S(2)}, u32[]{:S(2)}) async-start(f32[128,1,256]{2,1,0:T(1,128)} %reshape.206), calls=%async_computation.3 | async-start | bytes 262144 | tf_op jit(solution)/shard_map/all_to_all | solution.py:153
  137.3 0.7 copy-start.6
  149.5 0.7 copy-start.5

commit v3 on v2

--- a/solution.py
+++ b/solution.py
@@ -3,7 +3,11 @@
 import jax
 import jax.numpy as jnp
 from jax import lax
+from jax.experimental import pallas as pl
+from jax.experimental.pallas import tpu as pltpu
 from jax.sharding import PartitionSpec as P
+
+INTERPRET = False
 
 HIGHEST = lax.Precision.HIGHEST
 
@@ -73,6 +77,42 @@
         + taps[:, 1:2] * extended[:, 1:-1]
         + taps[:, 2:3] * extended[:, :-2]
     )
+
+
+def spectral_kernel(spec_ref, cos_ref, sin_ref, twc_ref, tws_ref, out_ref):
+    filter_count = (spec_ref.shape[0] - out_ref.shape[0]) // 2
+    pair_count = out_ref.shape[0] // 2
+    first_len, ctx_count = spec_ref.shape[1], spec_ref.shape[2]
+    row_total = pair_count + filter_count
+    cos_t = cos_ref[...]
+    sin_t = sin_ref[...]
+
+    def dot(a, b):
+        return jnp.dot(a, b, precision=HIGHEST, preferred_element_type=jnp.float32)
+
+    flat = (pair_count * first_len, ctx_count)
+    filt_flat = (filter_count * first_len, ctx_count)
+    x_re = spec_ref[0:pair_count].reshape(flat)
+    x_im = spec_ref[row_total : row_total + pair_count].reshape(flat)
+    h_re = spec_ref[pair_count:row_total].reshape(filt_flat)
+    h_im = spec_ref[row_total + pair_count :].reshape(filt_flat)
+    y_re = dot(x_re, cos_t) + dot(x_im, sin_t)
+    y_im = dot(x_im, cos_t) - dot(x_re, sin_t)
+    g_re = dot(h_re, cos_t) + dot(h_im, sin_t)
+    g_im = dot(h_im, cos_t) - dot(h_re, sin_t)
+    grouped = (filter_count, pair_count // filter_count, first_len, ctx_count)
+    y_re = y_re.reshape(grouped)
+    y_im = y_im.reshape(grouped)
+    g_re = g_re.reshape(filter_count, 1, first_len, ctx_count)
+    g_im = g_im.reshape(filter_count, 1, first_len, ctx_count)
+    p_re = (y_re * g_re - y_im * g_im).reshape(flat)
+    p_im = (y_re * g_im + y_im * g_re).reshape(flat)
+    b_re = (dot(p_re, cos_t) - dot(p_im, sin_t)).reshape(pair_count, first_len, ctx_count)
+    b_im = (dot(p_re, sin_t) + dot(p_im, cos_t)).reshape(pair_count, first_len, ctx_count)
+    tw_c = twc_ref[...][None]
+    tw_s = tws_ref[...][None]
+    out_ref[0:pair_count] = b_re * tw_c - b_im * tw_s
+    out_ref[pair_count:] = b_re * tw_s + b_im * tw_c
 
 
 def shards(query_proj, key_proj, value_proj, short_taps, long_filter, skip_scale, norm_gain):
@@ -115,29 +155,16 @@
         tiled=True,
     )
     square_tables = grid_product(ctx_count, ctx_count, ctx_count)
-    spec_real, spec_imag = dft_section(
-        apply_cols, spec[:row_total], spec[row_total:], square_tables, -1.0
-    )
-    data_real = spec_real[:pair_count]
-    data_imag = spec_imag[:pair_count]
-    filt_real = spec_real[pair_count:]
-    filt_imag = spec_imag[pair_count:]
-    grouped_shape = (filter_count, pair_count // filter_count, first_len, ctx_count)
-    group_real = data_real.reshape(grouped_shape)
-    group_imag = data_imag.reshape(grouped_shape)
-    prod_real = (group_real * filt_real[:, None] - group_imag * filt_imag[:, None]).reshape(
-        data_real.shape
-    )
-    prod_imag = (group_real * filt_imag[:, None] + group_imag * filt_real[:, None]).reshape(
-        data_real.shape
-    )
-    back_real, back_imag = dft_section(apply_cols, prod_real, prod_imag, square_tables, 1.0)
     freq_first = lax.broadcasted_iota(jnp.int32, (first_len, ctx_count), 0)
     time_third = lax.broadcasted_iota(jnp.int32, (first_len, ctx_count), 1)
     twist = trig_pair((freq_first + first_len * ctx_index) * time_third, padded_len)
-    back_real, back_imag = rotate(back_real, back_imag, twist, 1.0)
+    back_both = pl.pallas_call(
+        spectral_kernel,
+        out_shape=jax.ShapeDtypeStruct((2 * pair_count, first_len, ctx_count), jnp.float32),
+        interpret=INTERPRET,
+    )(spec, square_tables[0], square_tables[1], twist[0], twist[1])
     back = lax.all_to_all(
-        jnp.concatenate([back_real, back_imag], axis=0), "ctx", split_axis=2, concat_axis=2,
+        back_both, "ctx", split_axis=2, concat_axis=2,
         tiled=True,
     )
     back_real, back_imag = dft_section(

time: 152 us -> 151 us (level)
  matrix products: 10.8 us -> 6.68 us
  Pallas kernels: 0 us -> 3.47 us
    dot_general x16 -> x8, matrix products: 8.3 us -> 4.15 us  [apply_cols(): return jnp.einsum('ckn,nm->ckm', values, table, precision=HIGHEST)]
    pallas_call x0 -> x1, Pallas kernels: none -> 3.47 us  [shards(): pl.pallas_call(spectral_kernel, out_shape=jax.ShapeDtypeStruct((2 * pair_...]
    sin x1 -> x3, other arithmetic: 0.06 us -> 1.71 us  [trig_pair(): return (jnp.cos(angle), jnp.sin(angle))]
    all_to_all x1, waiting for transfers between devices: 14.9 us -> 13.4 us  [shards(): lax.all_to_all(jnp.concatenate([spec_real, spec_imag], axis=0), 'ctx', sp...]
    unnamed x30 -> x28, local copies, waits for them, and re-layouts: 11.1 us -> 10.1 us
  transfers between devices with their start and end apart: 5 -> 5, of which waited for: 4 -> 4; matrix products, arithmetic and copies ran while one was open for 0% -> 1% of each run, Pallas kernels for 0% -> 0%
where the time goes in v3:
time: 151 us; the launch traced here: 150 us
  waiting for transfers between devices  55.2 us (37%)
  starting transfers between devices  45.5 us (30%)
  local copies, waits for them, and re-layouts  18.5 us (12%)
  blocking collectives  11.2 us (7%)
  other arithmetic  9.35 us (6%)
  matrix products  6.68 us (4%)
  Pallas kernels  3.47 us (2%)
    all_to_all x1, starting transfers between devices, shards(): lax.all_to_all(both_in.reshape(2 * row_total, row_count, ctx_count), 'ctx...  21.3 us
    all_to_all x1, waiting for transfers between devices, shards(): lax.all_to_all(back_both, 'ctx', split_axis=2, concat_axis=2, tiled=True)  14.6 us
    all_to_all x1, waiting for transfers between devices, shards(): lax.all_to_all(both_in.reshape(2 * row_total, row_count, ctx_count), 'ctx...  13.8 us
    all_to_all x1, waiting for transfers between devices, shards(): lax.all_to_all(jnp.concatenate([spec_real, spec_imag], axis=0), 'ctx', sp...  13.4 us
    all_to_all x1, waiting for transfers between devices, shards(): lax.all_to_all(time_vals, 'ctx', split_axis=1, concat_axis=2, tiled=True)  13.3 us
    psum x1, blocking collectives, shards(): power = lax.psum(jnp.sum(mixed * mixed, axis=0), 'tp')  11.2 us
    unnamed x28, local copies, waits for them, and re-layouts  10.1 us
    all_to_all x1, starting transfers between devices, shards(): lax.all_to_all(back_both, 'ctx', split_axis=2, concat_axis=2, tiled=True)  6.4 us
  transfers between devices with their start and end apart: 5, of which 4 were waited for; matrix products, arithmetic and copies ran while one was open for 1% of the time, Pallas kernels for 0%

profile of v3, /device:TPU:1, one launch (start us, length us, event | category | flops | bytes accessed | tf_op | source)
XLA Modules:
  0.0 150.4 jit_solution(2017785988331999164)
XLA Ops:
  0.0 0.8 slice.99
  0.9 0.8 slice.100
  1.8 0.8 slice.101
  2.7 5.2 %collective-permute-start = (bf16[3,32,2]{1,2,0:T(2,128)(2,1)S(1)}, bf16[3,32,2]{1,2,0:T(2,128)(2,1)S(1)}, u32[]{:S(2)}, u32[]{:S(2)}) collective-permute-start(bf16[3,32,2]{1,2,0:T(2,128)(2,1)S(1)} %pad_maximum_fusion.4), channel_id=1, source_target_pairs={{0,4},{4,8},{8,12},{12,16},{16,20},{20,24},{24,28},{28,32},{32,36}... | collective-permute-start | bytes 1160 | tf_op jit(solution)/shard_map/ppermute | solution.py:18
  9.6 1.2 reshape.145
  10.8 21.3 %all-to-all-start = ((f32[128,1,288]{2,1,0:T(1,128)}), f32[128,1,288]{2,1,0:T(1,128)S(1)}, u32[]{:S(2)}, u32[]{:S(2)}) async-start(f32[128,1,288]{2,1,0:T(1,128)} %reshape.145), calls=%async_computation | async-start | bytes 393216 | tf_op jit(solution)/shard_map/all_to_all | solution.py:145
  32.2 13.8 %all-to-all-done = f32[128,1,288]{2,1,0:T(1,128)S(1)} async-done(((f32[128,1,288]{2,1,0:T(1,128)}), f32[128,1,288]{2,1,0:T(1,128)S(1)}, u32[]{:S(2)}, u32[]{:S(2)}) %all-to-all-start) | async-done | bytes 147488 | tf_op jit(solution)/shard_map/all_to_all | solution.py:145
  46.5 1.0 reduce
  52.7 1.8 %reshape.147 = f32[128,1,576]{2,1,0:T(1,128)} reshape(f32[128,16,36]{2,1,0:T(8,128)S(1)} %bitcast.148) | data formatting | bytes 589824
  54.5 6.4 %all-to-all-start.1 = ((f32[128,1,576]{2,1,0:T(1,128)}), f32[128,1,576]{2,1,0:T(1,128)S(1)}, u32[]{:S(2)}, u32[]{:S(2)}) async-start(f32[128,1,576]{2,1,0:T(1,128)} %reshape.147), calls=%async_computation.1 | async-start | bytes 655360 | tf_op jit(solution)/shard_map/all_to_all | solution.py:153
  60.9 0.9 fusion.42
  61.8 0.7 fusion.87
  62.5 13.4 %all-to-all-done.1 = f32[128,1,576]{2,1,0:T(1,128)S(1)} async-done(((f32[128,1,576]{2,1,0:T(1,128)}), f32[128,1,576]{2,1,0:T(1,128)S(1)}, u32[]{:S(2)}, u32[]{:S(2)}) %all-to-all-start.1) | async-done | bytes 294944 | tf_op jit(solution)/shard_map/all_to_all | solution.py:153
  75.9 1.3 reduce.1
  77.2 0.7 reshape.148
  78.0 1.2 copy.85.spec_ref
  79.2 3.5 %shard_map.73 = f32[32,16,128]{2,1,0:T(8,128)} custom-call(f32[36,16,128]{2,1,0:T(8,128)} %copy.85.spec_ref, f32[128,128]{1,0:T(8,128)} %get-tuple-element.40.cos_ref, f32[128,128]{1,0:T(8,128)} %get-tuple-element.39.sin_ref, f32[16,128]{1,0:T(8,128)} %get-tuple-element.31.twc_ref, f32[16,128]{1,0:T(8,128)} %get-tuple-element.30.tws_ref), custom_call_target="tpu_custom_call" | custom-call | tf_op jit(solution)/shard_map/pallas_call | solution.py:161
  82.6 1.5 copy.86
  84.1 1.1 reshape.149
  85.3 6.4 %all-to-all-start.2 = ((f32[128,1,512]{2,1,0:T(1,128)}), f32[128,1,512]{2,1,0:T(1,128)S(1)}, u32[]{:S(2)}, u32[]{:S(2)}) async-start(f32[128,1,512]{2,1,0:T(1,128)} %reshape.149), calls=%async_computation.2 | async-start | bytes 524288 | tf_op jit(solution)/shard_map/all_to_all | solution.py:166
  91.7 14.6 %all-to-all-done.2 = f32[128,1,512]{2,1,0:T(1,128)S(1)} async-done(((f32[128,1,512]{2,1,0:T(1,128)}), f32[128,1,512]{2,1,0:T(1,128)S(1)}, u32[]{:S(2)}, u32[]{:S(2)}) %all-to-all-start.2) | async-done | bytes 262176 | tf_op jit(solution)/shard_map/all_to_all | solution.py:166
  106.3 1.2 reduce.2
  112.3 1.9 %reduce.3 = f32[1024,32]{1,0:T(8,128)S(1)} reduce(f32[1024,1,32]{2,1,0:T(1,128)S(1)} %bitcast.152, f32[]{:T(128)} %broadcast.339), dimensions={1}, to_apply=%bitcast.130.reduce_sub_computation | reduce | bytes 262148
  114.2 0.9 reshape.151
  115.1 6.3 %all-to-all-start.3 = ((f32[128,1,256]{2,1,0:T(1,128)}), f32[128,1,256]{2,1,0:T(1,128)S(1)}, u32[]{:S(2)}, u32[]{:S(2)}) async-start(f32[128,1,256]{2,1,0:T(1,128)} %reshape.151), calls=%async_computation.3 | async-start | bytes 262144 | tf_op jit(solution)/shard_map/all_to_all | solution.py:180
  121.5 13.3 %all-to-all-done.3 = f32[128,1,256]{2,1,0:T(1,128)S(1)} async-done(((f32[128,1,256]{2,1,0:T(1,128)}), f32[128,1,256]{2,1,0:T(1,128)S(1)}, u32[]{:S(2)}, u32[]{:S(2)}) %all-to-all-start.3) | async-done | bytes 131104 | tf_op jit(solution)/shard_map/all_to_all | solution.py:180
  134.9 0.9 reduce.4
  135.7 0.9 reshape.152
  137.0 0.6 copy-done.6
  137.8 11.2 %psum.7 = f32[1024]{0:T(1024)S(1)} all-reduce(f32[1024]{0:T(1024)S(1)} %get-tuple-element.5), channel_id=1, replica_groups=mesh['ctx'=128,'tp'=4] {'tp'}, use_global_device_ids=true, to_apply=%region_1.2 | all-reduce | flops 1024 | bytes 8192 | tf_op jit(solution)/shard_map/psum | solution.py:184
  149.0 0.7 copy-done.5
  149.7 0.7 multiply_convert_fusion
  (76 shorter events, 13.0 us)
Async XLA Ops:
  0.0 7.8 %copy-start = (bf16[32,1024]{1,0:T(8,128)(2,1)S(1)}, bf16[32,1024]{1,0:T(8,128)(2,1)}, u32[]{:S(2)}) copy-start(bf16[32,1024]{1,0:T(8,128)(2,1)} %param.8) | copy-start | bytes 196612
  2.7 5.2 %copy-start.1 = (bf16[32,1024]{1,0:T(8,128)(2,1)S(1)}, bf16[32,1024]{1,0:T(8,128)(2,1)}, u32[]{:S(2)}) copy-start(bf16[32,1024]{1,0:T(8,128)(2,1)} %param.9) | copy-start | bytes 196612
  2.7 6.1 %collective-permute-start = (bf16[3,32,2]{1,2,0:T(2,128)(2,1)S(1)}, bf16[3,32,2]{1,2,0:T(2,128)(2,1)S(1)}, u32[]{:S(2)}, u32[]{:S(2)}) collective-permute-start(bf16[3,32,2]{1,2,0:T(2,128)(2,1)S(1)} %pad_maximum_fusion.4), channel_id=1, source_target_pairs={{0,4},{4,8},{8,12},{12,16},{16,20},{20,24},{24,28},{28,32},{32,36}... | collective-permute-start | bytes 1160 | tf_op jit(solution)/shard_map/ppermute | solution.py:18
  7.9 0.7 copy-start.4
  8.0 0.7 copy-start.3
  10.8 35.2 %all-to-all-start = ((f32[128,1,288]{2,1,0:T(1,128)}), f32[128,1,288]{2,1,0:T(1,128)S(1)}, u32[]{:S(2)}, u32[]{:S(2)}) async-start(f32[128,1,288]{2,1,0:T(1,128)} %reshape.145), calls=%async_computation | async-start | bytes 393216 | tf_op jit(solution)/shard_map/all_to_all | solution.py:145
  54.5 21.4 %all-to-all-start.1 = ((f32[128,1,576]{2,1,0:T(1,128)}), f32[128,1,576]{2,1,0:T(1,128)S(1)}, u32[]{:S(2)}, u32[]{:S(2)}) async-start(f32[128,1,576]{2,1,0:T(1,128)} %reshape.147), calls=%async_computation.1 | async-start | bytes 655360 | tf_op jit(solution)/shard_map/all_to_all | solution.py:153
  85.3 21.1 %all-to-all-start.2 = ((f32[128,1,512]{2,1,0:T(1,128)}), f32[128,1,512]{2,1,0:T(1,128)S(1)}, u32[]{:S(2)}, u32[]{:S(2)}) async-start(f32[128,1,512]{2,1,0:T(1,128)} %reshape.149), calls=%async_computation.2 | async-start | bytes 524288 | tf_op jit(solution)/shard_map/all_to_all | solution.py:166
  115.1 6.3 %copy-start.2 = (bf16[32,1024]{1,0:T(8,128)(2,1)S(1)}, bf16[32,1024]{1,0:T(8,128)(2,1)}, u32[]{:S(2)}) copy-start(bf16[32,1024]{1,0:T(8,128)(2,1)} %param.7) | copy-start | bytes 196612
  115.1 19.8 %all-to-all-start.3 = ((f32[128,1,256]{2,1,0:T(1,128)}), f32[128,1,256]{2,1,0:T(1,128)S(1)}, u32[]{:S(2)}, u32[]{:S(2)}) async-start(f32[128,1,256]{2,1,0:T(1,128)} %reshape.151), calls=%async_computation.3 | async-start | bytes 262144 | tf_op jit(solution)/shard_map/all_to_all | solution.py:180
  136.9 0.7 copy-start.6
  149.0 0.7 copy-start.5

commit v4 on v2

--- a/solution.py
+++ b/solution.py
@@ -73,6 +73,43 @@
         + taps[:, 1:2] * extended[:, 1:-1]
         + taps[:, 2:3] * extended[:, :-2]
     )
+
+
+def row_blocks(tables, direction):
+    cos_table, sin_table = tables
+    return jnp.stack(
+        [
+            jnp.stack([cos_table, -direction * sin_table], axis=1),
+            jnp.stack([direction * sin_table, cos_table], axis=1),
+        ]
+    )
+
+
+def col_blocks(tables, direction):
+    cos_table, sin_table = tables
+    return jnp.stack(
+        [
+            jnp.stack([cos_table, direction * sin_table], axis=1),
+            jnp.stack([-direction * sin_table, cos_table], axis=1),
+        ]
+    )
+
+
+def complex_rows(tables, values, direction):
+    return jnp.einsum("ukst,ctsn->ckun", row_blocks(tables, direction), values, precision=HIGHEST)
+
+
+def complex_cols(tables, values, direction):
+    return jnp.einsum("cksn,snum->ckum", values, col_blocks(tables, direction), precision=HIGHEST)
+
+
+def complex_rotate(values, tables, direction):
+    cos_table, sin_table = tables
+    real_part = values[:, :, 0]
+    imag_part = values[:, :, 1]
+    new_real = real_part * cos_table - direction * imag_part * sin_table
+    new_imag = direction * real_part * sin_table + imag_part * cos_table
+    return jnp.stack([new_real, new_imag], axis=2)
 
 
 def shards(query_proj, key_proj, value_proj, short_taps, long_filter, skip_scale, norm_gain):
@@ -106,49 +143,35 @@
         both_in.reshape(2 * row_total, row_count, ctx_count), "ctx", split_axis=2, concat_axis=1,
         tiled=True,
     )
-    moved = moved.reshape(2 * row_total, row_count, ctx_count)
-    spec_real, spec_imag = forward_local(
-        moved[:row_total], moved[row_total:], first_len, ctx_count, ctx_index
-    )
-    spec = lax.all_to_all(
-        jnp.concatenate([spec_real, spec_imag], axis=0), "ctx", split_axis=2, concat_axis=2,
-        tiled=True,
+    values = moved.reshape(2, row_total, row_count, ctx_count).transpose(1, 2, 0, 3)
+    values = complex_rows(grid_product(first_len, row_count, first_len), values, -1.0)
+    values = complex_rotate(
+        values, grid_product(first_len, ctx_count, first_len * ctx_count), -1.0
     )
     square_tables = grid_product(ctx_count, ctx_count, ctx_count)
-    spec_real, spec_imag = dft_section(
-        apply_cols, spec[:row_total], spec[row_total:], square_tables, -1.0
-    )
-    data_real = spec_real[:pair_count]
-    data_imag = spec_imag[:pair_count]
-    filt_real = spec_real[pair_count:]
-    filt_imag = spec_imag[pair_count:]
-    grouped_shape = (filter_count, pair_count // filter_count, first_len, ctx_count)
-    group_real = data_real.reshape(grouped_shape)
-    group_imag = data_imag.reshape(grouped_shape)
-    prod_real = (group_real * filt_real[:, None] - group_imag * filt_imag[:, None]).reshape(
-        data_real.shape
-    )
-    prod_imag = (group_real * filt_imag[:, None] + group_imag * filt_real[:, None]).reshape(
-        data_real.shape
-    )
-    back_real, back_imag = dft_section(apply_cols, prod_real, prod_imag, square_tables, 1.0)
+    values = complex_cols(square_tables, values, -1.0)
     freq_first = lax.broadcasted_iota(jnp.int32, (first_len, ctx_count), 0)
+    freq_second = lax.broadcasted_iota(jnp.int32, (first_len, ctx_count), 1)
+    twist = trig_pair((freq_first + first_len * freq_second) * ctx_index, padded_len)
+    values = complex_rotate(values, twist, -1.0)
+    spec = lax.all_to_all(values, "ctx", split_axis=3, concat_axis=3, tiled=True)
+    spec = complex_cols(square_tables, spec, -1.0)
+    data = spec[:pair_count].reshape(filter_count, pair_count // filter_count, first_len, 2, ctx_count)
+    filt = spec[pair_count:][:, None]
+    prod_real = data[:, :, :, 0] * filt[:, :, :, 0] - data[:, :, :, 1] * filt[:, :, :, 1]
+    prod_imag = data[:, :, :, 0] * filt[:, :, :, 1] + data[:, :, :, 1] * filt[:, :, :, 0]
+    prod = jnp.stack([prod_real, prod_imag], axis=3).reshape(pair_count, first_len, 2, ctx_count)
+    back = complex_cols(square_tables, prod, 1.0)
     time_third = lax.broadcasted_iota(jnp.int32, (first_len, ctx_count), 1)
     twist = trig_pair((freq_first + first_len * ctx_index) * time_third, padded_len)
-    back_real, back_imag = rotate(back_real, back_imag, twist, 1.0)
-    back = lax.all_to_all(
-        jnp.concatenate([back_real, back_imag], axis=0), "ctx", split_axis=2, concat_axis=2,
-        tiled=True,
-    )
-    back_real, back_imag = dft_section(
-        apply_cols, back[:pair_count], back[pair_count:], square_tables, 1.0
-    )
-    back_real, back_imag = rotate(
-        back_real, back_imag, grid_product(first_len, ctx_count, first_len * ctx_count), 1.0
-    )
-    last_tables = grid_product(row_count, first_len, first_len)
-    time_real, time_imag = dft_section(apply_rows, back_real, back_imag, last_tables, 1.0)
-    time_vals = jnp.concatenate([time_real, time_imag], axis=0)
+    back = complex_rotate(back, twist, 1.0)
+    back = lax.all_to_all(back, "ctx", split_axis=3, concat_axis=3, tiled=True)
+    back = complex_cols(square_tables, back, 1.0)
+    back = complex_rotate(
+        back, grid_product(first_len, ctx_count, first_len * ctx_count), 1.0
+    )
+    time_vals = complex_rows(grid_product(row_count, first_len, first_len), back, 1.0)
+    time_vals = time_vals.transpose(2, 0, 1, 3)
     time_vals = time_vals.reshape(chan_count, row_count * ctx_count, 1) * (1.0 / padded_len)
     convolved = lax.all_to_all(time_vals, "ctx", split_axis=1, concat_axis=2, tiled=True)
     convolved = convolved.reshape(2, filter_count, -1, tok_count).transpose(1, 0, 2, 3)

time: 152 us -> 158 us (1.039)
  local copies, waits for them, and re-layouts: 17.7 us -> 30 us
  matrix products: 10.8 us -> 6.02 us
  starting transfers between devices: 45.4 us -> 42.1 us
  other arithmetic: 8.37 us -> 11 us
    dot_general x24 -> x6, matrix products: 10.8 us -> 6.02 us  [the longest x4 5.26 us: complex_cols(): jnp.einsum('cksn,snum->ckum', values, col_blocks(tables, direction), prec...]
    unnamed x30 -> x18, local copies, waits for them, and re-layouts: 11.1 us -> 15.8 us
    all_to_all x0 -> x3, local copies, waits for them, and re-layouts: none -> 4.4 us  [the longest x2 4.23 us: shards(): lax.all_to_all(values, 'ctx', split_axis=3, concat_axis=3, tiled=True)]
    another operation x0 -> x2, local copies, waits for them, and re-layouts: none -> 3.79 us  [complex_rotate(): return jnp.stack([new_real, new_imag], axis=2)]
    all_to_all x1, starting transfers between devices: 21.3 us -> 18.2 us  [shards(): lax.all_to_all(both_in.reshape(2 * row_total, row_count, ctx_count), 'ctx...]
    convert_element_type x3, other arithmetic: 0.03 us -> 1.72 us  [causal_three(): values.astype(jnp.float32)]
  transfers between devices with their start and end apart: 5 -> 5, of which waited for: 4 -> 4; matrix products, arithmetic and copies ran while one was open for 0% -> 3% of each run, Pallas kernels for 0% -> 0%
where the time goes in v4:
time: 158 us
  waiting for transfers between devices  56.7 us (36%)
  starting transfers between devices  42.1 us (27%)
  local copies, waits for them, and re-layouts  30 us (19%)
  blocking collectives  11.2 us (7%)
  other arithmetic  11 us (7%)
  matrix products  6.02 us (4%)
    all_to_all x1, starting transfers between devices, shards(): lax.all_to_all(both_in.reshape(2 * row_total, row_count, ctx_count), 'ctx...  18.2 us
    unnamed x18, local copies, waits for them, and re-layouts  15.8 us
    all_to_all x1, waiting for transfers between devices, shards(): lax.all_to_all(values, 'ctx', split_axis=3, concat_axis=3, tiled=True)  15.1 us
    all_to_all x1, waiting for transfers between devices, shards(): back = lax.all_to_all(back, 'ctx', split_axis=3, concat_axis=3, tiled=True)  14.4 us
    all_to_all x1, waiting for transfers between devices, shards(): lax.all_to_all(both_in.reshape(2 * row_total, row_count, ctx_count), 'ctx...  13.8 us
    all_to_all x1, waiting for transfers between devices, shards(): lax.all_to_all(time_vals, 'ctx', split_axis=1, concat_axis=2, tiled=True)  13.3 us
    psum x1, blocking collectives, shards(): power = lax.psum(jnp.sum(mixed * mixed, axis=0), 'tp')  11.2 us
    all_to_all x1, starting transfers between devices, shards(): back = lax.all_to_all(back, 'ctx', split_axis=3, concat_axis=3, tiled=True)  6.37 us
  transfers between devices with their start and end apart: 5, of which 4 were waited for; matrix products, arithmetic and copies ran while one was open for 3% of the time, Pallas kernels for 0%

profile of v4, /device:TPU:1, one launch (start us, length us, event | category | flops | bytes accessed | tf_op | source)
XLA Modules:
  0.0 157.6 jit_solution(9332053510533246783)
XLA Ops:
  0.0 0.8 slice.127
  0.9 0.8 slice.128
  1.7 0.8 slice.129
  2.6 5.0 %collective-permute-start = (bf16[3,32,2]{1,2,0:T(2,128)(2,1)S(1)}, bf16[3,32,2]{1,2,0:T(2,128)(2,1)S(1)}, u32[]{:S(2)}, u32[]{:S(2)}) collective-permute-start(bf16[3,32,2]{1,2,0:T(2,128)(2,1)S(1)} %pad_maximum_fusion.10), channel_id=1, source_target_pairs={{0,4},{4,8},{8,12},{12,16},{16,20},{20,24},{24,28},{28,32},{32,36}... | collective-permute-start | bytes 1160 | tf_op jit(solution)/shard_map/ppermute | solution.py:14
  7.7 0.9 convert_element_type.158
  8.5 0.9 convert_element_type.161
  12.5 1.2 reshape.400
  13.7 18.2 %all-to-all-start = ((f32[128,1,288]{2,1,0:T(1,128)}), f32[128,1,288]{2,1,0:T(1,128)S(1)}, u32[]{:S(2)}, u32[]{:S(2)}) async-start(f32[128,1,288]{2,1,0:T(1,128)} %reshape.400), calls=%async_computation | async-start | bytes 393216 | tf_op jit(solution)/shard_map/all_to_all | solution.py:142
  32.0 13.8 %all-to-all-done = f32[128,1,288]{2,1,0:T(1,128)S(1)} async-done(((f32[128,1,288]{2,1,0:T(1,128)}), f32[128,1,288]{2,1,0:T(1,128)S(1)}, u32[]{:S(2)}, u32[]{:S(2)}) %all-to-all-start) | async-done | bytes 147488 | tf_op jit(solution)/shard_map/all_to_all | solution.py:142
  46.4 1.1 reduce
  49.7 1.9 %copy.81 = f32[18,16,2,128]{0,1,2,3:T(8,128)S(1)} copy(f32[18,16,2,128]{3,1,2,0:T(8,128)S(1)} %pad_maximum_fusion) | data formatting | bytes 589824 | tf_op jit(solution)/shard_map/stack | solution.py:112
  51.6 3.0 %reshape.402 = f32[128,1,576]{2,1,0:T(1,128)} reshape(f32[128,2,16,18]{3,2,1,0:T(8,128)S(1)} %bitcast.191) | data formatting | bytes 589824
  54.6 6.3 %all-to-all-start.1 = ((f32[128,1,576]{2,1,0:T(1,128)}), f32[128,1,576]{2,1,0:T(1,128)S(1)}, u32[]{:S(2)}, u32[]{:S(2)}) async-start(f32[128,1,576]{2,1,0:T(1,128)} %reshape.402), calls=%async_computation.1 | async-start | bytes 655360 | tf_op jit(solution)/shard_map/all_to_all | solution.py:157
  61.1 15.1 %all-to-all-done.1 = f32[128,1,576]{2,1,0:T(1,128)S(1)} async-done(((f32[128,1,576]{2,1,0:T(1,128)}), f32[128,1,576]{2,1,0:T(1,128)S(1)}, u32[]{:S(2)}, u32[]{:S(2)}) %all-to-all-start.1) | async-done | bytes 294944 | tf_op jit(solution)/shard_map/all_to_all | solution.py:157
  76.1 1.4 reduce.1
  77.6 2.4 %reshape.403 = f32[128,2,16,18]{3,2,1,0:T(8,128)S(1)} reshape(f32[128,576]{1,0:T(8,128)S(1)} %reduce.1) | data formatting | bytes 589824
  80.0 1.5 bitcast_bitcast_fusion.1
  81.5 2.7 %copy.95 = f32[18,16,2,128,1]{3,1,2,4,0:T(8,128)S(1)} copy(f32[18,16,2,128,1]{0,1,2,3,4:T(8,128)} %bitcast_bitcast_fusion.1) | data formatting | bytes 589824 | tf_op jit(solution)/shard_map/all_to_all | solution.py:157
  85.2 1.9 %copy.84 = f32[16,16,2,128]{1,2,0,3:T(2,128)S(1)} copy(f32[16,16,2,128]{3,1,2,0:T(8,128)S(1)} %pad_maximum_fusion.2) | data formatting | bytes 524288 | tf_op jit(solution)/shard_map/stack | solution.py:112
  87.1 3.6 %reshape.404 = f32[128,1,512]{2,1,0:T(1,128)} reshape(f32[128,16,2,16]{3,2,1,0:T(2,128)S(1)} %bitcast.192) | data formatting | bytes 524288
  90.7 6.4 %all-to-all-start.2 = ((f32[128,1,512]{2,1,0:T(1,128)}), f32[128,1,512]{2,1,0:T(1,128)S(1)}, u32[]{:S(2)}, u32[]{:S(2)}) async-start(f32[128,1,512]{2,1,0:T(1,128)} %reshape.404), calls=%async_computation.2 | async-start | bytes 524288 | tf_op jit(solution)/shard_map/all_to_all | solution.py:168
  97.3 14.4 %all-to-all-done.2 = f32[128,1,512]{2,1,0:T(1,128)S(1)} async-done(((f32[128,1,512]{2,1,0:T(1,128)}), f32[128,1,512]{2,1,0:T(1,128)S(1)}, u32[]{:S(2)}, u32[]{:S(2)}) %all-to-all-start.2) | async-done | bytes 262176 | tf_op jit(solution)/shard_map/all_to_all | solution.py:168
  111.7 1.3 reduce.2
  113.0 2.8 %reshape.405 = f32[128,16,2,16]{3,2,1,0:T(2,128)S(1)} reshape(f32[128,512]{1,0:T(8,128)S(1)} %reduce.2) | data formatting | bytes 524288
  116.0 4.1 %fusion.2 = f32[16,16,2,128]{3,1,2,0:T(8,128)S(1)} fusion(f32[16,16,2,128,1]{1,2,0,3,4:T(2,128)S(1)} %bitcast_bitcast_fusion, f32[1,128,2,128]{3,1,2,0:T(8,128)S(1)} %get-tuple-element.24, f32[1,128,2,128]{3,1,2,0:T(8,128)S(1)} %get-tuple-element.17), kind=kOutput, calls=%fused_computation.5 | convolution fusion | flops 201392128 | bytes 786432 | tf_op jit(solution)/shard_map/cksn,snum->ckum/dot_general | solution.py:103
  120.8 2.0 %reduce.3 = f32[1024,32]{1,0:T(8,128)S(1)} reduce(f32[1024,1,32]{2,1,0:T(1,128)S(1)} %bitcast.195, f32[]{:T(128)} %broadcast.614), dimensions={1}, to_apply=%bitcast.180.reduce_sub_computation | reduce | bytes 262148
  122.8 0.9 reshape.406
  123.7 6.1 %all-to-all-start.3 = ((f32[128,1,256]{2,1,0:T(1,128)}), f32[128,1,256]{2,1,0:T(1,128)S(1)}, u32[]{:S(2)}, u32[]{:S(2)}) async-start(f32[128,1,256]{2,1,0:T(1,128)} %reshape.406), calls=%async_computation.3 | async-start | bytes 262144 | tf_op jit(solution)/shard_map/all_to_all | solution.py:176
  129.9 13.3 %all-to-all-done.3 = f32[128,1,256]{2,1,0:T(1,128)S(1)} async-done(((f32[128,1,256]{2,1,0:T(1,128)}), f32[128,1,256]{2,1,0:T(1,128)S(1)}, u32[]{:S(2)}, u32[]{:S(2)}) %all-to-all-start.3) | async-done | bytes 131104 | tf_op jit(solution)/shard_map/all_to_all | solution.py:176
  143.3 1.0 reduce.4
  144.2 0.9 reshape.407
  145.6 11.2 %psum.7 = f32[1024]{0:T(1024)S(1)} all-reduce(f32[1024]{0:T(1024)S(1)} %get-tuple-element.5), channel_id=1, replica_groups=mesh['ctx'=128,'tp'=4] {'tp'}, use_global_device_ids=true, to_apply=%region_1.2 | all-reduce | flops 1024 | bytes 8192 | tf_op jit(solution)/shard_map/psum | solution.py:180
  (73 shorter events, 9.4 us)
Async XLA Ops:
  2.6 9.0 %collective-permute-start = (bf16[3,32,2]{1,2,0:T(2,128)(2,1)S(1)}, bf16[3,32,2]{1,2,0:T(2,128)(2,1)S(1)}, u32[]{:S(2)}, u32[]{:S(2)}) collective-permute-start(bf16[3,32,2]{1,2,0:T(2,128)(2,1)S(1)} %pad_maximum_fusion.10), channel_id=1, source_target_pairs={{0,4},{4,8},{8,12},{12,16},{16,20},{20,24},{24,28},{28,32},{32,36}... | collective-permute-start | bytes 1160 | tf_op jit(solution)/shard_map/ppermute | solution.py:14
  13.7 32.1 %all-to-all-start = ((f32[128,1,288]{2,1,0:T(1,128)}), f32[128,1,288]{2,1,0:T(1,128)S(1)}, u32[]{:S(2)}, u32[]{:S(2)}) async-start(f32[128,1,288]{2,1,0:T(1,128)} %reshape.400), calls=%async_computation | async-start | bytes 393216 | tf_op jit(solution)/shard_map/all_to_all | solution.py:142
  54.6 21.6 %all-to-all-start.1 = ((f32[128,1,576]{2,1,0:T(1,128)}), f32[128,1,576]{2,1,0:T(1,128)S(1)}, u32[]{:S(2)}, u32[]{:S(2)}) async-start(f32[128,1,576]{2,1,0:T(1,128)} %reshape.402), calls=%async_computation.1 | async-start | bytes 655360 | tf_op jit(solution)/shard_map/all_to_all | solution.py:157
  90.7 21.0 %all-to-all-start.2 = ((f32[128,1,512]{2,1,0:T(1,128)}), f32[128,1,512]{2,1,0:T(1,128)S(1)}, u32[]{:S(2)}, u32[]{:S(2)}) async-start(f32[128,1,512]{2,1,0:T(1,128)} %reshape.404), calls=%async_computation.2 | async-start | bytes 524288 | tf_op jit(solution)/shard_map/all_to_all | solution.py:168
  120.0 9.8 %copy-start = (bf16[32,1024]{1,0:T(8,128)(2,1)S(1)}, bf16[32,1024]{1,0:T(8,128)(2,1)}, u32[]{:S(2)}) copy-start(bf16[32,1024]{1,0:T(8,128)(2,1)} %param.7) | copy-start | bytes 196612
  120.8 24.6 %copy-start.2 = (f32[32]{0:T(128)S(1)}, f32[32]{0:T(128)}, u32[]{:S(2)}) copy-start(f32[32]{0:T(128)} %param.12) | copy-start | bytes 388
  122.8 34.1 %copy-start.1 = (f32[32]{0:T(128)S(1)}, f32[32]{0:T(128)}, u32[]{:S(2)}) copy-start(f32[32]{0:T(128)} %param.13) | copy-start | bytes 388
  123.7 19.6 %all-to-all-start.3 = ((f32[128,1,256]{2,1,0:T(1,128)}), f32[128,1,256]{2,1,0:T(1,128)S(1)}, u32[]{:S(2)}, u32[]{:S(2)}) async-start(f32[128,1,256]{2,1,0:T(1,128)} %reshape.406), calls=%async_computation.3 | async-start | bytes 262144 | tf_op jit(solution)/shard_map/all_to_all | solution.py:176

commit v5 on v2

--- a/solution.py
+++ b/solution.py
@@ -37,9 +37,27 @@
     cos_table, sin_table = tables
     if imag_part is None:
         return (apply_fn(cos_table, real_part), direction * apply_fn(sin_table, real_part))
-    new_real = apply_fn(cos_table, real_part) - direction * apply_fn(sin_table, imag_part)
-    new_imag = direction * apply_fn(sin_table, real_part) + apply_fn(cos_table, imag_part)
-    return (new_real, new_imag)
+    if apply_fn is apply_cols:
+        block = jnp.concatenate(
+            [
+                jnp.concatenate([cos_table, direction * sin_table], axis=1),
+                jnp.concatenate([-direction * sin_table, cos_table], axis=1),
+            ],
+            axis=0,
+        )
+        both = apply_cols(block, jnp.concatenate([real_part, imag_part], axis=2))
+        out_len = cos_table.shape[1]
+        return (both[:, :, :out_len], both[:, :, out_len:])
+    block = jnp.concatenate(
+        [
+            jnp.concatenate([cos_table, -direction * sin_table], axis=1),
+            jnp.concatenate([direction * sin_table, cos_table], axis=1),
+        ],
+        axis=0,
+    )
+    both = apply_rows(block, jnp.concatenate([real_part, imag_part], axis=1))
+    out_len = cos_table.shape[0]
+    return (both[:, :out_len], both[:, out_len:])
 
 
 def rotate(real_part, imag_part, tables, direction):

time: 152 us -> 143 us (0.941)
  matrix products: 10.8 us -> 2.41 us
    dot_general x16 -> x4, matrix products: 8.3 us -> 1.58 us  [apply_cols(): return jnp.einsum('ckn,nm->ckm', values, table, precision=HIGHEST)]
    dot_general x8 -> x2, matrix products: 2.54 us -> 0.84 us  [apply_rows(): return jnp.einsum('kt,ctn->ckn', table, values, precision=HIGHEST)]
  transfers between devices with their start and end apart: 5 -> 5, of which waited for: 4 -> 4; matrix products, arithmetic and copies ran while one was open for 0% -> 1% of each run, Pallas kernels for 0% -> 0%
where the time goes in v5:
time: 143 us
  waiting for transfers between devices  56.7 us (40%)
  starting transfers between devices  44.8 us (31%)
  local copies, waits for them, and re-layouts  17.7 us (12%)
  blocking collectives  11.3 us (8%)
  other arithmetic  9.24 us (6%)
  matrix products  2.41 us (2%)
    all_to_all x1, starting transfers between devices, shards(): lax.all_to_all(both_in.reshape(2 * row_total, row_count, ctx_count), 'ctx...  20.6 us
    all_to_all x1, waiting for transfers between devices, shards(): lax.all_to_all(jnp.concatenate([spec_real, spec_imag], axis=0), 'ctx', sp...  14.9 us
    all_to_all x1, waiting for transfers between devices, shards(): lax.all_to_all(jnp.concatenate([back_real, back_imag], axis=0), 'ctx', sp...  14.7 us
    all_to_all x1, waiting for transfers between devices, shards(): lax.all_to_all(both_in.reshape(2 * row_total, row_count, ctx_count), 'ctx...  13.8 us
    all_to_all x1, waiting for transfers between devices, shards(): lax.all_to_all(time_vals, 'ctx', split_axis=1, concat_axis=2, tiled=True)  13.3 us
    psum x1, blocking collectives, shards(): power = lax.psum(jnp.sum(mixed * mixed, axis=0), 'tp')  11.3 us
    unnamed x30, local copies, waits for them, and re-layouts  11 us
    all_to_all x1, starting transfers between devices, shards(): lax.all_to_all(time_vals, 'ctx', split_axis=1, concat_axis=2, tiled=True)  6.51 us
  transfers between devices with their start and end apart: 5, of which 4 were waited for; matrix products, arithmetic and copies ran while one was open for 1% of the time, Pallas kernels for 0%

profile of v5, /device:TPU:1, one launch (start us, length us, event | category | flops | bytes accessed | tf_op | source)
XLA Modules:
  0.0 142.7 jit_solution(14291167176386348804)
XLA Ops:
  0.0 0.8 slice.153
  0.9 0.8 slice.154
  1.8 0.8 slice.155
  2.7 5.2 %collective-permute-start = (bf16[3,32,2]{1,2,0:T(2,128)(2,1)S(1)}, bf16[3,32,2]{1,2,0:T(2,128)(2,1)S(1)}, u32[]{:S(2)}, u32[]{:S(2)}) collective-permute-start(bf16[3,32,2]{1,2,0:T(2,128)(2,1)S(1)} %pad_maximum_fusion.9), channel_id=1, source_target_pairs={{0,4},{4,8},{8,12},{12,16},{16,20},{20,24},{24,28},{28,32},{32,36}... | collective-permute-start | bytes 1160 | tf_op jit(solution)/shard_map/ppermute | solution.py:14
  10.3 1.2 reshape.198
  11.5 20.6 %all-to-all-start = ((f32[128,1,288]{2,1,0:T(1,128)}), f32[128,1,288]{2,1,0:T(1,128)S(1)}, u32[]{:S(2)}, u32[]{:S(2)}) async-start(f32[128,1,288]{2,1,0:T(1,128)} %reshape.198), calls=%async_computation | async-start | bytes 393216 | tf_op jit(solution)/shard_map/all_to_all | solution.py:123
  32.2 13.8 %all-to-all-done = f32[128,1,288]{2,1,0:T(1,128)S(1)} async-done(((f32[128,1,288]{2,1,0:T(1,128)}), f32[128,1,288]{2,1,0:T(1,128)S(1)}, u32[]{:S(2)}, u32[]{:S(2)}) %all-to-all-start) | async-done | bytes 147488 | tf_op jit(solution)/shard_map/all_to_all | solution.py:123
  46.0 0.5 broadcast.328
  46.6 1.1 reduce
  48.5 0.5 convolution_bitcast_fusion
  49.6 0.6 copy.77
  50.1 1.8 %reshape.200 = f32[128,1,576]{2,1,0:T(1,128)} reshape(f32[128,16,36]{2,1,0:T(8,128)S(1)} %bitcast.125) | data formatting | bytes 589824
  51.9 6.4 %all-to-all-start.1 = ((f32[128,1,576]{2,1,0:T(1,128)}), f32[128,1,576]{2,1,0:T(1,128)S(1)}, u32[]{:S(2)}, u32[]{:S(2)}) async-start(f32[128,1,576]{2,1,0:T(1,128)} %reshape.200), calls=%async_computation.1 | async-start | bytes 655360 | tf_op jit(solution)/shard_map/all_to_all | solution.py:131
  58.4 14.9 %all-to-all-done.1 = f32[128,1,576]{2,1,0:T(1,128)S(1)} async-done(((f32[128,1,576]{2,1,0:T(1,128)}), f32[128,1,576]{2,1,0:T(1,128)S(1)}, u32[]{:S(2)}, u32[]{:S(2)}) %all-to-all-start.1) | async-done | bytes 294944 | tf_op jit(solution)/shard_map/all_to_all | solution.py:131
  73.3 1.4 reduce.1
  74.8 0.7 reshape.201
  75.8 0.5 copy.89
  77.7 0.5 copy.80
  78.2 1.1 reshape.202
  79.4 6.2 %all-to-all-start.2 = ((f32[128,1,512]{2,1,0:T(1,128)}), f32[128,1,512]{2,1,0:T(1,128)S(1)}, u32[]{:S(2)}, u32[]{:S(2)}) async-start(f32[128,1,512]{2,1,0:T(1,128)} %reshape.202), calls=%async_computation.2 | async-start | bytes 524288 | tf_op jit(solution)/shard_map/all_to_all | solution.py:157
  85.7 14.7 %all-to-all-done.2 = f32[128,1,512]{2,1,0:T(1,128)S(1)} async-done(((f32[128,1,512]{2,1,0:T(1,128)}), f32[128,1,512]{2,1,0:T(1,128)S(1)}, u32[]{:S(2)}, u32[]{:S(2)}) %all-to-all-start.2) | async-done | bytes 262176 | tf_op jit(solution)/shard_map/all_to_all | solution.py:157
  100.4 1.3 reduce.2
  104.2 2.0 %reduce.3 = f32[1024,32]{1,0:T(8,128)S(1)} reduce(f32[1024,1,32]{2,1,0:T(1,128)S(1)} %bitcast.128, f32[]{:T(128)} %broadcast.328), dimensions={1}, to_apply=%bitcast.116.reduce_sub_computation | reduce | bytes 262148
  106.2 0.9 reshape.204
  107.1 6.5 %all-to-all-start.3 = ((f32[128,1,256]{2,1,0:T(1,128)}), f32[128,1,256]{2,1,0:T(1,128)S(1)}, u32[]{:S(2)}, u32[]{:S(2)}) async-start(f32[128,1,256]{2,1,0:T(1,128)} %reshape.204), calls=%async_computation.3 | async-start | bytes 262144 | tf_op jit(solution)/shard_map/all_to_all | solution.py:171
  113.7 13.3 %all-to-all-done.3 = f32[128,1,256]{2,1,0:T(1,128)S(1)} async-done(((f32[128,1,256]{2,1,0:T(1,128)}), f32[128,1,256]{2,1,0:T(1,128)S(1)}, u32[]{:S(2)}, u32[]{:S(2)}) %all-to-all-start.3) | async-done | bytes 131104 | tf_op jit(solution)/shard_map/all_to_all | solution.py:171
  127.1 1.0 reduce.4
  128.0 0.9 reshape.205
  129.2 0.6 copy-done.6
  130.0 11.3 %psum.7 = f32[1024]{0:T(1024)S(1)} all-reduce(f32[1024]{0:T(1024)S(1)} %get-tuple-element.5), channel_id=1, replica_groups=mesh['ctx'=128,'tp'=4] {'tp'}, use_global_device_ids=true, to_apply=%region_1.2 | all-reduce | flops 1024 | bytes 8192 | tf_op jit(solution)/shard_map/psum | solution.py:175
  141.3 0.7 copy-done.5
  142.0 0.7 multiply_convert_fusion
  (80 shorter events, 9.0 us)
Async XLA Ops:
  0.0 7.8 %copy-start = (bf16[32,1024]{1,0:T(8,128)(2,1)S(1)}, bf16[32,1024]{1,0:T(8,128)(2,1)}, u32[]{:S(2)}) copy-start(bf16[32,1024]{1,0:T(8,128)(2,1)} %param.8) | copy-start | bytes 196612
  2.7 5.2 %copy-start.1 = (bf16[32,1024]{1,0:T(8,128)(2,1)S(1)}, bf16[32,1024]{1,0:T(8,128)(2,1)}, u32[]{:S(2)}) copy-start(bf16[32,1024]{1,0:T(8,128)(2,1)} %param.9) | copy-start | bytes 196612
  2.7 6.7 %collective-permute-start = (bf16[3,32,2]{1,2,0:T(2,128)(2,1)S(1)}, bf16[3,32,2]{1,2,0:T(2,128)(2,1)S(1)}, u32[]{:S(2)}, u32[]{:S(2)}) collective-permute-start(bf16[3,32,2]{1,2,0:T(2,128)(2,1)S(1)} %pad_maximum_fusion.9), channel_id=1, source_target_pairs={{0,4},{4,8},{8,12},{12,16},{16,20},{20,24},{24,28},{28,32},{32,36}... | collective-permute-start | bytes 1160 | tf_op jit(solution)/shard_map/ppermute | solution.py:14
  8.3 0.7 copy-start.4
  8.6 0.7 copy-start.3
  11.5 34.6 %all-to-all-start = ((f32[128,1,288]{2,1,0:T(1,128)}), f32[128,1,288]{2,1,0:T(1,128)S(1)}, u32[]{:S(2)}, u32[]{:S(2)}) async-start(f32[128,1,288]{2,1,0:T(1,128)} %reshape.198), calls=%async_computation | async-start | bytes 393216 | tf_op jit(solution)/shard_map/all_to_all | solution.py:123
  51.9 21.4 %all-to-all-start.1 = ((f32[128,1,576]{2,1,0:T(1,128)}), f32[128,1,576]{2,1,0:T(1,128)S(1)}, u32[]{:S(2)}, u32[]{:S(2)}) async-start(f32[128,1,576]{2,1,0:T(1,128)} %reshape.200), calls=%async_computation.1 | async-start | bytes 655360 | tf_op jit(solution)/shard_map/all_to_all | solution.py:131
  79.4 21.0 %all-to-all-start.2 = ((f32[128,1,512]{2,1,0:T(1,128)}), f32[128,1,512]{2,1,0:T(1,128)S(1)}, u32[]{:S(2)}, u32[]{:S(2)}) async-start(f32[128,1,512]{2,1,0:T(1,128)} %reshape.202), calls=%async_computation.2 | async-start | bytes 524288 | tf_op jit(solution)/shard_map/all_to_all | solution.py:157
  107.1 6.5 %copy-start.2 = (bf16[32,1024]{1,0:T(8,128)(2,1)S(1)}, bf16[32,1024]{1,0:T(8,128)(2,1)}, u32[]{:S(2)}) copy-start(bf16[32,1024]{1,0:T(8,128)(2,1)} %param.7) | copy-start | bytes 196612
  107.1 20.0 %all-to-all-start.3 = ((f32[128,1,256]{2,1,0:T(1,128)}), f32[128,1,256]{2,1,0:T(1,128)S(1)}, u32[]{:S(2)}, u32[]{:S(2)}) async-start(f32[128,1,256]{2,1,0:T(1,128)} %reshape.204), calls=%async_computation.3 | async-start | bytes 262144 | tf_op jit(solution)/shard_map/all_to_all | solution.py:171
  129.2 0.7 copy-start.6
  141.3 0.7 copy-start.5

commit v6 on v5

--- a/solution.py
+++ b/solution.py
@@ -103,8 +103,9 @@
     padded_len = first_len * ctx_count * ctx_count
     filter_count = long_filter.shape[0]
     pair_count = chan_count // 2
-    tails = jnp.stack([query_proj[:, -2:], key_proj[:, -2:], value_proj[:, -2:]])
-    before = shifted(tails, "ctx", 1)
+    tile = min(128, tok_count)
+    tails = jnp.stack([query_proj[:, -tile:], key_proj[:, -tile:], value_proj[:, -tile:]])
+    before = shifted(tails, "ctx", 1)[:, :, -2:]
     q_conv = causal_three(query_proj, before[0], short_taps[0])
     k_conv = causal_three(key_proj, before[1], short_taps[1])
     v_conv = causal_three(value_proj, before[2], short_taps[2])

time: 143 us -> 146 us (1.021)
  starting transfers between devices: 44.8 us -> 49.3 us
  blocking collectives: 11.3 us -> 7.94 us
    psum x1, blocking collectives: 11.3 us -> 7.94 us  [shards(): power = lax.psum(jnp.sum(mixed * mixed, axis=0), 'tp')]
    slice x6 -> x0, local copies, waits for them, and re-layouts: 2.64 us -> none  [the longest x2 0.9 us: shards(): query_proj[:, -2:]]
    all_to_all x1, starting transfers between devices: 20.6 us -> 22.9 us  [shards(): lax.all_to_all(both_in.reshape(2 * row_total, row_count, ctx_count), 'ctx...]
    another operation x0 -> x3, local copies, waits for them, and re-layouts: none -> 1.54 us  [shards(): jnp.stack([query_proj[:, -tile:], key_proj[:, -tile:], value_proj[:, -til...]
    all_to_all x1, starting transfers between devices: 6.17 us -> 7.64 us  [shards(): lax.all_to_all(jnp.concatenate([back_real, back_imag], axis=0), 'ctx', sp...]
where the time goes in v6:
time: 146 us; the launch traced here: 145 us
  waiting for transfers between devices  57.9 us (40%)
  starting transfers between devices  49.3 us (34%)
  local copies, waits for them, and re-layouts  18 us (12%)
  other arithmetic  9.24 us (6%)
  blocking collectives  7.94 us (5%)
  matrix products  2.41 us (2%)
    all_to_all x1, starting transfers between devices, shards(): lax.all_to_all(both_in.reshape(2 * row_total, row_count, ctx_count), 'ctx...  22.9 us
    all_to_all x1, waiting for transfers between devices, shards(): lax.all_to_all(jnp.concatenate([spec_real, spec_imag], axis=0), 'ctx', sp...  15.5 us
    all_to_all x1, waiting for transfers between devices, shards(): lax.all_to_all(jnp.concatenate([back_real, back_imag], axis=0), 'ctx', sp...  14.9 us
    all_to_all x1, waiting for transfers between devices, shards(): lax.all_to_all(both_in.reshape(2 * row_total, row_count, ctx_count), 'ctx...  14.3 us
    all_to_all x1, waiting for transfers between devices, shards(): lax.all_to_all(time_vals, 'ctx', split_axis=1, concat_axis=2, tiled=True)  13.2 us
    unnamed x30, local copies, waits for them, and re-layouts  12.4 us
    psum x1, blocking collectives, shards(): power = lax.psum(jnp.sum(mixed * mixed, axis=0), 'tp')  7.94 us
    all_to_all x1, starting transfers between devices, shards(): lax.all_to_all(jnp.concatenate([back_real, back_imag], axis=0), 'ctx', sp...  7.64 us
  transfers between devices with their start and end apart: 5, of which 4 were waited for; matrix products, arithmetic and copies ran while one was open for 1% of the time, Pallas kernels for 0%

profile of v6, /device:TPU:1, one launch (start us, length us, event | category | flops | bytes accessed | tf_op | source)
XLA Modules:
  0.0 145.3 jit_solution(10572025889210932358)
XLA Ops:
  0.0 0.7 slice_bitcast_fusion.4
  0.7 0.7 slice_bitcast_fusion.2
  1.6 5.0 %collective-permute-start = (bf16[3,32,128]{1,2,0:T(8,128)(2,1)S(1)}, bf16[3,32,128]{1,2,0:T(8,128)(2,1)S(1)}, u32[]{:S(2)}, u32[]{:S(2)}) collective-permute-start(bf16[3,32,128]{1,2,0:T(8,128)(2,1)S(1)} %copy.106), channel_id=1, source_target_pairs={{0,4},{4,8},{8,12},{12,16},{16,20},{20,24},{24,28},{28,32},{32,36}... | collective-permute-start | bytes 73736 | tf_op jit(solution)/shard_map/ppermute | solution.py:14
  7.9 0.8 copy-done.2
  8.7 0.7 copy-done.3
  10.3 1.2 reshape.198
  11.6 22.9 %all-to-all-start = ((f32[128,1,288]{2,1,0:T(1,128)}), f32[128,1,288]{2,1,0:T(1,128)S(1)}, u32[]{:S(2)}, u32[]{:S(2)}) async-start(f32[128,1,288]{2,1,0:T(1,128)} %reshape.198), calls=%async_computation | async-start | bytes 393216 | tf_op jit(solution)/shard_map/all_to_all | solution.py:124
  34.5 14.3 %all-to-all-done = f32[128,1,288]{2,1,0:T(1,128)S(1)} async-done(((f32[128,1,288]{2,1,0:T(1,128)}), f32[128,1,288]{2,1,0:T(1,128)S(1)}, u32[]{:S(2)}, u32[]{:S(2)}) %all-to-all-start) | async-done | bytes 147488 | tf_op jit(solution)/shard_map/all_to_all | solution.py:124
  48.8 0.5 broadcast.328
  49.3 1.1 reduce
  51.3 0.5 convolution_bitcast_fusion
  52.3 0.6 copy.115
  52.9 1.8 %reshape.200 = f32[128,1,576]{2,1,0:T(1,128)} reshape(f32[128,16,36]{2,1,0:T(8,128)S(1)} %bitcast.128) | data formatting | bytes 589824
  54.7 6.4 %all-to-all-start.1 = ((f32[128,1,576]{2,1,0:T(1,128)}), f32[128,1,576]{2,1,0:T(1,128)S(1)}, u32[]{:S(2)}, u32[]{:S(2)}) async-start(f32[128,1,576]{2,1,0:T(1,128)} %reshape.200), calls=%async_computation.1 | async-start | bytes 655360 | tf_op jit(solution)/shard_map/all_to_all | solution.py:132
  61.2 15.5 %all-to-all-done.1 = f32[128,1,576]{2,1,0:T(1,128)S(1)} async-done(((f32[128,1,576]{2,1,0:T(1,128)}), f32[128,1,576]{2,1,0:T(1,128)S(1)}, u32[]{:S(2)}, u32[]{:S(2)}) %all-to-all-start.1) | async-done | bytes 294944 | tf_op jit(solution)/shard_map/all_to_all | solution.py:132
  76.7 1.4 reduce.1
  78.1 0.7 reshape.201
  81.0 0.5 copy.118
  81.6 1.2 reshape.202
  82.7 7.6 %all-to-all-start.2 = ((f32[128,1,512]{2,1,0:T(1,128)}), f32[128,1,512]{2,1,0:T(1,128)S(1)}, u32[]{:S(2)}, u32[]{:S(2)}) async-start(f32[128,1,512]{2,1,0:T(1,128)} %reshape.202), calls=%async_computation.2 | async-start | bytes 524288 | tf_op jit(solution)/shard_map/all_to_all | solution.py:158
  90.6 14.9 %all-to-all-done.2 = f32[128,1,512]{2,1,0:T(1,128)S(1)} async-done(((f32[128,1,512]{2,1,0:T(1,128)}), f32[128,1,512]{2,1,0:T(1,128)S(1)}, u32[]{:S(2)}, u32[]{:S(2)}) %all-to-all-start.2) | async-done | bytes 262176 | tf_op jit(solution)/shard_map/all_to_all | solution.py:158
  105.5 1.3 reduce.2
  109.3 2.0 %reduce.3 = f32[1024,32]{1,0:T(8,128)S(1)} reduce(f32[1024,1,32]{2,1,0:T(1,128)S(1)} %bitcast.131, f32[]{:T(128)} %broadcast.328), dimensions={1}, to_apply=%bitcast.119.reduce_sub_computation | reduce | bytes 262148
  111.2 0.9 reshape.204
  112.2 7.4 %all-to-all-start.3 = ((f32[128,1,256]{2,1,0:T(1,128)}), f32[128,1,256]{2,1,0:T(1,128)S(1)}, u32[]{:S(2)}, u32[]{:S(2)}) async-start(f32[128,1,256]{2,1,0:T(1,128)} %reshape.204), calls=%async_computation.3 | async-start | bytes 262144 | tf_op jit(solution)/shard_map/all_to_all | solution.py:172
  119.7 13.2 %all-to-all-done.3 = f32[128,1,256]{2,1,0:T(1,128)S(1)} async-done(((f32[128,1,256]{2,1,0:T(1,128)}), f32[128,1,256]{2,1,0:T(1,128)S(1)}, u32[]{:S(2)}, u32[]{:S(2)}) %all-to-all-start.3) | async-done | bytes 131104 | tf_op jit(solution)/shard_map/all_to_all | solution.py:172
  133.0 1.0 reduce.4
  133.9 0.9 reshape.205
  135.1 0.6 copy-done.6
  136.0 7.9 %psum.7 = f32[1024]{0:T(1024)S(1)} all-reduce(f32[1024]{0:T(1024)S(1)} %get-tuple-element.5), channel_id=1, replica_groups=mesh['ctx'=128,'tp'=4] {'tp'}, use_global_device_ids=true, to_apply=%region_1.2 | all-reduce | flops 1024 | bytes 8192 | tf_op jit(solution)/shard_map/psum | solution.py:176
  143.9 0.7 copy-done.5
  144.6 0.7 multiply_convert_fusion
  (77 shorter events, 9.1 us)
Async XLA Ops:
  1.6 7.9 %collective-permute-start = (bf16[3,32,128]{1,2,0:T(8,128)(2,1)S(1)}, bf16[3,32,128]{1,2,0:T(8,128)(2,1)S(1)}, u32[]{:S(2)}, u32[]{:S(2)}) collective-permute-start(bf16[3,32,128]{1,2,0:T(8,128)(2,1)S(1)} %copy.106), channel_id=1, source_target_pairs={{0,4},{4,8},{8,12},{12,16},{16,20},{20,24},{24,28},{28,32},{32,36}... | collective-permute-start | bytes 73736 | tf_op jit(solution)/shard_map/ppermute | solution.py:14
  6.7 0.7 copy-start.4
  7.0 0.8 copy-start.1
  7.8 0.8 copy-start.2
  8.7 0.7 copy-start.3
  11.6 37.2 %all-to-all-start = ((f32[128,1,288]{2,1,0:T(1,128)}), f32[128,1,288]{2,1,0:T(1,128)S(1)}, u32[]{:S(2)}, u32[]{:S(2)}) async-start(f32[128,1,288]{2,1,0:T(1,128)} %reshape.198), calls=%async_computation | async-start | bytes 393216 | tf_op jit(solution)/shard_map/all_to_all | solution.py:124
  54.7 22.0 %all-to-all-start.1 = ((f32[128,1,576]{2,1,0:T(1,128)}), f32[128,1,576]{2,1,0:T(1,128)S(1)}, u32[]{:S(2)}, u32[]{:S(2)}) async-start(f32[128,1,576]{2,1,0:T(1,128)} %reshape.200), calls=%async_computation.1 | async-start | bytes 655360 | tf_op jit(solution)/shard_map/all_to_all | solution.py:132
  82.7 22.8 %all-to-all-start.2 = ((f32[128,1,512]{2,1,0:T(1,128)}), f32[128,1,512]{2,1,0:T(1,128)S(1)}, u32[]{:S(2)}, u32[]{:S(2)}) async-start(f32[128,1,512]{2,1,0:T(1,128)} %reshape.202), calls=%async_computation.2 | async-start | bytes 524288 | tf_op jit(solution)/shard_map/all_to_all | solution.py:158
  112.2 7.4 %copy-start = (bf16[32,1024]{1,0:T(8,128)(2,1)S(1)}, bf16[32,1024]{1,0:T(8,128)(2,1)}, u32[]{:S(2)}) copy-start(bf16[32,1024]{1,0:T(8,128)(2,1)} %param.7) | copy-start | bytes 196612
  112.2 20.8 %all-to-all-start.3 = ((f32[128,1,256]{2,1,0:T(1,128)}), f32[128,1,256]{2,1,0:T(1,128)S(1)}, u32[]{:S(2)}, u32[]{:S(2)}) async-start(f32[128,1,256]{2,1,0:T(1,128)} %reshape.204), calls=%async_computation.3 | async-start | bytes 262144 | tf_op jit(solution)/shard_map/all_to_all | solution.py:172
  135.1 0.7 copy-start.6
  143.9 0.7 copy-start.5

commit v7 on v5

--- a/solution.py
+++ b/solution.py
@@ -5,7 +5,7 @@
 from jax import lax
 from jax.sharding import PartitionSpec as P
 
-HIGHEST = lax.Precision.HIGHEST
+MATMUL_PRECISION = lax.Precision.HIGH
 
 
 def shifted(x, axis, by):
@@ -26,11 +26,11 @@
 
 
 def apply_rows(table, values):
-    return jnp.einsum("kt,ctn->ckn", table, values, precision=HIGHEST)
+    return jnp.einsum("kt,ctn->ckn", table, values, precision=MATMUL_PRECISION)
 
 
 def apply_cols(table, values):
-    return jnp.einsum("ckn,nm->ckm", values, table, precision=HIGHEST)
+    return jnp.einsum("ckn,nm->ckm", values, table, precision=MATMUL_PRECISION)
 
 
 def dft_section(apply_fn, real_part, imag_part, tables, direction):

time: 143 us -> 143 us (level)
  no operation moved by 1% of the time
where the time goes in v7:
time: 143 us; the launch traced here: 142 us
  waiting for transfers between devices  56.8 us (40%)
  starting transfers between devices  44.6 us (31%)
  local copies, waits for them, and re-layouts  17.7 us (12%)
  blocking collectives  11.2 us (8%)
  other arithmetic  9.24 us (6%)
  matrix products  1.79 us (1%)
    all_to_all x1, starting transfers between devices, shards(): lax.all_to_all(both_in.reshape(2 * row_total, row_count, ctx_count), 'ctx...  20.6 us
    all_to_all x1, waiting for transfers between devices, shards(): lax.all_to_all(jnp.concatenate([spec_real, spec_imag], axis=0), 'ctx', sp...  14.9 us
    all_to_all x1, waiting for transfers between devices, shards(): lax.all_to_all(jnp.concatenate([back_real, back_imag], axis=0), 'ctx', sp...  14.7 us
    all_to_all x1, waiting for transfers between devices, shards(): lax.all_to_all(both_in.reshape(2 * row_total, row_count, ctx_count), 'ctx...  13.8 us
    all_to_all x1, waiting for transfers between devices, shards(): lax.all_to_all(time_vals, 'ctx', split_axis=1, concat_axis=2, tiled=True)  13.4 us
    psum x1, blocking collectives, shards(): power = lax.psum(jnp.sum(mixed * mixed, axis=0), 'tp')  11.2 us
    unnamed x30, local copies, waits for them, and re-layouts  11 us
    all_to_all x1, starting transfers between devices, shards(): lax.all_to_all(jnp.concatenate([spec_real, spec_imag], axis=0), 'ctx', sp...  6.36 us
  transfers between devices with their start and end apart: 5, of which 4 were waited for; matrix products, arithmetic and copies ran while one was open for 1% of the time, Pallas kernels for 0%

profile of v7, /device:TPU:1, one launch (start us, length us, event | category | flops | bytes accessed | tf_op | source)
XLA Modules:
  0.0 141.8 jit_solution(2030881067301260327)
XLA Ops:
  0.0 0.8 slice.153
  0.9 0.8 slice.154
  1.8 0.8 slice.155
  2.7 5.2 %collective-permute-start = (bf16[3,32,2]{1,2,0:T(2,128)(2,1)S(1)}, bf16[3,32,2]{1,2,0:T(2,128)(2,1)S(1)}, u32[]{:S(2)}, u32[]{:S(2)}) collective-permute-start(bf16[3,32,2]{1,2,0:T(2,128)(2,1)S(1)} %pad_maximum_fusion.9), channel_id=1, source_target_pairs={{0,4},{4,8},{8,12},{12,16},{16,20},{20,24},{24,28},{28,32},{32,36}... | collective-permute-start | bytes 1160 | tf_op jit(solution)/shard_map/ppermute | solution.py:14
  10.3 1.2 reshape.198
  11.5 20.6 %all-to-all-start = ((f32[128,1,288]{2,1,0:T(1,128)}), f32[128,1,288]{2,1,0:T(1,128)S(1)}, u32[]{:S(2)}, u32[]{:S(2)}) async-start(f32[128,1,288]{2,1,0:T(1,128)} %reshape.198), calls=%async_computation | async-start | bytes 393216 | tf_op jit(solution)/shard_map/all_to_all | solution.py:123
  32.2 13.8 %all-to-all-done = f32[128,1,288]{2,1,0:T(1,128)S(1)} async-done(((f32[128,1,288]{2,1,0:T(1,128)}), f32[128,1,288]{2,1,0:T(1,128)S(1)}, u32[]{:S(2)}, u32[]{:S(2)}) %all-to-all-start) | async-done | bytes 147488 | tf_op jit(solution)/shard_map/all_to_all | solution.py:123
  46.0 0.5 broadcast.328
  46.6 1.1 reduce
  49.3 0.6 copy.77
  49.9 1.8 %reshape.200 = f32[128,1,576]{2,1,0:T(1,128)} reshape(f32[128,16,36]{2,1,0:T(8,128)S(1)} %bitcast.125) | data formatting | bytes 589824
  51.7 6.4 %all-to-all-start.1 = ((f32[128,1,576]{2,1,0:T(1,128)}), f32[128,1,576]{2,1,0:T(1,128)S(1)}, u32[]{:S(2)}, u32[]{:S(2)}) async-start(f32[128,1,576]{2,1,0:T(1,128)} %reshape.200), calls=%async_computation.1 | async-start | bytes 655360 | tf_op jit(solution)/shard_map/all_to_all | solution.py:131
  58.2 14.9 %all-to-all-done.1 = f32[128,1,576]{2,1,0:T(1,128)S(1)} async-done(((f32[128,1,576]{2,1,0:T(1,128)}), f32[128,1,576]{2,1,0:T(1,128)S(1)}, u32[]{:S(2)}, u32[]{:S(2)}) %all-to-all-start.1) | async-done | bytes 294944 | tf_op jit(solution)/shard_map/all_to_all | solution.py:131
  73.1 1.4 %reduce.1 = f32[128,576]{1,0:T(8,128)S(1)} reduce(f32[128,1,576]{2,1,0:T(1,128)S(1)} %all-to-all-done.1, f32[]{:T(128)} %broadcast.328), dimensions={1}, to_apply=%all_to_all.31.reduce_sub_computation | reduce | bytes 589828 | tf_op jit(solution)/shard_map/all_to_all | solution.py:131
  74.5 0.7 reshape.201
  75.6 0.5 copy.89
  76.1 0.5 copy.90
  77.2 0.5 copy.80
  77.8 1.1 reshape.202
  78.9 6.2 %all-to-all-start.2 = ((f32[128,1,512]{2,1,0:T(1,128)}), f32[128,1,512]{2,1,0:T(1,128)S(1)}, u32[]{:S(2)}, u32[]{:S(2)}) async-start(f32[128,1,512]{2,1,0:T(1,128)} %reshape.202), calls=%async_computation.2 | async-start | bytes 524288 | tf_op jit(solution)/shard_map/all_to_all | solution.py:157
  85.3 14.7 %all-to-all-done.2 = f32[128,1,512]{2,1,0:T(1,128)S(1)} async-done(((f32[128,1,512]{2,1,0:T(1,128)}), f32[128,1,512]{2,1,0:T(1,128)S(1)}, u32[]{:S(2)}, u32[]{:S(2)}) %all-to-all-start.2) | async-done | bytes 262176 | tf_op jit(solution)/shard_map/all_to_all | solution.py:157
  100.0 1.3 reduce.2
  103.6 2.0 %reduce.3 = f32[1024,32]{1,0:T(8,128)S(1)} reduce(f32[1024,1,32]{2,1,0:T(1,128)S(1)} %bitcast.128, f32[]{:T(128)} %broadcast.328), dimensions={1}, to_apply=%bitcast.116.reduce_sub_computation | reduce | bytes 262148
  105.6 0.9 reshape.204
  106.5 6.3 %all-to-all-start.3 = ((f32[128,1,256]{2,1,0:T(1,128)}), f32[128,1,256]{2,1,0:T(1,128)S(1)}, u32[]{:S(2)}, u32[]{:S(2)}) async-start(f32[128,1,256]{2,1,0:T(1,128)} %reshape.204), calls=%async_computation.3 | async-start | bytes 262144 | tf_op jit(solution)/shard_map/all_to_all | solution.py:171
  112.9 13.4 %all-to-all-done.3 = f32[128,1,256]{2,1,0:T(1,128)S(1)} async-done(((f32[128,1,256]{2,1,0:T(1,128)}), f32[128,1,256]{2,1,0:T(1,128)S(1)}, u32[]{:S(2)}, u32[]{:S(2)}) %all-to-all-start.3) | async-done | bytes 131104 | tf_op jit(solution)/shard_map/all_to_all | solution.py:171
  126.2 1.0 reduce.4
  127.2 0.9 reshape.205
  128.4 0.6 copy-done.6
  129.2 11.2 %psum.7 = f32[1024]{0:T(1024)S(1)} all-reduce(f32[1024]{0:T(1024)S(1)} %get-tuple-element.5), channel_id=1, replica_groups=mesh['ctx'=128,'tp'=4] {'tp'}, use_global_device_ids=true, to_apply=%region_1.2 | all-reduce | flops 1024 | bytes 8192 | tf_op jit(solution)/shard_map/psum | solution.py:175
  140.5 0.7 copy-done.5
  141.1 0.7 multiply_convert_fusion
  (80 shorter events, 8.4 us)
Async XLA Ops:
  0.0 7.8 %copy-start = (bf16[32,1024]{1,0:T(8,128)(2,1)S(1)}, bf16[32,1024]{1,0:T(8,128)(2,1)}, u32[]{:S(2)}) copy-start(bf16[32,1024]{1,0:T(8,128)(2,1)} %param.8) | copy-start | bytes 196612
  2.7 5.2 %copy-start.1 = (bf16[32,1024]{1,0:T(8,128)(2,1)S(1)}, bf16[32,1024]{1,0:T(8,128)(2,1)}, u32[]{:S(2)}) copy-start(bf16[32,1024]{1,0:T(8,128)(2,1)} %param.9) | copy-start | bytes 196612
  2.7 6.7 %collective-permute-start = (bf16[3,32,2]{1,2,0:T(2,128)(2,1)S(1)}, bf16[3,32,2]{1,2,0:T(2,128)(2,1)S(1)}, u32[]{:S(2)}, u32[]{:S(2)}) collective-permute-start(bf16[3,32,2]{1,2,0:T(2,128)(2,1)S(1)} %pad_maximum_fusion.9), channel_id=1, source_target_pairs={{0,4},{4,8},{8,12},{12,16},{16,20},{20,24},{24,28},{28,32},{32,36}... | collective-permute-start | bytes 1160 | tf_op jit(solution)/shard_map/ppermute | solution.py:14
  8.3 0.7 copy-start.4
  8.6 0.7 copy-start.3
  11.5 34.6 %all-to-all-start = ((f32[128,1,288]{2,1,0:T(1,128)}), f32[128,1,288]{2,1,0:T(1,128)S(1)}, u32[]{:S(2)}, u32[]{:S(2)}) async-start(f32[128,1,288]{2,1,0:T(1,128)} %reshape.198), calls=%async_computation | async-start | bytes 393216 | tf_op jit(solution)/shard_map/all_to_all | solution.py:123
  51.7 21.4 %all-to-all-start.1 = ((f32[128,1,576]{2,1,0:T(1,128)}), f32[128,1,576]{2,1,0:T(1,128)S(1)}, u32[]{:S(2)}, u32[]{:S(2)}) async-start(f32[128,1,576]{2,1,0:T(1,128)} %reshape.200), calls=%async_computation.1 | async-start | bytes 655360 | tf_op jit(solution)/shard_map/all_to_all | solution.py:131
  78.9 21.0 %all-to-all-start.2 = ((f32[128,1,512]{2,1,0:T(1,128)}), f32[128,1,512]{2,1,0:T(1,128)S(1)}, u32[]{:S(2)}, u32[]{:S(2)}) async-start(f32[128,1,512]{2,1,0:T(1,128)} %reshape.202), calls=%async_computation.2 | async-start | bytes 524288 | tf_op jit(solution)/shard_map/all_to_all | solution.py:157
  106.5 6.3 %copy-start.2 = (bf16[32,1024]{1,0:T(8,128)(2,1)S(1)}, bf16[32,1024]{1,0:T(8,128)(2,1)}, u32[]{:S(2)}) copy-start(bf16[32,1024]{1,0:T(8,128)(2,1)} %param.7) | copy-start | bytes 196612
  106.5 19.8 %all-to-all-start.3 = ((f32[128,1,256]{2,1,0:T(1,128)}), f32[128,1,256]{2,1,0:T(1,128)S(1)}, u32[]{:S(2)}, u32[]{:S(2)}) async-start(f32[128,1,256]{2,1,0:T(1,128)} %reshape.204), calls=%async_computation.3 | async-start | bytes 262144 | tf_op jit(solution)/shard_map/all_to_all | solution.py:171
  128.4 0.7 copy-start.6
  140.5 0.7 copy-start.5

commit v8 on v5

--- a/solution.py
+++ b/solution.py
@@ -120,6 +120,11 @@
         axis=0,
     )
     row_total = pair_count + filter_count
+    skip_part = skip_scale[:, None] * product
+    gated_q = norm_gain[:, None] * q_conv
+    both_in, skip_part, gated_q, q_conv = lax.optimization_barrier(
+        (both_in, skip_part, gated_q, q_conv)
+    )
     moved = lax.all_to_all(
         both_in.reshape(2 * row_total, row_count, ctx_count), "ctx", split_axis=2, concat_axis=1,
         tiled=True,
@@ -171,12 +176,11 @@
     convolved = lax.all_to_all(time_vals, "ctx", split_axis=1, concat_axis=2, tiled=True)
     convolved = convolved.reshape(2, filter_count, -1, tok_count).transpose(1, 0, 2, 3)
     convolved = convolved.reshape(chan_count, tok_count)
-    mixed = q_conv * (convolved + skip_scale[:, None] * product)
+    gate = convolved + skip_part
+    mixed = q_conv * gate
     power = lax.psum(jnp.sum(mixed * mixed, axis=0), "tp")
     total_channels = chan_count * lax.axis_size("tp")
-    return (norm_gain[:, None] * mixed * lax.rsqrt(power / total_channels + 1e-05)).astype(
-        jnp.bfloat16
-    )
+    return (gated_q * gate * lax.rsqrt(power / total_channels + 1e-05)).astype(jnp.bfloat16)
 
 
 def solution(mesh):

time: 143 us -> 144 us (level)
  blocking collectives: 11.3 us -> 30.5 us
  waiting for transfers between devices: 56.7 us -> 43.4 us
  starting transfers between devices: 44.8 us -> 37.7 us
    all_to_all x0 -> x1, blocking collectives: none -> 19.3 us  [shards(): lax.all_to_all(time_vals, 'ctx', split_axis=1, concat_axis=2, tiled=True)]
    all_to_all x1 -> x0, waiting for transfers between devices: 13.3 us -> none  [shards(): lax.all_to_all(time_vals, 'ctx', split_axis=1, concat_axis=2, tiled=True)]
    all_to_all x1 -> x0, starting transfers between devices: 6.51 us -> none  [shards(): lax.all_to_all(time_vals, 'ctx', split_axis=1, concat_axis=2, tiled=True)]
    unnamed x30 -> x31, local copies, waits for them, and re-layouts: 11 us -> 12.4 us
  transfers between devices with their start and end apart: 5 -> 4, of which waited for: 4 -> 3; matrix products, arithmetic and copies ran while one was open for 1% -> 1% of each run, Pallas kernels for 0% -> 0%
where the time goes in v8:
time: 144 us
  waiting for transfers between devices  43.4 us (30%)
  starting transfers between devices  37.7 us (26%)
  blocking collectives  30.5 us (21%)
  local copies, waits for them, and re-layouts  19.1 us (13%)
  other arithmetic  9.9 us (7%)
  matrix products  2.41 us (2%)
    all_to_all x1, starting transfers between devices, shards(): lax.all_to_all(both_in.reshape(2 * row_total, row_count, ctx_count), 'ctx...  20.1 us
    all_to_all x1, blocking collectives, shards(): lax.all_to_all(time_vals, 'ctx', split_axis=1, concat_axis=2, tiled=True)  19.3 us
    all_to_all x1, waiting for transfers between devices, shards(): lax.all_to_all(jnp.concatenate([spec_real, spec_imag], axis=0), 'ctx', sp...  15 us
    all_to_all x1, waiting for transfers between devices, shards(): lax.all_to_all(jnp.concatenate([back_real, back_imag], axis=0), 'ctx', sp...  14.6 us
    all_to_all x1, waiting for transfers between devices, shards(): lax.all_to_all(both_in.reshape(2 * row_total, row_count, ctx_count), 'ctx...  13.8 us
    unnamed x31, local copies, waits for them, and re-layouts  12.4 us
    psum x1, blocking collectives, shards(): power = lax.psum(jnp.sum(mixed * mixed, axis=0), 'tp')  11.2 us
    all_to_all x1, starting transfers between devices, shards(): lax.all_to_all(jnp.concatenate([spec_real, spec_imag], axis=0), 'ctx', sp...  6.35 us
  transfers between devices with their start and end apart: 4, of which 3 were waited for; matrix products, arithmetic and copies ran while one was open for 1% of the time, Pallas kernels for 0%

profile of v8, /device:TPU:1, one launch (start us, length us, event | category | flops | bytes accessed | tf_op | source)
XLA Modules:
  0.0 143.6 jit_solution(7220007540687005794)
XLA Ops:
  0.0 0.8 slice.155
  0.9 0.8 slice.154
  1.8 0.8 slice.153
  2.7 5.2 %collective-permute-start = (bf16[3,32,2]{1,2,0:T(2,128)(2,1)S(1)}, bf16[3,32,2]{1,2,0:T(2,128)(2,1)S(1)}, u32[]{:S(2)}, u32[]{:S(2)}) collective-permute-start(bf16[3,32,2]{1,2,0:T(2,128)(2,1)S(1)} %pad_maximum_fusion.9), channel_id=1, source_target_pairs={{0,4},{4,8},{8,12},{12,16},{16,20},{20,24},{24,28},{28,32},{32,36}... | collective-permute-start | bytes 1160 | tf_op jit(solution)/shard_map/ppermute | solution.py:14
  7.9 0.8 copy-done.4
  10.2 0.7 copy-done.7
  11.2 0.6 copy-done.5
  11.9 0.6 copy-done.8
  12.6 0.9 broadcast_multiply_fusion
  13.7 1.2 reshape.195
  15.0 20.1 %all-to-all-start = ((f32[128,1,288]{2,1,0:T(1,128)}), f32[128,1,288]{2,1,0:T(1,128)S(1)}, u32[]{:S(2)}, u32[]{:S(2)}) async-start(f32[128,1,288]{2,1,0:T(1,128)} %reshape.195), calls=%async_computation | async-start | bytes 393216 | tf_op jit(solution)/shard_map/all_to_all | solution.py:128
  35.1 13.8 %all-to-all-done = f32[128,1,288]{2,1,0:T(1,128)S(1)} async-done(((f32[128,1,288]{2,1,0:T(1,128)}), f32[128,1,288]{2,1,0:T(1,128)S(1)}, u32[]{:S(2)}, u32[]{:S(2)}) %all-to-all-start) | async-done | bytes 147488 | tf_op jit(solution)/shard_map/all_to_all | solution.py:128
  49.5 1.1 reduce
  51.4 0.5 convolution_bitcast_fusion
  52.5 0.6 copy.68
  53.1 1.8 %reshape.197 = f32[128,1,576]{2,1,0:T(1,128)} reshape(f32[128,16,36]{2,1,0:T(8,128)S(1)} %bitcast.115) | data formatting | bytes 589824
  54.9 6.4 %all-to-all-start.1 = ((f32[128,1,576]{2,1,0:T(1,128)}), f32[128,1,576]{2,1,0:T(1,128)S(1)}, u32[]{:S(2)}, u32[]{:S(2)}) async-start(f32[128,1,576]{2,1,0:T(1,128)} %reshape.197), calls=%async_computation.1 | async-start | bytes 655360 | tf_op jit(solution)/shard_map/all_to_all | solution.py:136
  61.4 15.0 %all-to-all-done.1 = f32[128,1,576]{2,1,0:T(1,128)S(1)} async-done(((f32[128,1,576]{2,1,0:T(1,128)}), f32[128,1,576]{2,1,0:T(1,128)S(1)}, u32[]{:S(2)}, u32[]{:S(2)}) %all-to-all-start.1) | async-done | bytes 294944 | tf_op jit(solution)/shard_map/all_to_all | solution.py:136
  76.3 1.4 reduce.1
  77.7 0.7 reshape.198
  80.7 0.5 copy.71
  81.2 1.2 reshape.199
  82.4 6.2 %all-to-all-start.2 = ((f32[128,1,512]{2,1,0:T(1,128)}), f32[128,1,512]{2,1,0:T(1,128)S(1)}, u32[]{:S(2)}, u32[]{:S(2)}) async-start(f32[128,1,512]{2,1,0:T(1,128)} %reshape.199), calls=%async_computation.2 | async-start | bytes 524288 | tf_op jit(solution)/shard_map/all_to_all | solution.py:162
  88.7 14.6 %all-to-all-done.2 = f32[128,1,512]{2,1,0:T(1,128)S(1)} async-done(((f32[128,1,512]{2,1,0:T(1,128)}), f32[128,1,512]{2,1,0:T(1,128)S(1)}, u32[]{:S(2)}, u32[]{:S(2)}) %all-to-all-start.2) | async-done | bytes 262176 | tf_op jit(solution)/shard_map/all_to_all | solution.py:162
  103.3 1.3 reduce.2
  107.1 2.0 %reduce.3 = f32[1024,32]{1,0:T(8,128)S(1)} reduce(f32[1024,1,32]{2,1,0:T(1,128)S(1)} %bitcast.118, f32[]{:T(128)} %broadcast.327), dimensions={1}, to_apply=%bitcast.108.reduce_sub_computation | reduce | bytes 262148
  109.3 19.3 %all_to_all.40 = f32[128,1,256]{2,1,0:T(1,128)S(1)} all-to-all(f32[128,1,256]{2,1,0:T(1,128)S(1)} %reshape.201), channel_id=1, replica_groups=mesh['ctx'=128,'tp'=4] {'ctx'}, dimensions={0} | all-to-all | bytes 262144 | tf_op jit(solution)/shard_map/all_to_all | solution.py:176
  128.6 1.0 reduce.4
  129.6 0.9 reshape.202
  130.8 0.9 copy-done.1
  131.7 11.2 %psum.7 = f32[1024]{0:T(1024)S(1)} all-reduce(f32[1024]{0:T(1024)S(1)} %multiply_reduce_fusion), channel_id=1, replica_groups=mesh['ctx'=128,'tp'=4] {'tp'}, use_global_device_ids=true, to_apply=%region_1.2 | all-reduce | flops 1024 | bytes 8192 | tf_op jit(solution)/shard_map/psum | solution.py:181
  142.9 0.7 multiply_convert_fusion
  (83 shorter events, 9.8 us)
Async XLA Ops:
  0.0 7.9 %copy-start.2 = (bf16[32,1024]{1,0:T(8,128)(2,1)S(1)}, bf16[32,1024]{1,0:T(8,128)(2,1)}, u32[]{:S(2)}) copy-start(bf16[32,1024]{1,0:T(8,128)(2,1)} %param.9) | copy-start | bytes 196612
  2.7 5.2 %copy-start.3 = (bf16[32,1024]{1,0:T(8,128)(2,1)S(1)}, bf16[32,1024]{1,0:T(8,128)(2,1)}, u32[]{:S(2)}) copy-start(bf16[32,1024]{1,0:T(8,128)(2,1)} %param.8) | copy-start | bytes 196612
  2.7 7.3 %collective-permute-start = (bf16[3,32,2]{1,2,0:T(2,128)(2,1)S(1)}, bf16[3,32,2]{1,2,0:T(2,128)(2,1)S(1)}, u32[]{:S(2)}, u32[]{:S(2)}) collective-permute-start(bf16[3,32,2]{1,2,0:T(2,128)(2,1)S(1)} %pad_maximum_fusion.9), channel_id=1, source_target_pairs={{0,4},{4,8},{8,12},{12,16},{16,20},{20,24},{24,28},{28,32},{32,36}... | collective-permute-start | bytes 1160 | tf_op jit(solution)/shard_map/ppermute | solution.py:14
  7.9 0.8 copy-start.4
  9.2 0.7 copy-start.6
  10.2 0.7 copy-start.7
  11.1 0.7 copy-start.5
  11.9 0.7 copy-start.8
  15.0 34.0 %all-to-all-start = ((f32[128,1,288]{2,1,0:T(1,128)}), f32[128,1,288]{2,1,0:T(1,128)S(1)}, u32[]{:S(2)}, u32[]{:S(2)}) async-start(f32[128,1,288]{2,1,0:T(1,128)} %reshape.195), calls=%async_computation | async-start | bytes 393216 | tf_op jit(solution)/shard_map/all_to_all | solution.py:128
  54.9 21.5 %all-to-all-start.1 = ((f32[128,1,576]{2,1,0:T(1,128)}), f32[128,1,576]{2,1,0:T(1,128)S(1)}, u32[]{:S(2)}, u32[]{:S(2)}) async-start(f32[128,1,576]{2,1,0:T(1,128)} %reshape.197), calls=%async_computation.1 | async-start | bytes 655360 | tf_op jit(solution)/shard_map/all_to_all | solution.py:136
  82.4 20.9 %all-to-all-start.2 = ((f32[128,1,512]{2,1,0:T(1,128)}), f32[128,1,512]{2,1,0:T(1,128)S(1)}, u32[]{:S(2)}, u32[]{:S(2)}) async-start(f32[128,1,512]{2,1,0:T(1,128)} %reshape.199), calls=%async_computation.2 | async-start | bytes 524288 | tf_op jit(solution)/shard_map/all_to_all | solution.py:162
  130.7 0.9 copy-start.1
  131.7 11.3 %copy-start = (f32[32,1024]{1,0:T(8,128)S(1)}, f32[32,1024]{1,0:T(8,128)}, u32[]{:S(2)}) copy-start(f32[32,1024]{1,0:T(8,128)} %get-tuple-element.9) | copy-start | bytes 393220

commit v9 on v5

--- a/solution.py
+++ b/solution.py
@@ -164,13 +164,24 @@
     back_real, back_imag = rotate(
         back_real, back_imag, grid_product(first_len, ctx_count, first_len * ctx_count), 1.0
     )
-    last_tables = grid_product(row_count, first_len, first_len)
-    time_real, time_imag = dft_section(apply_rows, back_real, back_imag, last_tables, 1.0)
-    time_vals = jnp.concatenate([time_real, time_imag], axis=0)
-    time_vals = time_vals.reshape(chan_count, row_count * ctx_count, 1) * (1.0 / padded_len)
-    convolved = lax.all_to_all(time_vals, "ctx", split_axis=1, concat_axis=2, tiled=True)
-    convolved = convolved.reshape(2, filter_count, -1, tok_count).transpose(1, 0, 2, 3)
-    convolved = convolved.reshape(chan_count, tok_count)
+    last_cos, last_sin = grid_product(row_count, first_len, first_len)
+    last_block = jnp.concatenate(
+        [
+            jnp.concatenate([last_cos, -last_sin], axis=1),
+            jnp.concatenate([last_sin, last_cos], axis=1),
+        ],
+        axis=0,
+    )
+    time_vals = jnp.einsum(
+        "ut,ctq->uqc", last_block, jnp.concatenate([back_real, back_imag], axis=1),
+        precision=HIGHEST,
+    )
+    time_vals = time_vals.reshape(2, row_count, ctx_count, pair_count).transpose(1, 2, 0, 3)
+    time_vals = time_vals.reshape(ctx_count, tok_count // ctx_count, chan_count)
+    time_vals = time_vals * (1.0 / padded_len)
+    convolved = lax.all_to_all(time_vals, "ctx", split_axis=0, concat_axis=0, tiled=True)
+    convolved = convolved.transpose(2, 1, 0).reshape(2, filter_count, -1, tok_count)
+    convolved = convolved.transpose(1, 0, 2, 3).reshape(chan_count, tok_count)
     mixed = q_conv * (convolved + skip_scale[:, None] * product)
     power = lax.psum(jnp.sum(mixed * mixed, axis=0), "tp")
     total_channels = chan_count * lax.axis_size("tp")

time: 143 us -> 141 us (0.986)
  other arithmetic: 9.24 us -> 7.28 us
    unnamed x1 -> x0, other arithmetic: 1.95 us -> none
where the time goes in v9:
time: 141 us
  waiting for transfers between devices  56.8 us (40%)
  starting transfers between devices  44.6 us (32%)
  local copies, waits for them, and re-layouts  17.8 us (13%)
  blocking collectives  11.3 us (8%)
  other arithmetic  7.28 us (5%)
  matrix products  2.41 us (2%)
    all_to_all x1, starting transfers between devices, shards(): lax.all_to_all(both_in.reshape(2 * row_total, row_count, ctx_count), 'ctx...  20.6 us
    all_to_all x1, waiting for transfers between devices, shards(): lax.all_to_all(jnp.concatenate([spec_real, spec_imag], axis=0), 'ctx', sp...  14.9 us
    all_to_all x1, waiting for transfers between devices, shards(): lax.all_to_all(jnp.concatenate([back_real, back_imag], axis=0), 'ctx', sp...  14.6 us
    all_to_all x1, waiting for transfers between devices, shards(): lax.all_to_all(both_in.reshape(2 * row_total, row_count, ctx_count), 'ctx...  13.8 us
    all_to_all x1, waiting for transfers between devices, shards(): lax.all_to_all(time_vals, 'ctx', split_axis=0, concat_axis=0, tiled=True)  13.4 us
    psum x1, blocking collectives, shards(): power = lax.psum(jnp.sum(mixed * mixed, axis=0), 'tp')  11.3 us
    unnamed x30, local copies, waits for them, and re-layouts  10.3 us
    all_to_all x1, starting transfers between devices, shards(): lax.all_to_all(jnp.concatenate([spec_real, spec_imag], axis=0), 'ctx', sp...  6.35 us
  transfers between devices with their start and end apart: 5, of which 4 were waited for; matrix products, arithmetic and copies ran while one was open for 1% of the time, Pallas kernels for 0%

profile of v9, /device:TPU:1, one launch (start us, length us, event | category | flops | bytes accessed | tf_op | source)
XLA Modules:
  0.0 140.6 jit_solution(14453759055977268145)
XLA Ops:
  0.0 0.8 slice.147
  0.9 0.8 slice.148
  1.8 0.8 slice.149
  2.7 5.2 %collective-permute-start = (bf16[3,32,2]{1,2,0:T(2,128)(2,1)S(1)}, bf16[3,32,2]{1,2,0:T(2,128)(2,1)S(1)}, u32[]{:S(2)}, u32[]{:S(2)}) collective-permute-start(bf16[3,32,2]{1,2,0:T(2,128)(2,1)S(1)} %pad_maximum_fusion.9), channel_id=1, source_target_pairs={{0,4},{4,8},{8,12},{12,16},{16,20},{20,24},{24,28},{28,32},{32,36}... | collective-permute-start | bytes 1160 | tf_op jit(solution)/shard_map/ppermute | solution.py:14
  10.3 1.2 reshape.188
  11.5 20.6 %all-to-all-start = ((f32[128,1,288]{2,1,0:T(1,128)}), f32[128,1,288]{2,1,0:T(1,128)S(1)}, u32[]{:S(2)}, u32[]{:S(2)}) async-start(f32[128,1,288]{2,1,0:T(1,128)} %reshape.188), calls=%async_computation | async-start | bytes 393216 | tf_op jit(solution)/shard_map/all_to_all | solution.py:123
  32.2 13.8 %all-to-all-done = f32[128,1,288]{2,1,0:T(1,128)S(1)} async-done(((f32[128,1,288]{2,1,0:T(1,128)}), f32[128,1,288]{2,1,0:T(1,128)S(1)}, u32[]{:S(2)}, u32[]{:S(2)}) %all-to-all-start) | async-done | bytes 147488 | tf_op jit(solution)/shard_map/all_to_all | solution.py:123
  46.0 0.5 broadcast.326
  46.6 1.1 reduce
  48.5 0.5 convolution_bitcast_fusion
  49.6 0.6 copy.77
  50.1 1.8 %reshape.190 = f32[128,1,576]{2,1,0:T(1,128)} reshape(f32[128,16,36]{2,1,0:T(8,128)S(1)} %bitcast.120) | data formatting | bytes 589824
  51.9 6.3 %all-to-all-start.1 = ((f32[128,1,576]{2,1,0:T(1,128)}), f32[128,1,576]{2,1,0:T(1,128)S(1)}, u32[]{:S(2)}, u32[]{:S(2)}) async-start(f32[128,1,576]{2,1,0:T(1,128)} %reshape.190), calls=%async_computation.1 | async-start | bytes 655360 | tf_op jit(solution)/shard_map/all_to_all | solution.py:131
  58.4 14.9 %all-to-all-done.1 = f32[128,1,576]{2,1,0:T(1,128)S(1)} async-done(((f32[128,1,576]{2,1,0:T(1,128)}), f32[128,1,576]{2,1,0:T(1,128)S(1)}, u32[]{:S(2)}, u32[]{:S(2)}) %all-to-all-start.1) | async-done | bytes 294944 | tf_op jit(solution)/shard_map/all_to_all | solution.py:131
  73.4 1.4 %reduce.1 = f32[128,576]{1,0:T(8,128)S(1)} reduce(f32[128,1,576]{2,1,0:T(1,128)S(1)} %all-to-all-done.1, f32[]{:T(128)} %broadcast.326), dimensions={1}, to_apply=%all_to_all.23.reduce_sub_computation | reduce | bytes 589828 | tf_op jit(solution)/shard_map/all_to_all | solution.py:131
  74.8 0.7 reshape.191
  75.9 0.5 copy.88
  76.4 0.5 copy.89
  77.7 0.5 copy.80
  78.3 1.1 reshape.192
  79.4 6.2 %all-to-all-start.2 = ((f32[128,1,512]{2,1,0:T(1,128)}), f32[128,1,512]{2,1,0:T(1,128)S(1)}, u32[]{:S(2)}, u32[]{:S(2)}) async-start(f32[128,1,512]{2,1,0:T(1,128)} %reshape.192), calls=%async_computation.2 | async-start | bytes 524288 | tf_op jit(solution)/shard_map/all_to_all | solution.py:157
  85.8 14.6 %all-to-all-done.2 = f32[128,1,512]{2,1,0:T(1,128)S(1)} async-done(((f32[128,1,512]{2,1,0:T(1,128)}), f32[128,1,512]{2,1,0:T(1,128)S(1)}, u32[]{:S(2)}, u32[]{:S(2)}) %all-to-all-start.2) | async-done | bytes 262176 | tf_op jit(solution)/shard_map/all_to_all | solution.py:157
  100.4 1.3 reduce.2
  104.4 0.6 mul.594
  105.0 0.9 reshape.194
  105.9 6.3 %all-to-all-start.3 = ((f32[128,1,256]{2,1,0:T(1,128)}), f32[128,1,256]{2,1,0:T(1,128)S(1)}, u32[]{:S(2)}, u32[]{:S(2)}) async-start(f32[128,1,256]{2,1,0:T(1,128)} %reshape.194), calls=%async_computation.3 | async-start | bytes 262144 | tf_op jit(solution)/shard_map/all_to_all | solution.py:182
  112.3 13.4 %all-to-all-done.3 = f32[128,1,256]{2,1,0:T(1,128)S(1)} async-done(((f32[128,1,256]{2,1,0:T(1,128)}), f32[128,1,256]{2,1,0:T(1,128)S(1)}, u32[]{:S(2)}, u32[]{:S(2)}) %all-to-all-start.3) | async-done | bytes 131104 | tf_op jit(solution)/shard_map/all_to_all | solution.py:182
  125.7 1.0 reduce.3
  127.1 0.6 copy-done.6
  127.9 11.3 %psum.7 = f32[1024]{0:T(1024)S(1)} all-reduce(f32[1024]{0:T(1024)S(1)} %get-tuple-element.5), channel_id=1, replica_groups=mesh['ctx'=128,'tp'=4] {'tp'}, use_global_device_ids=true, to_apply=%region_1.2 | all-reduce | flops 1024 | bytes 8192 | tf_op jit(solution)/shard_map/psum | solution.py:186
  139.2 0.7 copy-done.5
  139.8 0.7 multiply_convert_fusion
  (78 shorter events, 8.9 us)
Async XLA Ops:
  0.0 7.8 %copy-start = (bf16[32,1024]{1,0:T(8,128)(2,1)S(1)}, bf16[32,1024]{1,0:T(8,128)(2,1)}, u32[]{:S(2)}) copy-start(bf16[32,1024]{1,0:T(8,128)(2,1)} %param.8) | copy-start | bytes 196612
  2.7 5.2 %copy-start.1 = (bf16[32,1024]{1,0:T(8,128)(2,1)S(1)}, bf16[32,1024]{1,0:T(8,128)(2,1)}, u32[]{:S(2)}) copy-start(bf16[32,1024]{1,0:T(8,128)(2,1)} %param.9) | copy-start | bytes 196612
  2.7 6.7 %collective-permute-start = (bf16[3,32,2]{1,2,0:T(2,128)(2,1)S(1)}, bf16[3,32,2]{1,2,0:T(2,128)(2,1)S(1)}, u32[]{:S(2)}, u32[]{:S(2)}) collective-permute-start(bf16[3,32,2]{1,2,0:T(2,128)(2,1)S(1)} %pad_maximum_fusion.9), channel_id=1, source_target_pairs={{0,4},{4,8},{8,12},{12,16},{16,20},{20,24},{24,28},{28,32},{32,36}... | collective-permute-start | bytes 1160 | tf_op jit(solution)/shard_map/ppermute | solution.py:14
  8.3 0.7 copy-start.4
  8.6 0.7 copy-start.3
  11.5 34.6 %all-to-all-start = ((f32[128,1,288]{2,1,0:T(1,128)}), f32[128,1,288]{2,1,0:T(1,128)S(1)}, u32[]{:S(2)}, u32[]{:S(2)}) async-start(f32[128,1,288]{2,1,0:T(1,128)} %reshape.188), calls=%async_computation | async-start | bytes 393216 | tf_op jit(solution)/shard_map/all_to_all | solution.py:123
  51.9 21.4 %all-to-all-start.1 = ((f32[128,1,576]{2,1,0:T(1,128)}), f32[128,1,576]{2,1,0:T(1,128)S(1)}, u32[]{:S(2)}, u32[]{:S(2)}) async-start(f32[128,1,576]{2,1,0:T(1,128)} %reshape.190), calls=%async_computation.1 | async-start | bytes 655360 | tf_op jit(solution)/shard_map/all_to_all | solution.py:131
  79.4 20.9 %all-to-all-start.2 = ((f32[128,1,512]{2,1,0:T(1,128)}), f32[128,1,512]{2,1,0:T(1,128)S(1)}, u32[]{:S(2)}, u32[]{:S(2)}) async-start(f32[128,1,512]{2,1,0:T(1,128)} %reshape.192), calls=%async_computation.2 | async-start | bytes 524288 | tf_op jit(solution)/shard_map/all_to_all | solution.py:157
  105.9 6.3 %copy-start.2 = (bf16[32,1024]{1,0:T(8,128)(2,1)S(1)}, bf16[32,1024]{1,0:T(8,128)(2,1)}, u32[]{:S(2)}) copy-start(bf16[32,1024]{1,0:T(8,128)(2,1)} %param.7) | copy-start | bytes 196612
  105.9 19.8 %all-to-all-start.3 = ((f32[128,1,256]{2,1,0:T(1,128)}), f32[128,1,256]{2,1,0:T(1,128)S(1)}, u32[]{:S(2)}, u32[]{:S(2)}) async-start(f32[128,1,256]{2,1,0:T(1,128)} %reshape.194), calls=%async_computation.3 | async-start | bytes 262144 | tf_op jit(solution)/shard_map/all_to_all | solution.py:182
  127.1 0.7 copy-start.6
  139.2 0.7 copy-start.5

commit v10 on v9

--- a/solution.py
+++ b/solution.py
@@ -171,14 +171,13 @@
             jnp.concatenate([last_sin, last_cos], axis=1),
         ],
         axis=0,
-    )
+    ) * (1.0 / padded_len)
     time_vals = jnp.einsum(
         "ut,ctq->uqc", last_block, jnp.concatenate([back_real, back_imag], axis=1),
         precision=HIGHEST,
     )
     time_vals = time_vals.reshape(2, row_count, ctx_count, pair_count).transpose(1, 2, 0, 3)
     time_vals = time_vals.reshape(ctx_count, tok_count // ctx_count, chan_count)
-    time_vals = time_vals * (1.0 / padded_len)
     convolved = lax.all_to_all(time_vals, "ctx", split_axis=0, concat_axis=0, tiled=True)
     convolved = convolved.transpose(2, 1, 0).reshape(2, filter_count, -1, tok_count)
     convolved = convolved.transpose(1, 0, 2, 3).reshape(chan_count, tok_count)

time: 141 us -> 141 us (level)
  no operation moved by 1% of the time
where the time goes in v10:
time: 141 us
  waiting for transfers between devices  56.7 us (40%)
  starting transfers between devices  44.6 us (32%)
  local copies, waits for them, and re-layouts  17.8 us (13%)
  blocking collectives  11.3 us (8%)
  other arithmetic  7.28 us (5%)
  matrix products  2.41 us (2%)
    all_to_all x1, starting transfers between devices, shards(): lax.all_to_all(both_in.reshape(2 * row_total, row_count, ctx_count), 'ctx...  20.6 us
    all_to_all x1, waiting for transfers between devices, shards(): lax.all_to_all(jnp.concatenate([spec_real, spec_imag], axis=0), 'ctx', sp...  14.9 us
    all_to_all x1, waiting for transfers between devices, shards(): lax.all_to_all(jnp.concatenate([back_real, back_imag], axis=0), 'ctx', sp...  14.6 us
    all_to_all x1, waiting for transfers between devices, shards(): lax.all_to_all(both_in.reshape(2 * row_total, row_count, ctx_count), 'ctx...  13.8 us
    all_to_all x1, waiting for transfers between devices, shards(): lax.all_to_all(time_vals, 'ctx', split_axis=0, concat_axis=0, tiled=True)  13.3 us
    psum x1, blocking collectives, shards(): power = lax.psum(jnp.sum(mixed * mixed, axis=0), 'tp')  11.3 us
    unnamed x30, local copies, waits for them, and re-layouts  10.3 us
    all_to_all x1, starting transfers between devices, shards(): lax.all_to_all(jnp.concatenate([spec_real, spec_imag], axis=0), 'ctx', sp...  6.35 us
  transfers between devices with their start and end apart: 5, of which 4 were waited for; matrix products, arithmetic and copies ran while one was open for 1% of the time, Pallas kernels for 0%

profile of v10, /device:TPU:1, one launch (start us, length us, event | category | flops | bytes accessed | tf_op | source)
XLA Modules:
  0.0 140.6 jit_solution(13806503790709621271)
XLA Ops:
  0.0 0.8 slice.147
  0.9 0.8 slice.148
  1.8 0.8 slice.149
  2.7 5.2 %collective-permute-start = (bf16[3,32,2]{1,2,0:T(2,128)(2,1)S(1)}, bf16[3,32,2]{1,2,0:T(2,128)(2,1)S(1)}, u32[]{:S(2)}, u32[]{:S(2)}) collective-permute-start(bf16[3,32,2]{1,2,0:T(2,128)(2,1)S(1)} %pad_maximum_fusion.9), channel_id=1, source_target_pairs={{0,4},{4,8},{8,12},{12,16},{16,20},{20,24},{24,28},{28,32},{32,36}... | collective-permute-start | bytes 1160 | tf_op jit(solution)/shard_map/ppermute | solution.py:14
  10.3 1.2 reshape.190
  11.5 20.6 %all-to-all-start = ((f32[128,1,288]{2,1,0:T(1,128)}), f32[128,1,288]{2,1,0:T(1,128)S(1)}, u32[]{:S(2)}, u32[]{:S(2)}) async-start(f32[128,1,288]{2,1,0:T(1,128)} %reshape.190), calls=%async_computation | async-start | bytes 393216 | tf_op jit(solution)/shard_map/all_to_all | solution.py:123
  32.2 13.8 %all-to-all-done = f32[128,1,288]{2,1,0:T(1,128)S(1)} async-done(((f32[128,1,288]{2,1,0:T(1,128)}), f32[128,1,288]{2,1,0:T(1,128)S(1)}, u32[]{:S(2)}, u32[]{:S(2)}) %all-to-all-start) | async-done | bytes 147488 | tf_op jit(solution)/shard_map/all_to_all | solution.py:123
  46.0 0.5 broadcast.318
  46.6 1.1 reduce
  48.5 0.5 convolution_bitcast_fusion
  49.6 0.6 copy.77
  50.1 1.8 %reshape.192 = f32[128,1,576]{2,1,0:T(1,128)} reshape(f32[128,16,36]{2,1,0:T(8,128)S(1)} %bitcast.120) | data formatting | bytes 589824
  51.9 6.3 %all-to-all-start.1 = ((f32[128,1,576]{2,1,0:T(1,128)}), f32[128,1,576]{2,1,0:T(1,128)S(1)}, u32[]{:S(2)}, u32[]{:S(2)}) async-start(f32[128,1,576]{2,1,0:T(1,128)} %reshape.192), calls=%async_computation.1 | async-start | bytes 655360 | tf_op jit(solution)/shard_map/all_to_all | solution.py:131
  58.4 14.9 %all-to-all-done.1 = f32[128,1,576]{2,1,0:T(1,128)S(1)} async-done(((f32[128,1,576]{2,1,0:T(1,128)}), f32[128,1,576]{2,1,0:T(1,128)S(1)}, u32[]{:S(2)}, u32[]{:S(2)}) %all-to-all-start.1) | async-done | bytes 294944 | tf_op jit(solution)/shard_map/all_to_all | solution.py:131
  73.4 1.4 %reduce.1 = f32[128,576]{1,0:T(8,128)S(1)} reduce(f32[128,1,576]{2,1,0:T(1,128)S(1)} %all-to-all-done.1, f32[]{:T(128)} %broadcast.318), dimensions={1}, to_apply=%all_to_all.23.reduce_sub_computation | reduce | bytes 589828 | tf_op jit(solution)/shard_map/all_to_all | solution.py:131
  74.8 0.7 reshape.193
  75.9 0.5 copy.88
  76.4 0.5 copy.89
  77.7 0.5 copy.80
  78.3 1.1 reshape.194
  79.4 6.2 %all-to-all-start.2 = ((f32[128,1,512]{2,1,0:T(1,128)}), f32[128,1,512]{2,1,0:T(1,128)S(1)}, u32[]{:S(2)}, u32[]{:S(2)}) async-start(f32[128,1,512]{2,1,0:T(1,128)} %reshape.194), calls=%async_computation.2 | async-start | bytes 524288 | tf_op jit(solution)/shard_map/all_to_all | solution.py:157
  85.8 14.6 %all-to-all-done.2 = f32[128,1,512]{2,1,0:T(1,128)S(1)} async-done(((f32[128,1,512]{2,1,0:T(1,128)}), f32[128,1,512]{2,1,0:T(1,128)S(1)}, u32[]{:S(2)}, u32[]{:S(2)}) %all-to-all-start.2) | async-done | bytes 262176 | tf_op jit(solution)/shard_map/all_to_all | solution.py:157
  100.4 1.3 reduce.2
  104.4 0.6 reshape.180
  105.0 0.9 reshape.196
  105.9 6.3 %all-to-all-start.3 = ((f32[128,1,256]{2,1,0:T(1,128)}), f32[128,1,256]{2,1,0:T(1,128)S(1)}, u32[]{:S(2)}, u32[]{:S(2)}) async-start(f32[128,1,256]{2,1,0:T(1,128)} %reshape.196), calls=%async_computation.3 | async-start | bytes 262144 | tf_op jit(solution)/shard_map/all_to_all | solution.py:181
  112.3 13.3 %all-to-all-done.3 = f32[128,1,256]{2,1,0:T(1,128)S(1)} async-done(((f32[128,1,256]{2,1,0:T(1,128)}), f32[128,1,256]{2,1,0:T(1,128)S(1)}, u32[]{:S(2)}, u32[]{:S(2)}) %all-to-all-start.3) | async-done | bytes 131104 | tf_op jit(solution)/shard_map/all_to_all | solution.py:181
  125.7 1.0 reduce.3
  127.1 0.6 copy-done.6
  127.9 11.3 %psum.7 = f32[1024]{0:T(1024)S(1)} all-reduce(f32[1024]{0:T(1024)S(1)} %get-tuple-element.5), channel_id=1, replica_groups=mesh['ctx'=128,'tp'=4] {'tp'}, use_global_device_ids=true, to_apply=%region_1.2 | all-reduce | flops 1024 | bytes 8192 | tf_op jit(solution)/shard_map/psum | solution.py:185
  139.2 0.7 copy-done.5
  139.8 0.7 multiply_convert_fusion
  (78 shorter events, 8.9 us)
Async XLA Ops:
  0.0 7.8 %copy-start = (bf16[32,1024]{1,0:T(8,128)(2,1)S(1)}, bf16[32,1024]{1,0:T(8,128)(2,1)}, u32[]{:S(2)}) copy-start(bf16[32,1024]{1,0:T(8,128)(2,1)} %param.8) | copy-start | bytes 196612
  2.7 5.2 %copy-start.1 = (bf16[32,1024]{1,0:T(8,128)(2,1)S(1)}, bf16[32,1024]{1,0:T(8,128)(2,1)}, u32[]{:S(2)}) copy-start(bf16[32,1024]{1,0:T(8,128)(2,1)} %param.9) | copy-start | bytes 196612
  2.7 6.7 %collective-permute-start = (bf16[3,32,2]{1,2,0:T(2,128)(2,1)S(1)}, bf16[3,32,2]{1,2,0:T(2,128)(2,1)S(1)}, u32[]{:S(2)}, u32[]{:S(2)}) collective-permute-start(bf16[3,32,2]{1,2,0:T(2,128)(2,1)S(1)} %pad_maximum_fusion.9), channel_id=1, source_target_pairs={{0,4},{4,8},{8,12},{12,16},{16,20},{20,24},{24,28},{28,32},{32,36}... | collective-permute-start | bytes 1160 | tf_op jit(solution)/shard_map/ppermute | solution.py:14
  8.3 0.7 copy-start.4
  8.6 0.7 copy-start.3
  11.5 34.6 %all-to-all-start = ((f32[128,1,288]{2,1,0:T(1,128)}), f32[128,1,288]{2,1,0:T(1,128)S(1)}, u32[]{:S(2)}, u32[]{:S(2)}) async-start(f32[128,1,288]{2,1,0:T(1,128)} %reshape.190), calls=%async_computation | async-start | bytes 393216 | tf_op jit(solution)/shard_map/all_to_all | solution.py:123
  51.9 21.4 %all-to-all-start.1 = ((f32[128,1,576]{2,1,0:T(1,128)}), f32[128,1,576]{2,1,0:T(1,128)S(1)}, u32[]{:S(2)}, u32[]{:S(2)}) async-start(f32[128,1,576]{2,1,0:T(1,128)} %reshape.192), calls=%async_computation.1 | async-start | bytes 655360 | tf_op jit(solution)/shard_map/all_to_all | solution.py:131
  79.4 20.9 %all-to-all-start.2 = ((f32[128,1,512]{2,1,0:T(1,128)}), f32[128,1,512]{2,1,0:T(1,128)S(1)}, u32[]{:S(2)}, u32[]{:S(2)}) async-start(f32[128,1,512]{2,1,0:T(1,128)} %reshape.194), calls=%async_computation.2 | async-start | bytes 524288 | tf_op jit(solution)/shard_map/all_to_all | solution.py:157
  105.9 6.3 %copy-start.2 = (bf16[32,1024]{1,0:T(8,128)(2,1)S(1)}, bf16[32,1024]{1,0:T(8,128)(2,1)}, u32[]{:S(2)}) copy-start(bf16[32,1024]{1,0:T(8,128)(2,1)} %param.7) | copy-start | bytes 196612
  105.9 19.8 %all-to-all-start.3 = ((f32[128,1,256]{2,1,0:T(1,128)}), f32[128,1,256]{2,1,0:T(1,128)S(1)}, u32[]{:S(2)}, u32[]{:S(2)}) async-start(f32[128,1,256]{2,1,0:T(1,128)} %reshape.196), calls=%async_computation.3 | async-start | bytes 262144 | tf_op jit(solution)/shard_map/all_to_all | solution.py:181
  127.1 0.7 copy-start.6
  139.2 0.7 copy-start.5

commit v11 on v10

--- a/solution.py
+++ b/solution.py
@@ -120,6 +120,7 @@
         axis=0,
     )
     row_total = pair_count + filter_count
+    both_in, scales = lax.optimization_barrier((both_in, jnp.stack([skip_scale, norm_gain])))
     moved = lax.all_to_all(
         both_in.reshape(2 * row_total, row_count, ctx_count), "ctx", split_axis=2, concat_axis=1,
         tiled=True,
@@ -181,10 +182,10 @@
     convolved = lax.all_to_all(time_vals, "ctx", split_axis=0, concat_axis=0, tiled=True)
     convolved = convolved.transpose(2, 1, 0).reshape(2, filter_count, -1, tok_count)
     convolved = convolved.transpose(1, 0, 2, 3).reshape(chan_count, tok_count)
-    mixed = q_conv * (convolved + skip_scale[:, None] * product)
+    mixed = q_conv * (convolved + scales[0][:, None] * product)
     power = lax.psum(jnp.sum(mixed * mixed, axis=0), "tp")
     total_channels = chan_count * lax.axis_size("tp")
-    return (norm_gain[:, None] * mixed * lax.rsqrt(power / total_channels + 1e-05)).astype(
+    return (scales[1][:, None] * mixed * lax.rsqrt(power / total_channels + 1e-05)).astype(
         jnp.bfloat16
     )
 

time: 141 us -> 141 us (level)
    unnamed x30 -> x27, local copies, waits for them, and re-layouts: 10.3 us -> 10 us
where the time goes in v11:
time: 141 us; the launch traced here: 140 us
  waiting for transfers between devices  56.8 us (40%)
  starting transfers between devices  44.2 us (31%)
  local copies, waits for them, and re-layouts  17.5 us (12%)
  blocking collectives  11.2 us (8%)
  other arithmetic  7.27 us (5%)
  matrix products  2.41 us (2%)
    all_to_all x1, starting transfers between devices, shards(): lax.all_to_all(both_in.reshape(2 * row_total, row_count, ctx_count), 'ctx...  20.2 us
    all_to_all x1, waiting for transfers between devices, shards(): lax.all_to_all(jnp.concatenate([spec_real, spec_imag], axis=0), 'ctx', sp...  14.9 us
    all_to_all x1, waiting for transfers between devices, shards(): lax.all_to_all(jnp.concatenate([back_real, back_imag], axis=0), 'ctx', sp...  14.7 us
    all_to_all x1, waiting for transfers between devices, shards(): lax.all_to_all(both_in.reshape(2 * row_total, row_count, ctx_count), 'ctx...  13.8 us
    all_to_all x1, waiting for transfers between devices, shards(): lax.all_to_all(time_vals, 'ctx', split_axis=0, concat_axis=0, tiled=True)  13.4 us
    psum x1, blocking collectives, shards(): power = lax.psum(jnp.sum(mixed * mixed, axis=0), 'tp')  11.2 us
    unnamed x27, local copies, waits for them, and re-layouts  10 us
    all_to_all x1, starting transfers between devices, shards(): lax.all_to_all(jnp.concatenate([spec_real, spec_imag], axis=0), 'ctx', sp...  6.35 us
  transfers between devices with their start and end apart: 5, of which 4 were waited for; matrix products, arithmetic and copies ran while one was open for 1% of the time, Pallas kernels for 0%

profile of v11, /device:TPU:1, one launch (start us, length us, event | category | flops | bytes accessed | tf_op | source)
XLA Modules:
  0.0 139.9 jit_solution(7819933527452411367)
XLA Ops:
  0.0 0.8 slice.153
  0.9 0.8 slice.154
  1.8 0.8 slice.155
  2.7 5.2 %collective-permute-start = (bf16[3,32,2]{1,2,0:T(2,128)(2,1)S(1)}, bf16[3,32,2]{1,2,0:T(2,128)(2,1)S(1)}, u32[]{:S(2)}, u32[]{:S(2)}) collective-permute-start(bf16[3,32,2]{1,2,0:T(2,128)(2,1)S(1)} %pad_maximum_fusion.9), channel_id=1, source_target_pairs={{0,4},{4,8},{8,12},{12,16},{16,20},{20,24},{24,28},{28,32},{32,36}... | collective-permute-start | bytes 1160 | tf_op jit(solution)/shard_map/ppermute | solution.py:14
  9.1 0.6 copy-done.5
  10.3 0.7 copy-done.3
  11.4 1.2 reshape.187
  12.6 20.2 %all-to-all-start = ((f32[128,1,288]{2,1,0:T(1,128)}), f32[128,1,288]{2,1,0:T(1,128)S(1)}, u32[]{:S(2)}, u32[]{:S(2)}) async-start(f32[128,1,288]{2,1,0:T(1,128)} %reshape.187), calls=%async_computation | async-start | bytes 393216 | tf_op jit(solution)/shard_map/all_to_all | solution.py:124
  32.9 13.8 %all-to-all-done = f32[128,1,288]{2,1,0:T(1,128)S(1)} async-done(((f32[128,1,288]{2,1,0:T(1,128)}), f32[128,1,288]{2,1,0:T(1,128)S(1)}, u32[]{:S(2)}, u32[]{:S(2)}) %all-to-all-start) | async-done | bytes 147488 | tf_op jit(solution)/shard_map/all_to_all | solution.py:124
  46.7 0.5 broadcast.315
  47.2 1.1 reduce
  49.2 0.5 convolution_bitcast_fusion
  50.2 0.6 copy.68
  50.8 1.8 %reshape.189 = f32[128,1,576]{2,1,0:T(1,128)} reshape(f32[128,16,36]{2,1,0:T(8,128)S(1)} %bitcast.115) | data formatting | bytes 589824
  52.6 6.4 %all-to-all-start.1 = ((f32[128,1,576]{2,1,0:T(1,128)}), f32[128,1,576]{2,1,0:T(1,128)S(1)}, u32[]{:S(2)}, u32[]{:S(2)}) async-start(f32[128,1,576]{2,1,0:T(1,128)} %reshape.189), calls=%async_computation.1 | async-start | bytes 655360 | tf_op jit(solution)/shard_map/all_to_all | solution.py:132
  59.1 14.9 %all-to-all-done.1 = f32[128,1,576]{2,1,0:T(1,128)S(1)} async-done(((f32[128,1,576]{2,1,0:T(1,128)}), f32[128,1,576]{2,1,0:T(1,128)S(1)}, u32[]{:S(2)}, u32[]{:S(2)}) %all-to-all-start.1) | async-done | bytes 294944 | tf_op jit(solution)/shard_map/all_to_all | solution.py:132
  74.0 1.4 %reduce.1 = f32[128,576]{1,0:T(8,128)S(1)} reduce(f32[128,1,576]{2,1,0:T(1,128)S(1)} %all-to-all-done.1, f32[]{:T(128)} %broadcast.315), dimensions={1}, to_apply=%all_to_all.23.reduce_sub_computation | reduce | bytes 589828 | tf_op jit(solution)/shard_map/all_to_all | solution.py:132
  75.5 0.7 reshape.190
  76.5 0.5 copy.77
  77.0 0.5 copy.78
  78.4 0.5 copy.71
  78.9 1.2 reshape.191
  80.1 6.2 %all-to-all-start.2 = ((f32[128,1,512]{2,1,0:T(1,128)}), f32[128,1,512]{2,1,0:T(1,128)S(1)}, u32[]{:S(2)}, u32[]{:S(2)}) async-start(f32[128,1,512]{2,1,0:T(1,128)} %reshape.191), calls=%async_computation.2 | async-start | bytes 524288 | tf_op jit(solution)/shard_map/all_to_all | solution.py:158
  86.4 14.7 %all-to-all-done.2 = f32[128,1,512]{2,1,0:T(1,128)S(1)} async-done(((f32[128,1,512]{2,1,0:T(1,128)}), f32[128,1,512]{2,1,0:T(1,128)S(1)}, u32[]{:S(2)}, u32[]{:S(2)}) %all-to-all-start.2) | async-done | bytes 262176 | tf_op jit(solution)/shard_map/all_to_all | solution.py:158
  101.1 1.3 reduce.2
  105.1 0.6 reshape.177
  105.7 0.9 reshape.193
  106.6 6.3 %all-to-all-start.3 = ((f32[128,1,256]{2,1,0:T(1,128)}), f32[128,1,256]{2,1,0:T(1,128)S(1)}, u32[]{:S(2)}, u32[]{:S(2)}) async-start(f32[128,1,256]{2,1,0:T(1,128)} %reshape.193), calls=%async_computation.3 | async-start | bytes 262144 | tf_op jit(solution)/shard_map/all_to_all | solution.py:182
  113.0 13.4 %all-to-all-done.3 = f32[128,1,256]{2,1,0:T(1,128)S(1)} async-done(((f32[128,1,256]{2,1,0:T(1,128)}), f32[128,1,256]{2,1,0:T(1,128)S(1)}, u32[]{:S(2)}, u32[]{:S(2)}) %all-to-all-start.3) | async-done | bytes 131104 | tf_op jit(solution)/shard_map/all_to_all | solution.py:182
  126.4 1.0 reduce.3
  128.0 11.2 %psum.7 = f32[1024]{0:T(1024)S(1)} all-reduce(f32[1024]{0:T(1024)S(1)} %get-tuple-element.9), channel_id=1, replica_groups=mesh['ctx'=128,'tp'=4] {'tp'}, use_global_device_ids=true, to_apply=%region_1.2 | all-reduce | flops 1024 | bytes 8192 | tf_op jit(solution)/shard_map/psum | solution.py:186
  139.2 0.7 multiply_convert_fusion
  (79 shorter events, 8.7 us)
Async XLA Ops:
  0.0 7.8 %copy-start = (bf16[32,1024]{1,0:T(8,128)(2,1)S(1)}, bf16[32,1024]{1,0:T(8,128)(2,1)}, u32[]{:S(2)}) copy-start(bf16[32,1024]{1,0:T(8,128)(2,1)} %param.8) | copy-start | bytes 196612
  2.7 5.2 %copy-start.1 = (bf16[32,1024]{1,0:T(8,128)(2,1)S(1)}, bf16[32,1024]{1,0:T(8,128)(2,1)}, u32[]{:S(2)}) copy-start(bf16[32,1024]{1,0:T(8,128)(2,1)} %param.9) | copy-start | bytes 196612
  2.7 7.1 %collective-permute-start = (bf16[3,32,2]{1,2,0:T(2,128)(2,1)S(1)}, bf16[3,32,2]{1,2,0:T(2,128)(2,1)S(1)}, u32[]{:S(2)}, u32[]{:S(2)}) collective-permute-start(bf16[3,32,2]{1,2,0:T(2,128)(2,1)S(1)} %pad_maximum_fusion.9), channel_id=1, source_target_pairs={{0,4},{4,8},{8,12},{12,16},{16,20},{20,24},{24,28},{28,32},{32,36}... | collective-permute-start | bytes 1160 | tf_op jit(solution)/shard_map/ppermute | solution.py:14
  8.3 0.7 copy-start.4
  9.0 0.7 copy-start.5
  9.1 0.7 copy-start.6
  10.2 0.7 copy-start.3
  12.6 34.2 %all-to-all-start = ((f32[128,1,288]{2,1,0:T(1,128)}), f32[128,1,288]{2,1,0:T(1,128)S(1)}, u32[]{:S(2)}, u32[]{:S(2)}) async-start(f32[128,1,288]{2,1,0:T(1,128)} %reshape.187), calls=%async_computation | async-start | bytes 393216 | tf_op jit(solution)/shard_map/all_to_all | solution.py:124
  52.6 21.4 %all-to-all-start.1 = ((f32[128,1,576]{2,1,0:T(1,128)}), f32[128,1,576]{2,1,0:T(1,128)S(1)}, u32[]{:S(2)}, u32[]{:S(2)}) async-start(f32[128,1,576]{2,1,0:T(1,128)} %reshape.189), calls=%async_computation.1 | async-start | bytes 655360 | tf_op jit(solution)/shard_map/all_to_all | solution.py:132
  80.1 21.0 %all-to-all-start.2 = ((f32[128,1,512]{2,1,0:T(1,128)}), f32[128,1,512]{2,1,0:T(1,128)S(1)}, u32[]{:S(2)}, u32[]{:S(2)}) async-start(f32[128,1,512]{2,1,0:T(1,128)} %reshape.191), calls=%async_computation.2 | async-start | bytes 524288 | tf_op jit(solution)/shard_map/all_to_all | solution.py:158
  106.6 6.3 %copy-start.2 = (bf16[32,1024]{1,0:T(8,128)(2,1)S(1)}, bf16[32,1024]{1,0:T(8,128)(2,1)}, u32[]{:S(2)}) copy-start(bf16[32,1024]{1,0:T(8,128)(2,1)} %param.7) | copy-start | bytes 196612
  106.6 19.8 %all-to-all-start.3 = ((f32[128,1,256]{2,1,0:T(1,128)}), f32[128,1,256]{2,1,0:T(1,128)S(1)}, u32[]{:S(2)}, u32[]{:S(2)}) async-start(f32[128,1,256]{2,1,0:T(1,128)} %reshape.193), calls=%async_computation.3 | async-start | bytes 262144 | tf_op jit(solution)/shard_map/all_to_all | solution.py:182

commit v12 on v10

--- a/solution.py
+++ b/solution.py
@@ -75,13 +75,23 @@
     real_part, imag_part = rotate(
         real_part, imag_part, grid_product(first_len, ctx_count, first_len * ctx_count), -1.0
     )
-    real_part, imag_part = dft_section(
-        apply_cols, real_part, imag_part, grid_product(ctx_count, ctx_count, ctx_count), -1.0
-    )
-    freq_first = lax.broadcasted_iota(jnp.int32, (first_len, ctx_count), 0)
-    freq_second = lax.broadcasted_iota(jnp.int32, (first_len, ctx_count), 1)
+    cos_table, sin_table = grid_product(ctx_count, ctx_count, ctx_count)
+    block = jnp.concatenate(
+        [
+            jnp.concatenate([cos_table, -sin_table], axis=1),
+            jnp.concatenate([sin_table, cos_table], axis=1),
+        ],
+        axis=0,
+    )
+    both = jnp.einsum(
+        "ckn,nm->mck", jnp.concatenate([real_part, imag_part], axis=2), block,
+        precision=HIGHEST,
+    )
+    freq_second = lax.broadcasted_iota(jnp.int32, (ctx_count, 1, first_len), 0)
+    freq_first = lax.broadcasted_iota(jnp.int32, (ctx_count, 1, first_len), 2)
     twist = trig_pair((freq_first + first_len * freq_second) * ctx_index, padded_len)
-    return rotate(real_part, imag_part, twist, -1.0)
+    real_part, imag_part = rotate(both[:ctx_count], both[ctx_count:], twist, -1.0)
+    return jnp.stack([real_part, imag_part], axis=1).reshape(ctx_count, -1)
 
 
 def causal_three(values, before, taps):
@@ -125,13 +135,9 @@
         tiled=True,
     )
     moved = moved.reshape(2 * row_total, row_count, ctx_count)
-    spec_real, spec_imag = forward_local(
-        moved[:row_total], moved[row_total:], first_len, ctx_count, ctx_index
-    )
-    spec = lax.all_to_all(
-        jnp.concatenate([spec_real, spec_imag], axis=0), "ctx", split_axis=2, concat_axis=2,
-        tiled=True,
-    )
+    spec = forward_local(moved[:row_total], moved[row_total:], first_len, ctx_count, ctx_index)
+    spec = lax.all_to_all(spec, "ctx", split_axis=0, concat_axis=0, tiled=True)
+    spec = spec.reshape(ctx_count, 2 * row_total, first_len).transpose(1, 2, 0)
     square_tables = grid_product(ctx_count, ctx_count, ctx_count)
     spec_real, spec_imag = dft_section(
         apply_cols, spec[:row_total], spec[row_total:], square_tables, -1.0

time: 141 us -> 137 us (0.972)
  local copies, waits for them, and re-layouts: 17.8 us -> 14.6 us
    unnamed x30 -> x26, local copies, waits for them, and re-layouts: 10.3 us -> 6.85 us
    all_to_all x1 -> x0, other arithmetic: 1.42 us -> none  [shards(): lax.all_to_all(jnp.concatenate([spec_real, spec_imag], axis=0), 'ctx', sp...]
where the time goes in v12:
time: 137 us; the launch traced here: 136 us
  waiting for transfers between devices  56.7 us (41%)
  starting transfers between devices  44.5 us (32%)
  local copies, waits for them, and re-layouts  14.6 us (11%)
  blocking collectives  11.2 us (8%)
  other arithmetic  6.17 us (5%)
  matrix products  2.59 us (2%)
    all_to_all x1, starting transfers between devices, shards(): lax.all_to_all(both_in.reshape(2 * row_total, row_count, ctx_count), 'ctx...  20.6 us
    all_to_all x1, waiting for transfers between devices, shards(): spec = lax.all_to_all(spec, 'ctx', split_axis=0, concat_axis=0, tiled=True)  14.8 us
    all_to_all x1, waiting for transfers between devices, shards(): lax.all_to_all(jnp.concatenate([back_real, back_imag], axis=0), 'ctx', sp...  14.7 us
    all_to_all x1, waiting for transfers between devices, shards(): lax.all_to_all(both_in.reshape(2 * row_total, row_count, ctx_count), 'ctx...  13.9 us
    all_to_all x1, waiting for transfers between devices, shards(): lax.all_to_all(time_vals, 'ctx', split_axis=0, concat_axis=0, tiled=True)  13.3 us
    psum x1, blocking collectives, shards(): power = lax.psum(jnp.sum(mixed * mixed, axis=0), 'tp')  11.2 us
    unnamed x26, local copies, waits for them, and re-layouts  6.85 us
    all_to_all x1, starting transfers between devices, shards(): lax.all_to_all(jnp.concatenate([back_real, back_imag], axis=0), 'ctx', sp...  6.34 us
  transfers between devices with their start and end apart: 5, of which 4 were waited for; matrix products, arithmetic and copies ran while one was open for 1% of the time, Pallas kernels for 0%

profile of v12, /device:TPU:1, one launch (start us, length us, event | category | flops | bytes accessed | tf_op | source)
XLA Modules:
  0.0 136.3 jit_solution(8069271230559174410)
XLA Ops:
  0.0 0.8 slice.147
  0.9 0.8 slice.148
  1.8 0.8 slice.149
  2.7 5.2 %collective-permute-start = (bf16[3,32,2]{1,2,0:T(2,128)(2,1)S(1)}, bf16[3,32,2]{1,2,0:T(2,128)(2,1)S(1)}, u32[]{:S(2)}, u32[]{:S(2)}) collective-permute-start(bf16[3,32,2]{1,2,0:T(2,128)(2,1)S(1)} %pad_maximum_fusion.13), channel_id=1, source_target_pairs={{0,4},{4,8},{8,12},{12,16},{16,20},{20,24},{24,28},{28,32},{32,36}... | collective-permute-start | bytes 1160 | tf_op jit(solution)/shard_map/ppermute | solution.py:14
  10.3 1.2 reshape.187
  11.5 20.6 %all-to-all-start = ((f32[128,1,288]{2,1,0:T(1,128)}), f32[128,1,288]{2,1,0:T(1,128)S(1)}, u32[]{:S(2)}, u32[]{:S(2)}) async-start(f32[128,1,288]{2,1,0:T(1,128)} %reshape.187), calls=%async_computation | async-start | bytes 393216 | tf_op jit(solution)/shard_map/all_to_all | solution.py:133
  32.2 13.9 %all-to-all-done = f32[128,1,288]{2,1,0:T(1,128)S(1)} async-done(((f32[128,1,288]{2,1,0:T(1,128)}), f32[128,1,288]{2,1,0:T(1,128)S(1)}, u32[]{:S(2)}, u32[]{:S(2)}) %all-to-all-start) | async-done | bytes 147488 | tf_op jit(solution)/shard_map/all_to_all | solution.py:133
  46.0 0.5 broadcast.297
  46.6 1.1 reduce
  48.5 0.5 convolution_bitcast_fusion
  49.1 0.6 fusion
  49.9 0.9 copy.85
  50.8 6.2 %all-to-all-start.1 = ((f32[128,1,576]{2,1,0:T(1,128)}), f32[128,1,576]{2,1,0:T(1,128)S(1)}, u32[]{:S(2)}, u32[]{:S(2)}) async-start(f32[128,1,576]{2,1,0:T(1,128)} %copy.85), calls=%async_computation.1 | async-start | bytes 655360 | tf_op jit(solution)/shard_map/all_to_all | solution.py:139
  57.4 14.8 %all-to-all-done.1 = f32[128,1,576]{2,1,0:T(1,128)S(1)} async-done(((f32[128,1,576]{2,1,0:T(1,128)}), f32[128,1,576]{2,1,0:T(1,128)S(1)}, u32[]{:S(2)}, u32[]{:S(2)}) %all-to-all-start.1) | async-done | bytes 294944 | tf_op jit(solution)/shard_map/all_to_all | solution.py:139
  72.4 0.4 fusion.2
  73.3 0.5 copy.87
  73.8 1.2 reshape.189
  75.0 6.3 %all-to-all-start.2 = ((f32[128,1,512]{2,1,0:T(1,128)}), f32[128,1,512]{2,1,0:T(1,128)S(1)}, u32[]{:S(2)}, u32[]{:S(2)}) async-start(f32[128,1,512]{2,1,0:T(1,128)} %reshape.189), calls=%async_computation.2 | async-start | bytes 524288 | tf_op jit(solution)/shard_map/all_to_all | solution.py:163
  81.5 14.7 %all-to-all-done.2 = f32[128,1,512]{2,1,0:T(1,128)S(1)} async-done(((f32[128,1,512]{2,1,0:T(1,128)}), f32[128,1,512]{2,1,0:T(1,128)S(1)}, u32[]{:S(2)}, u32[]{:S(2)}) %all-to-all-start.2) | async-done | bytes 262176 | tf_op jit(solution)/shard_map/all_to_all | solution.py:163
  96.2 1.3 reduce.1
  98.1 0.4 copy.95
  98.5 0.4 copy.96
  99.7 0.5 copy.90
  100.2 0.6 reshape.176
  100.8 0.9 reshape.191
  101.7 6.3 %all-to-all-start.3 = ((f32[128,1,256]{2,1,0:T(1,128)}), f32[128,1,256]{2,1,0:T(1,128)S(1)}, u32[]{:S(2)}, u32[]{:S(2)}) async-start(f32[128,1,256]{2,1,0:T(1,128)} %reshape.191), calls=%async_computation.3 | async-start | bytes 262144 | tf_op jit(solution)/shard_map/all_to_all | solution.py:187
  108.1 13.3 %all-to-all-done.3 = f32[128,1,256]{2,1,0:T(1,128)S(1)} async-done(((f32[128,1,256]{2,1,0:T(1,128)}), f32[128,1,256]{2,1,0:T(1,128)S(1)}, u32[]{:S(2)}, u32[]{:S(2)}) %all-to-all-start.3) | async-done | bytes 131104 | tf_op jit(solution)/shard_map/all_to_all | solution.py:187
  121.4 1.0 reduce.2
  122.8 0.6 copy-done.6
  123.7 11.2 %psum.7 = f32[1024]{0:T(1024)S(1)} all-reduce(f32[1024]{0:T(1024)S(1)} %get-tuple-element.5), channel_id=1, replica_groups=mesh['ctx'=128,'tp'=4] {'tp'}, use_global_device_ids=true, to_apply=%region_1.2 | all-reduce | flops 1024 | bytes 8192 | tf_op jit(solution)/shard_map/psum | solution.py:191
  134.9 0.7 copy-done.5
  135.6 0.7 multiply_convert_fusion
  (77 shorter events, 7.0 us)
Async XLA Ops:
  0.0 7.8 %copy-start = (bf16[32,1024]{1,0:T(8,128)(2,1)S(1)}, bf16[32,1024]{1,0:T(8,128)(2,1)}, u32[]{:S(2)}) copy-start(bf16[32,1024]{1,0:T(8,128)(2,1)} %param.8) | copy-start | bytes 196612
  2.7 5.2 %copy-start.1 = (bf16[32,1024]{1,0:T(8,128)(2,1)S(1)}, bf16[32,1024]{1,0:T(8,128)(2,1)}, u32[]{:S(2)}) copy-start(bf16[32,1024]{1,0:T(8,128)(2,1)} %param.9) | copy-start | bytes 196612
  2.7 6.8 %collective-permute-start = (bf16[3,32,2]{1,2,0:T(2,128)(2,1)S(1)}, bf16[3,32,2]{1,2,0:T(2,128)(2,1)S(1)}, u32[]{:S(2)}, u32[]{:S(2)}) collective-permute-start(bf16[3,32,2]{1,2,0:T(2,128)(2,1)S(1)} %pad_maximum_fusion.13), channel_id=1, source_target_pairs={{0,4},{4,8},{8,12},{12,16},{16,20},{20,24},{24,28},{28,32},{32,36}... | collective-permute-start | bytes 1160 | tf_op jit(solution)/shard_map/ppermute | solution.py:14
  8.3 0.7 copy-start.4
  8.6 0.7 copy-start.3
  11.5 34.6 %all-to-all-start = ((f32[128,1,288]{2,1,0:T(1,128)}), f32[128,1,288]{2,1,0:T(1,128)S(1)}, u32[]{:S(2)}, u32[]{:S(2)}) async-start(f32[128,1,288]{2,1,0:T(1,128)} %reshape.187), calls=%async_computation | async-start | bytes 393216 | tf_op jit(solution)/shard_map/all_to_all | solution.py:133
  50.8 21.4 %all-to-all-start.1 = ((f32[128,1,576]{2,1,0:T(1,128)}), f32[128,1,576]{2,1,0:T(1,128)S(1)}, u32[]{:S(2)}, u32[]{:S(2)}) async-start(f32[128,1,576]{2,1,0:T(1,128)} %copy.85), calls=%async_computation.1 | async-start | bytes 655360 | tf_op jit(solution)/shard_map/all_to_all | solution.py:139
  75.0 21.2 %all-to-all-start.2 = ((f32[128,1,512]{2,1,0:T(1,128)}), f32[128,1,512]{2,1,0:T(1,128)S(1)}, u32[]{:S(2)}, u32[]{:S(2)}) async-start(f32[128,1,512]{2,1,0:T(1,128)} %reshape.189), calls=%async_computation.2 | async-start | bytes 524288 | tf_op jit(solution)/shard_map/all_to_all | solution.py:163
  101.7 6.3 %copy-start.2 = (bf16[32,1024]{1,0:T(8,128)(2,1)S(1)}, bf16[32,1024]{1,0:T(8,128)(2,1)}, u32[]{:S(2)}) copy-start(bf16[32,1024]{1,0:T(8,128)(2,1)} %param.7) | copy-start | bytes 196612
  101.7 19.7 %all-to-all-start.3 = ((f32[128,1,256]{2,1,0:T(1,128)}), f32[128,1,256]{2,1,0:T(1,128)S(1)}, u32[]{:S(2)}, u32[]{:S(2)}) async-start(f32[128,1,256]{2,1,0:T(1,128)} %reshape.191), calls=%async_computation.3 | async-start | bytes 262144 | tf_op jit(solution)/shard_map/all_to_all | solution.py:187
  122.8 0.7 copy-start.6
  134.9 0.7 copy-start.5

commit v13 on v12

--- a/solution.py
+++ b/solution.py
@@ -155,15 +155,25 @@
     prod_imag = (group_real * filt_imag[:, None] + group_imag * filt_real[:, None]).reshape(
         data_real.shape
     )
-    back_real, back_imag = dft_section(apply_cols, prod_real, prod_imag, square_tables, 1.0)
-    freq_first = lax.broadcasted_iota(jnp.int32, (first_len, ctx_count), 0)
-    time_third = lax.broadcasted_iota(jnp.int32, (first_len, ctx_count), 1)
+    inv_cos, inv_sin = square_tables
+    inv_block = jnp.concatenate(
+        [
+            jnp.concatenate([inv_cos, inv_sin], axis=1),
+            jnp.concatenate([-inv_sin, inv_cos], axis=1),
+        ],
+        axis=0,
+    )
+    back = jnp.einsum(
+        "ckn,nm->mck", jnp.concatenate([prod_real, prod_imag], axis=2), inv_block,
+        precision=HIGHEST,
+    )
+    time_third = lax.broadcasted_iota(jnp.int32, (ctx_count, 1, first_len), 0)
+    freq_first = lax.broadcasted_iota(jnp.int32, (ctx_count, 1, first_len), 2)
     twist = trig_pair((freq_first + first_len * ctx_index) * time_third, padded_len)
-    back_real, back_imag = rotate(back_real, back_imag, twist, 1.0)
-    back = lax.all_to_all(
-        jnp.concatenate([back_real, back_imag], axis=0), "ctx", split_axis=2, concat_axis=2,
-        tiled=True,
-    )
+    back_real, back_imag = rotate(back[:ctx_count], back[ctx_count:], twist, 1.0)
+    back = jnp.stack([back_real, back_imag], axis=1).reshape(ctx_count, -1)
+    back = lax.all_to_all(back, "ctx", split_axis=0, concat_axis=0, tiled=True)
+    back = back.reshape(ctx_count, 2 * pair_count, first_len).transpose(1, 2, 0)
     back_real, back_imag = dft_section(
         apply_cols, back[:pair_count], back[pair_count:], square_tables, 1.0
     )

time: 137 us -> 133 us (0.971)
  local copies, waits for them, and re-layouts: 14.6 us -> 12.3 us
    unnamed x26 -> x22, local copies, waits for them, and re-layouts: 6.85 us -> 4.53 us
where the time goes in v13:
time: 133 us
  waiting for transfers between devices  56.5 us (42%)
  starting transfers between devices  44.6 us (34%)
  local copies, waits for them, and re-layouts  12.3 us (9%)
  blocking collectives  11.3 us (8%)
  other arithmetic  4.92 us (4%)
  matrix products  2.6 us (2%)
    all_to_all x1, starting transfers between devices, shards(): lax.all_to_all(both_in.reshape(2 * row_total, row_count, ctx_count), 'ctx...  20.6 us
    all_to_all x1, waiting for transfers between devices, shards(): spec = lax.all_to_all(spec, 'ctx', split_axis=0, concat_axis=0, tiled=True)  14.8 us
    all_to_all x1, waiting for transfers between devices, shards(): back = lax.all_to_all(back, 'ctx', split_axis=0, concat_axis=0, tiled=True)  14.5 us
    all_to_all x1, waiting for transfers between devices, shards(): lax.all_to_all(both_in.reshape(2 * row_total, row_count, ctx_count), 'ctx...  13.8 us
    all_to_all x1, waiting for transfers between devices, shards(): lax.all_to_all(time_vals, 'ctx', split_axis=0, concat_axis=0, tiled=True)  13.3 us
    psum x1, blocking collectives, shards(): power = lax.psum(jnp.sum(mixed * mixed, axis=0), 'tp')  11.3 us
    all_to_all x1, starting transfers between devices, shards(): back = lax.all_to_all(back, 'ctx', split_axis=0, concat_axis=0, tiled=True)  6.35 us
    all_to_all x1, starting transfers between devices, shards(): lax.all_to_all(time_vals, 'ctx', split_axis=0, concat_axis=0, tiled=True)  6.31 us
  transfers between devices with their start and end apart: 5, of which 4 were waited for; matrix products, arithmetic and copies ran while one was open for 1% of the time, Pallas kernels for 0%

profile of v13, /device:TPU:1, one launch (start us, length us, event | category | flops | bytes accessed | tf_op | source)
XLA Modules:
  0.0 132.7 jit_solution(6822399138200799980)
XLA Ops:
  0.0 0.8 slice.147
  0.9 0.8 slice.148
  1.8 0.8 slice.149
  2.7 5.2 %collective-permute-start = (bf16[3,32,2]{1,2,0:T(2,128)(2,1)S(1)}, bf16[3,32,2]{1,2,0:T(2,128)(2,1)S(1)}, u32[]{:S(2)}, u32[]{:S(2)}) collective-permute-start(bf16[3,32,2]{1,2,0:T(2,128)(2,1)S(1)} %pad_maximum_fusion.16), channel_id=1, source_target_pairs={{0,4},{4,8},{8,12},{12,16},{16,20},{20,24},{24,28},{28,32},{32,36}... | collective-permute-start | bytes 1160 | tf_op jit(solution)/shard_map/ppermute | solution.py:14
  8.6 0.4 copy-done.4
  10.3 1.2 reshape.213
  11.5 20.6 %all-to-all-start = ((f32[128,1,288]{2,1,0:T(1,128)}), f32[128,1,288]{2,1,0:T(1,128)S(1)}, u32[]{:S(2)}, u32[]{:S(2)}) async-start(f32[128,1,288]{2,1,0:T(1,128)} %reshape.213), calls=%async_computation | async-start | bytes 393216 | tf_op jit(solution)/shard_map/all_to_all | solution.py:133
  32.2 13.8 %all-to-all-done = f32[128,1,288]{2,1,0:T(1,128)S(1)} async-done(((f32[128,1,288]{2,1,0:T(1,128)}), f32[128,1,288]{2,1,0:T(1,128)S(1)}, u32[]{:S(2)}, u32[]{:S(2)}) %all-to-all-start) | async-done | bytes 147488 | tf_op jit(solution)/shard_map/all_to_all | solution.py:133
  46.0 0.5 broadcast.320
  46.6 1.1 reduce
  48.5 0.5 convolution_bitcast_fusion
  49.1 0.6 fusion
  49.9 0.9 copy.84
  50.8 6.2 %all-to-all-start.1 = ((f32[128,1,576]{2,1,0:T(1,128)}), f32[128,1,576]{2,1,0:T(1,128)S(1)}, u32[]{:S(2)}, u32[]{:S(2)}) async-start(f32[128,1,576]{2,1,0:T(1,128)} %copy.84), calls=%async_computation.1 | async-start | bytes 655360 | tf_op jit(solution)/shard_map/all_to_all | solution.py:139
  57.4 14.8 %all-to-all-done.1 = f32[128,1,576]{2,1,0:T(1,128)S(1)} async-done(((f32[128,1,576]{2,1,0:T(1,128)}), f32[128,1,576]{2,1,0:T(1,128)S(1)}, u32[]{:S(2)}, u32[]{:S(2)}) %all-to-all-start.1) | async-done | bytes 294944 | tf_op jit(solution)/shard_map/all_to_all | solution.py:139
  72.4 0.4 fusion.2
  72.9 0.4 fusion.14
  73.3 0.8 copy.86
  74.2 6.4 %all-to-all-start.2 = ((f32[128,1,512]{2,1,0:T(1,128)}), f32[128,1,512]{2,1,0:T(1,128)S(1)}, u32[]{:S(2)}, u32[]{:S(2)}) async-start(f32[128,1,512]{2,1,0:T(1,128)} %copy.86), calls=%async_computation.2 | async-start | bytes 524288 | tf_op jit(solution)/shard_map/all_to_all | solution.py:175
  80.7 14.5 %all-to-all-done.2 = f32[128,1,512]{2,1,0:T(1,128)S(1)} async-done(((f32[128,1,512]{2,1,0:T(1,128)}), f32[128,1,512]{2,1,0:T(1,128)S(1)}, u32[]{:S(2)}, u32[]{:S(2)}) %all-to-all-start.2) | async-done | bytes 262176 | tf_op jit(solution)/shard_map/all_to_all | solution.py:175
  95.3 0.4 fusion.18
  95.8 0.3 convolution_bitcast_fusion.1
  96.1 0.5 copy.88
  96.6 0.6 reshape.201
  97.1 0.9 reshape.215
  98.0 6.3 %all-to-all-start.3 = ((f32[128,1,256]{2,1,0:T(1,128)}), f32[128,1,256]{2,1,0:T(1,128)S(1)}, u32[]{:S(2)}, u32[]{:S(2)}) async-start(f32[128,1,256]{2,1,0:T(1,128)} %reshape.215), calls=%async_computation.3 | async-start | bytes 262144 | tf_op jit(solution)/shard_map/all_to_all | solution.py:197
  104.5 13.3 %all-to-all-done.3 = f32[128,1,256]{2,1,0:T(1,128)S(1)} async-done(((f32[128,1,256]{2,1,0:T(1,128)}), f32[128,1,256]{2,1,0:T(1,128)S(1)}, u32[]{:S(2)}, u32[]{:S(2)}) %all-to-all-start.3) | async-done | bytes 131104 | tf_op jit(solution)/shard_map/all_to_all | solution.py:197
  117.8 1.0 reduce.1
  119.2 0.6 copy-done.6
  120.0 11.3 %psum.7 = f32[1024]{0:T(1024)S(1)} all-reduce(f32[1024]{0:T(1024)S(1)} %get-tuple-element.5), channel_id=1, replica_groups=mesh['ctx'=128,'tp'=4] {'tp'}, use_global_device_ids=true, to_apply=%region_1.2 | all-reduce | flops 1024 | bytes 8192 | tf_op jit(solution)/shard_map/psum | solution.py:201
  131.3 0.7 copy-done.5
  132.0 0.7 multiply_convert_fusion
  (73 shorter events, 5.1 us)
Async XLA Ops:
  0.0 7.8 %copy-start = (bf16[32,1024]{1,0:T(8,128)(2,1)S(1)}, bf16[32,1024]{1,0:T(8,128)(2,1)}, u32[]{:S(2)}) copy-start(bf16[32,1024]{1,0:T(8,128)(2,1)} %param.8) | copy-start | bytes 196612
  2.7 5.2 %copy-start.1 = (bf16[32,1024]{1,0:T(8,128)(2,1)S(1)}, bf16[32,1024]{1,0:T(8,128)(2,1)}, u32[]{:S(2)}) copy-start(bf16[32,1024]{1,0:T(8,128)(2,1)} %param.9) | copy-start | bytes 196612
  2.7 6.8 %collective-permute-start = (bf16[3,32,2]{1,2,0:T(2,128)(2,1)S(1)}, bf16[3,32,2]{1,2,0:T(2,128)(2,1)S(1)}, u32[]{:S(2)}, u32[]{:S(2)}) collective-permute-start(bf16[3,32,2]{1,2,0:T(2,128)(2,1)S(1)} %pad_maximum_fusion.16), channel_id=1, source_target_pairs={{0,4},{4,8},{8,12},{12,16},{16,20},{20,24},{24,28},{28,32},{32,36}... | collective-permute-start | bytes 1160 | tf_op jit(solution)/shard_map/ppermute | solution.py:14
  8.3 0.7 copy-start.4
  8.6 0.7 copy-start.3
  11.5 34.5 %all-to-all-start = ((f32[128,1,288]{2,1,0:T(1,128)}), f32[128,1,288]{2,1,0:T(1,128)S(1)}, u32[]{:S(2)}, u32[]{:S(2)}) async-start(f32[128,1,288]{2,1,0:T(1,128)} %reshape.213), calls=%async_computation | async-start | bytes 393216 | tf_op jit(solution)/shard_map/all_to_all | solution.py:133
  50.8 21.4 %all-to-all-start.1 = ((f32[128,1,576]{2,1,0:T(1,128)}), f32[128,1,576]{2,1,0:T(1,128)S(1)}, u32[]{:S(2)}, u32[]{:S(2)}) async-start(f32[128,1,576]{2,1,0:T(1,128)} %copy.84), calls=%async_computation.1 | async-start | bytes 655360 | tf_op jit(solution)/shard_map/all_to_all | solution.py:139
  74.2 21.0 %all-to-all-start.2 = ((f32[128,1,512]{2,1,0:T(1,128)}), f32[128,1,512]{2,1,0:T(1,128)S(1)}, u32[]{:S(2)}, u32[]{:S(2)}) async-start(f32[128,1,512]{2,1,0:T(1,128)} %copy.86), calls=%async_computation.2 | async-start | bytes 524288 | tf_op jit(solution)/shard_map/all_to_all | solution.py:175
  98.0 6.3 %copy-start.2 = (bf16[32,1024]{1,0:T(8,128)(2,1)S(1)}, bf16[32,1024]{1,0:T(8,128)(2,1)}, u32[]{:S(2)}) copy-start(bf16[32,1024]{1,0:T(8,128)(2,1)} %param.7) | copy-start | bytes 196612
  98.0 19.8 %all-to-all-start.3 = ((f32[128,1,256]{2,1,0:T(1,128)}), f32[128,1,256]{2,1,0:T(1,128)S(1)}, u32[]{:S(2)}, u32[]{:S(2)}) async-start(f32[128,1,256]{2,1,0:T(1,128)} %reshape.215), calls=%async_computation.3 | async-start | bytes 262144 | tf_op jit(solution)/shard_map/all_to_all | solution.py:197
  119.2 0.7 copy-start.6
  131.3 0.7 copy-start.5

commit v14 on v13

--- a/solution.py
+++ b/solution.py
@@ -130,10 +130,9 @@
         axis=0,
     )
     row_total = pair_count + filter_count
-    moved = lax.all_to_all(
-        both_in.reshape(2 * row_total, row_count, ctx_count), "ctx", split_axis=2, concat_axis=1,
-        tiled=True,
-    )
+    moved = both_in.reshape(2 * row_total, row_count, ctx_count).transpose(2, 0, 1)
+    moved = lax.all_to_all(moved.reshape(ctx_count, -1), "ctx", split_axis=0, concat_axis=0, tiled=True)
+    moved = moved.reshape(ctx_count, 2 * row_total, row_count).transpose(1, 0, 2)
     moved = moved.reshape(2 * row_total, row_count, ctx_count)
     spec = forward_local(moved[:row_total], moved[row_total:], first_len, ctx_count, ctx_index)
     spec = lax.all_to_all(spec, "ctx", split_axis=0, concat_axis=0, tiled=True)

time: 133 us -> 132 us (level)
    unnamed x22 -> x20, local copies, waits for them, and re-layouts: 4.53 us -> 3.14 us
where the time goes in v14:
time: 132 us; the launch traced here: 131 us
  waiting for transfers between devices  56.5 us (43%)
  starting transfers between devices  44.6 us (34%)
  local copies, waits for them, and re-layouts  12 us (9%)
  blocking collectives  11.2 us (8%)
  other arithmetic  3.81 us (3%)
  matrix products  2.6 us (2%)
    all_to_all x1, starting transfers between devices, shards(): lax.all_to_all(moved.reshape(ctx_count, -1), 'ctx', split_axis=0, concat_...  20.6 us
    all_to_all x1, waiting for transfers between devices, shards(): spec = lax.all_to_all(spec, 'ctx', split_axis=0, concat_axis=0, tiled=True)  14.8 us
    all_to_all x1, waiting for transfers between devices, shards(): back = lax.all_to_all(back, 'ctx', split_axis=0, concat_axis=0, tiled=True)  14.5 us
    all_to_all x1, waiting for transfers between devices, shards(): lax.all_to_all(moved.reshape(ctx_count, -1), 'ctx', split_axis=0, concat_...  13.8 us
    all_to_all x1, waiting for transfers between devices, shards(): lax.all_to_all(time_vals, 'ctx', split_axis=0, concat_axis=0, tiled=True)  13.3 us
    psum x1, blocking collectives, shards(): power = lax.psum(jnp.sum(mixed * mixed, axis=0), 'tp')  11.2 us
    all_to_all x1, starting transfers between devices, shards(): back = lax.all_to_all(back, 'ctx', split_axis=0, concat_axis=0, tiled=True)  6.35 us
    all_to_all x1, starting transfers between devices, shards(): lax.all_to_all(time_vals, 'ctx', split_axis=0, concat_axis=0, tiled=True)  6.3 us
  transfers between devices with their start and end apart: 5, of which 4 were waited for; matrix products, arithmetic and copies ran while one was open for 1% of the time, Pallas kernels for 0%

profile of v14, /device:TPU:1, one launch (start us, length us, event | category | flops | bytes accessed | tf_op | source)
XLA Modules:
  0.0 131.2 jit_solution(5517629579151876780)
XLA Ops:
  0.0 0.8 slice.147
  0.9 0.8 slice.148
  1.8 0.8 slice.149
  2.7 5.2 %collective-permute-start = (bf16[3,32,2]{1,2,0:T(2,128)(2,1)S(1)}, bf16[3,32,2]{1,2,0:T(2,128)(2,1)S(1)}, u32[]{:S(2)}, u32[]{:S(2)}) collective-permute-start(bf16[3,32,2]{1,2,0:T(2,128)(2,1)S(1)} %pad_maximum_fusion.16), channel_id=1, source_target_pairs={{0,4},{4,8},{8,12},{12,16},{16,20},{20,24},{24,28},{28,32},{32,36}... | collective-permute-start | bytes 1160 | tf_op jit(solution)/shard_map/ppermute | solution.py:14
  8.6 0.4 copy-done.4
  9.0 0.3 copy-done.3
  10.0 0.8 copy.75
  10.9 20.6 %all-to-all-start = ((f32[128,1,288]{2,1,0:T(1,128)}), f32[128,1,288]{2,1,0:T(1,128)S(1)}, u32[]{:S(2)}, u32[]{:S(2)}) async-start(f32[128,1,288]{2,1,0:T(1,128)} %copy.75), calls=%async_computation | async-start | bytes 393216 | tf_op jit(solution)/shard_map/all_to_all | solution.py:134
  31.6 13.8 %all-to-all-done = f32[128,1,288]{2,1,0:T(1,128)S(1)} async-done(((f32[128,1,288]{2,1,0:T(1,128)}), f32[128,1,288]{2,1,0:T(1,128)S(1)}, u32[]{:S(2)}, u32[]{:S(2)}) %all-to-all-start) | async-done | bytes 147488 | tf_op jit(solution)/shard_map/all_to_all | solution.py:134
  46.5 0.5 convolution_bitcast_fusion
  47.1 0.6 fusion
  47.8 0.9 copy.83
  48.7 6.2 %all-to-all-start.1 = ((f32[128,1,576]{2,1,0:T(1,128)}), f32[128,1,576]{2,1,0:T(1,128)S(1)}, u32[]{:S(2)}, u32[]{:S(2)}) async-start(f32[128,1,576]{2,1,0:T(1,128)} %copy.83), calls=%async_computation.1 | async-start | bytes 655360 | tf_op jit(solution)/shard_map/all_to_all | solution.py:138
  55.3 14.8 %all-to-all-done.1 = f32[128,1,576]{2,1,0:T(1,128)S(1)} async-done(((f32[128,1,576]{2,1,0:T(1,128)}), f32[128,1,576]{2,1,0:T(1,128)S(1)}, u32[]{:S(2)}, u32[]{:S(2)}) %all-to-all-start.1) | async-done | bytes 294944 | tf_op jit(solution)/shard_map/all_to_all | solution.py:138
  70.3 0.4 fusion.2
  70.8 0.4 fusion.14
  71.3 0.8 copy.85
  72.1 6.4 %all-to-all-start.2 = ((f32[128,1,512]{2,1,0:T(1,128)}), f32[128,1,512]{2,1,0:T(1,128)S(1)}, u32[]{:S(2)}, u32[]{:S(2)}) async-start(f32[128,1,512]{2,1,0:T(1,128)} %copy.85), calls=%async_computation.2 | async-start | bytes 524288 | tf_op jit(solution)/shard_map/all_to_all | solution.py:174
  78.7 14.5 %all-to-all-done.2 = f32[128,1,512]{2,1,0:T(1,128)S(1)} async-done(((f32[128,1,512]{2,1,0:T(1,128)}), f32[128,1,512]{2,1,0:T(1,128)S(1)}, u32[]{:S(2)}, u32[]{:S(2)}) %all-to-all-start.2) | async-done | bytes 262176 | tf_op jit(solution)/shard_map/all_to_all | solution.py:174
  93.3 0.4 fusion.18
  93.7 0.3 convolution_bitcast_fusion.1
  94.1 0.5 copy.87
  94.5 0.6 reshape.209
  95.1 0.9 reshape.221
  96.0 6.3 %all-to-all-start.3 = ((f32[128,1,256]{2,1,0:T(1,128)}), f32[128,1,256]{2,1,0:T(1,128)S(1)}, u32[]{:S(2)}, u32[]{:S(2)}) async-start(f32[128,1,256]{2,1,0:T(1,128)} %reshape.221), calls=%async_computation.3 | async-start | bytes 262144 | tf_op jit(solution)/shard_map/all_to_all | solution.py:196
  102.5 13.3 %all-to-all-done.3 = f32[128,1,256]{2,1,0:T(1,128)S(1)} async-done(((f32[128,1,256]{2,1,0:T(1,128)}), f32[128,1,256]{2,1,0:T(1,128)S(1)}, u32[]{:S(2)}, u32[]{:S(2)}) %all-to-all-start.3) | async-done | bytes 131104 | tf_op jit(solution)/shard_map/all_to_all | solution.py:196
  115.8 0.5 broadcast.320
  116.3 1.0 reduce
  117.7 0.6 copy-done.6
  118.6 11.2 %psum.7 = f32[1024]{0:T(1024)S(1)} all-reduce(f32[1024]{0:T(1024)S(1)} %get-tuple-element.5), channel_id=1, replica_groups=mesh['ctx'=128,'tp'=4] {'tp'}, use_global_device_ids=true, to_apply=%region_1.2 | all-reduce | flops 1024 | bytes 8192 | tf_op jit(solution)/shard_map/psum | solution.py:200
  129.8 0.7 copy-done.5
  130.5 0.7 multiply_convert_fusion
  (72 shorter events, 4.7 us)
Async XLA Ops:
  0.0 7.8 %copy-start = (bf16[32,1024]{1,0:T(8,128)(2,1)S(1)}, bf16[32,1024]{1,0:T(8,128)(2,1)}, u32[]{:S(2)}) copy-start(bf16[32,1024]{1,0:T(8,128)(2,1)} %param.8) | copy-start | bytes 196612
  2.7 5.2 %copy-start.1 = (bf16[32,1024]{1,0:T(8,128)(2,1)S(1)}, bf16[32,1024]{1,0:T(8,128)(2,1)}, u32[]{:S(2)}) copy-start(bf16[32,1024]{1,0:T(8,128)(2,1)} %param.9) | copy-start | bytes 196612
  2.7 6.8 %collective-permute-start = (bf16[3,32,2]{1,2,0:T(2,128)(2,1)S(1)}, bf16[3,32,2]{1,2,0:T(2,128)(2,1)S(1)}, u32[]{:S(2)}, u32[]{:S(2)}) collective-permute-start(bf16[3,32,2]{1,2,0:T(2,128)(2,1)S(1)} %pad_maximum_fusion.16), channel_id=1, source_target_pairs={{0,4},{4,8},{8,12},{12,16},{16,20},{20,24},{24,28},{28,32},{32,36}... | collective-permute-start | bytes 1160 | tf_op jit(solution)/shard_map/ppermute | solution.py:14
  8.3 0.7 copy-start.4
  8.6 0.7 copy-start.3
  10.9 34.5 %all-to-all-start = ((f32[128,1,288]{2,1,0:T(1,128)}), f32[128,1,288]{2,1,0:T(1,128)S(1)}, u32[]{:S(2)}, u32[]{:S(2)}) async-start(f32[128,1,288]{2,1,0:T(1,128)} %copy.75), calls=%async_computation | async-start | bytes 393216 | tf_op jit(solution)/shard_map/all_to_all | solution.py:134
  48.7 21.4 %all-to-all-start.1 = ((f32[128,1,576]{2,1,0:T(1,128)}), f32[128,1,576]{2,1,0:T(1,128)S(1)}, u32[]{:S(2)}, u32[]{:S(2)}) async-start(f32[128,1,576]{2,1,0:T(1,128)} %copy.83), calls=%async_computation.1 | async-start | bytes 655360 | tf_op jit(solution)/shard_map/all_to_all | solution.py:138
  72.1 21.0 %all-to-all-start.2 = ((f32[128,1,512]{2,1,0:T(1,128)}), f32[128,1,512]{2,1,0:T(1,128)S(1)}, u32[]{:S(2)}, u32[]{:S(2)}) async-start(f32[128,1,512]{2,1,0:T(1,128)} %copy.85), calls=%async_computation.2 | async-start | bytes 524288 | tf_op jit(solution)/shard_map/all_to_all | solution.py:174
  96.0 6.3 %copy-start.2 = (bf16[32,1024]{1,0:T(8,128)(2,1)S(1)}, bf16[32,1024]{1,0:T(8,128)(2,1)}, u32[]{:S(2)}) copy-start(bf16[32,1024]{1,0:T(8,128)(2,1)} %param.7) | copy-start | bytes 196612
  96.0 19.8 %all-to-all-start.3 = ((f32[128,1,256]{2,1,0:T(1,128)}), f32[128,1,256]{2,1,0:T(1,128)S(1)}, u32[]{:S(2)}, u32[]{:S(2)}) async-start(f32[128,1,256]{2,1,0:T(1,128)} %reshape.221), calls=%async_computation.3 | async-start | bytes 262144 | tf_op jit(solution)/shard_map/all_to_all | solution.py:196
  117.7 0.7 copy-start.6
  129.8 0.7 copy-start.5

commit v15 on v14

--- a/solution.py
+++ b/solution.py
@@ -136,11 +136,16 @@
     moved = moved.reshape(2 * row_total, row_count, ctx_count)
     spec = forward_local(moved[:row_total], moved[row_total:], first_len, ctx_count, ctx_index)
     spec = lax.all_to_all(spec, "ctx", split_axis=0, concat_axis=0, tiled=True)
-    spec = spec.reshape(ctx_count, 2 * row_total, first_len).transpose(1, 2, 0)
     square_tables = grid_product(ctx_count, ctx_count, ctx_count)
-    spec_real, spec_imag = dft_section(
-        apply_cols, spec[:row_total], spec[row_total:], square_tables, -1.0
-    )
+    fwd_cos, fwd_sin = square_tables
+    gather_block = jnp.stack(
+        [jnp.stack([fwd_cos, -fwd_sin], axis=1), jnp.stack([fwd_sin, fwd_cos], axis=1)], axis=1
+    )
+    spec = jnp.einsum(
+        "jhrk,jhum->urkm", spec.reshape(ctx_count, 2, row_total, first_len), gather_block,
+        precision=HIGHEST,
+    )
+    spec_real, spec_imag = spec[0], spec[1]
     data_real = spec_real[:pair_count]
     data_imag = spec_imag[:pair_count]
     filt_real = spec_real[pair_count:]

time: 132 us -> 132 us (level)
  transfers between devices with their start and end apart: 5 -> 5, of which waited for: 4 -> 4; matrix products, arithmetic and copies ran while one was open for 1% -> 2% of each run, Pallas kernels for 0% -> 0%
where the time goes in v15:
time: 132 us; the launch traced here: 131 us
  waiting for transfers between devices  55.9 us (42%)
  starting transfers between devices  44.6 us (34%)
  local copies, waits for them, and re-layouts  11.9 us (9%)
  blocking collectives  11.3 us (9%)
  other arithmetic  4.39 us (3%)
  matrix products  2.81 us (2%)
    all_to_all x1, starting transfers between devices, shards(): lax.all_to_all(moved.reshape(ctx_count, -1), 'ctx', split_axis=0, concat_...  20.6 us
    all_to_all x1, waiting for transfers between devices, shards(): spec = lax.all_to_all(spec, 'ctx', split_axis=0, concat_axis=0, tiled=True)  14.5 us
    all_to_all x1, waiting for transfers between devices, shards(): back = lax.all_to_all(back, 'ctx', split_axis=0, concat_axis=0, tiled=True)  14.2 us
    all_to_all x1, waiting for transfers between devices, shards(): lax.all_to_all(moved.reshape(ctx_count, -1), 'ctx', split_axis=0, concat_...  13.8 us
    all_to_all x1, waiting for transfers between devices, shards(): lax.all_to_all(time_vals, 'ctx', split_axis=0, concat_axis=0, tiled=True)  13.3 us
    psum x1, blocking collectives, shards(): power = lax.psum(jnp.sum(mixed * mixed, axis=0), 'tp')  11.3 us
    all_to_all x1, starting transfers between devices, shards(): back = lax.all_to_all(back, 'ctx', split_axis=0, concat_axis=0, tiled=True)  6.34 us
    all_to_all x1, starting transfers between devices, shards(): lax.all_to_all(time_vals, 'ctx', split_axis=0, concat_axis=0, tiled=True)  6.28 us
  transfers between devices with their start and end apart: 5, of which 4 were waited for; matrix products, arithmetic and copies ran while one was open for 2% of the time, Pallas kernels for 0%

profile of v15, /device:TPU:1, one launch (start us, length us, event | category | flops | bytes accessed | tf_op | source)
XLA Modules:
  0.0 131.3 jit_solution(8752601731849040152)
XLA Ops:
  0.0 0.8 slice.145
  0.9 0.8 slice.146
  1.8 0.8 slice.147
  2.7 5.2 %collective-permute-start = (bf16[3,32,2]{1,2,0:T(2,128)(2,1)S(1)}, bf16[3,32,2]{1,2,0:T(2,128)(2,1)S(1)}, u32[]{:S(2)}, u32[]{:S(2)}) collective-permute-start(bf16[3,32,2]{1,2,0:T(2,128)(2,1)S(1)} %pad_maximum_fusion.15), channel_id=1, source_target_pairs={{0,4},{4,8},{8,12},{12,16},{16,20},{20,24},{24,28},{28,32},{32,36}... | collective-permute-start | bytes 1160 | tf_op jit(solution)/shard_map/ppermute | solution.py:14
  8.6 0.4 copy-done.4
  9.0 0.3 copy-done.3
  10.0 0.8 copy.87
  10.8 20.6 %all-to-all-start = ((f32[128,1,288]{2,1,0:T(1,128)}), f32[128,1,288]{2,1,0:T(1,128)S(1)}, u32[]{:S(2)}, u32[]{:S(2)}) async-start(f32[128,1,288]{2,1,0:T(1,128)} %copy.87), calls=%async_computation | async-start | bytes 393216 | tf_op jit(solution)/shard_map/all_to_all | solution.py:134
  31.5 13.8 %all-to-all-done = f32[128,1,288]{2,1,0:T(1,128)S(1)} async-done(((f32[128,1,288]{2,1,0:T(1,128)}), f32[128,1,288]{2,1,0:T(1,128)S(1)}, u32[]{:S(2)}, u32[]{:S(2)}) %all-to-all-start) | async-done | bytes 147488 | tf_op jit(solution)/shard_map/all_to_all | solution.py:134
  46.5 0.5 convolution_bitcast_fusion.1
  47.1 0.6 fusion.2
  47.8 0.9 copy.95
  48.7 6.2 %all-to-all-start.1 = ((f32[128,1,576]{2,1,0:T(1,128)}), f32[128,1,576]{2,1,0:T(1,128)S(1)}, u32[]{:S(2)}, u32[]{:S(2)}) async-start(f32[128,1,576]{2,1,0:T(1,128)} %copy.95), calls=%async_computation.1 | async-start | bytes 655360 | tf_op jit(solution)/shard_map/all_to_all | solution.py:138
  55.6 14.5 %all-to-all-done.1 = f32[128,1,576]{2,1,0:T(1,128)S(1)} async-done(((f32[128,1,576]{2,1,0:T(1,128)}), f32[128,1,576]{2,1,0:T(1,128)S(1)}, u32[]{:S(2)}, u32[]{:S(2)}) %all-to-all-start.1) | async-done | bytes 294944 | tf_op jit(solution)/shard_map/all_to_all | solution.py:138
  70.3 0.5 convolution_bitcast_fusion
  70.9 0.5 fusion.9
  71.5 0.8 copy.99
  72.3 6.3 %all-to-all-start.2 = ((f32[128,1,512]{2,1,0:T(1,128)}), f32[128,1,512]{2,1,0:T(1,128)S(1)}, u32[]{:S(2)}, u32[]{:S(2)}) async-start(f32[128,1,512]{2,1,0:T(1,128)} %copy.99), calls=%async_computation.2 | async-start | bytes 524288 | tf_op jit(solution)/shard_map/all_to_all | solution.py:179
  79.1 14.2 %all-to-all-done.2 = f32[128,1,512]{2,1,0:T(1,128)S(1)} async-done(((f32[128,1,512]{2,1,0:T(1,128)}), f32[128,1,512]{2,1,0:T(1,128)S(1)}, u32[]{:S(2)}, u32[]{:S(2)}) %all-to-all-start.2) | async-done | bytes 262176 | tf_op jit(solution)/shard_map/all_to_all | solution.py:179
  93.5 0.4 fusion.13
  93.9 0.3 convolution_bitcast_fusion.2
  94.2 0.5 copy.101
  94.7 0.6 reshape.290
  95.3 0.9 reshape.304
  96.2 6.3 %all-to-all-start.3 = ((f32[128,1,256]{2,1,0:T(1,128)}), f32[128,1,256]{2,1,0:T(1,128)S(1)}, u32[]{:S(2)}, u32[]{:S(2)}) async-start(f32[128,1,256]{2,1,0:T(1,128)} %reshape.304), calls=%async_computation.3 | async-start | bytes 262144 | tf_op jit(solution)/shard_map/all_to_all | solution.py:201
  102.6 13.3 %all-to-all-done.3 = f32[128,1,256]{2,1,0:T(1,128)S(1)} async-done(((f32[128,1,256]{2,1,0:T(1,128)}), f32[128,1,256]{2,1,0:T(1,128)S(1)}, u32[]{:S(2)}, u32[]{:S(2)}) %all-to-all-start.3) | async-done | bytes 131104 | tf_op jit(solution)/shard_map/all_to_all | solution.py:201
  115.9 0.5 broadcast.422
  116.4 1.0 reduce
  117.9 0.6 copy-done.6
  118.7 11.3 %psum.7 = f32[1024]{0:T(1024)S(1)} all-reduce(f32[1024]{0:T(1024)S(1)} %get-tuple-element.5), channel_id=1, replica_groups=mesh['ctx'=128,'tp'=4] {'tp'}, use_global_device_ids=true, to_apply=%region_1.2 | all-reduce | flops 1024 | bytes 8192 | tf_op jit(solution)/shard_map/psum | solution.py:205
  130.0 0.7 copy-done.5
  130.6 0.7 multiply_convert_fusion
  (75 shorter events, 5.3 us)
Async XLA Ops:
  0.0 7.8 %copy-start = (bf16[32,1024]{1,0:T(8,128)(2,1)S(1)}, bf16[32,1024]{1,0:T(8,128)(2,1)}, u32[]{:S(2)}) copy-start(bf16[32,1024]{1,0:T(8,128)(2,1)} %param.8) | copy-start | bytes 196612
  2.7 5.2 %copy-start.1 = (bf16[32,1024]{1,0:T(8,128)(2,1)S(1)}, bf16[32,1024]{1,0:T(8,128)(2,1)}, u32[]{:S(2)}) copy-start(bf16[32,1024]{1,0:T(8,128)(2,1)} %param.9) | copy-start | bytes 196612
  2.7 6.8 %collective-permute-start = (bf16[3,32,2]{1,2,0:T(2,128)(2,1)S(1)}, bf16[3,32,2]{1,2,0:T(2,128)(2,1)S(1)}, u32[]{:S(2)}, u32[]{:S(2)}) collective-permute-start(bf16[3,32,2]{1,2,0:T(2,128)(2,1)S(1)} %pad_maximum_fusion.15), channel_id=1, source_target_pairs={{0,4},{4,8},{8,12},{12,16},{16,20},{20,24},{24,28},{28,32},{32,36}... | collective-permute-start | bytes 1160 | tf_op jit(solution)/shard_map/ppermute | solution.py:14
  8.3 0.7 copy-start.4
  8.6 0.7 copy-start.3
  10.8 34.5 %all-to-all-start = ((f32[128,1,288]{2,1,0:T(1,128)}), f32[128,1,288]{2,1,0:T(1,128)S(1)}, u32[]{:S(2)}, u32[]{:S(2)}) async-start(f32[128,1,288]{2,1,0:T(1,128)} %copy.87), calls=%async_computation | async-start | bytes 393216 | tf_op jit(solution)/shard_map/all_to_all | solution.py:134
  48.7 21.4 %all-to-all-start.1 = ((f32[128,1,576]{2,1,0:T(1,128)}), f32[128,1,576]{2,1,0:T(1,128)S(1)}, u32[]{:S(2)}, u32[]{:S(2)}) async-start(f32[128,1,576]{2,1,0:T(1,128)} %copy.95), calls=%async_computation.1 | async-start | bytes 655360 | tf_op jit(solution)/shard_map/all_to_all | solution.py:138
  72.3 21.0 %all-to-all-start.2 = ((f32[128,1,512]{2,1,0:T(1,128)}), f32[128,1,512]{2,1,0:T(1,128)S(1)}, u32[]{:S(2)}, u32[]{:S(2)}) async-start(f32[128,1,512]{2,1,0:T(1,128)} %copy.99), calls=%async_computation.2 | async-start | bytes 524288 | tf_op jit(solution)/shard_map/all_to_all | solution.py:179
  96.2 6.3 %copy-start.2 = (bf16[32,1024]{1,0:T(8,128)(2,1)S(1)}, bf16[32,1024]{1,0:T(8,128)(2,1)}, u32[]{:S(2)}) copy-start(bf16[32,1024]{1,0:T(8,128)(2,1)} %param.7) | copy-start | bytes 196612
  96.2 19.8 %all-to-all-start.3 = ((f32[128,1,256]{2,1,0:T(1,128)}), f32[128,1,256]{2,1,0:T(1,128)S(1)}, u32[]{:S(2)}, u32[]{:S(2)}) async-start(f32[128,1,256]{2,1,0:T(1,128)} %reshape.304), calls=%async_computation.3 | async-start | bytes 262144 | tf_op jit(solution)/shard_map/all_to_all | solution.py:201
  117.8 0.7 copy-start.6
  130.0 0.7 copy-start.5
